TPU v7x, 32 devices: a whole 2x2x4 slice. The times are simulated.
32 devices in a mesh: groups: 2 (over y), row: 16 (over z, x, core).
Axes of the slice: x: 2, y: 2, z: 4, core: 2. Of those that a mesh axis runs over, the one named last changes fastest.
Arguments:
- features: bfloat16 [576, 16384], P(None, ('groups', 'row')), parts along dimension 1, may hold values from -150 to 150
- labels: int32 [16384], P(('groups', 'row')), parts along dimension 0, may hold values 0 or 1
- other_predictor: float32 [16384], P(('groups', 'row')), parts along dimension 0, may hold values from -6 to 6
- coefficients: float32 [8192], P('groups'), parts along dimension 0, may hold values from -0.09375 to 0.09375
- panel_block: int32 [2], P('groups'), parts along dimension 0, may hold values from 0 to 55
Outputs:
- r_factor: float32 [1152, 576], P('groups'), parts along dimension 0
- residual: float32 [16384], P(('groups', 'row')), parts along dimension 0
There are 2 independent parts, one for each index of `groups`. A program takes and returns all parts, laid end to end along the dimension named above; each array names one. Nothing has to cross between parts.
All inputs are finite; a program needn't handle non-finite values. No bound on the sum of `labels` on one device may be relied on, other than what follows from the above.
Results may differ from a plain program's by a relative error of at most 0.0003.
Values sent between devices are 32-bit elements; how exact they have to be, the bound alone decides.
No kernel may reach another device: no remote copies, remote signals or barrier semaphores. Data moves between devices by JAX's collectives and lax.ppermute only.
A program may use at most 64 MiB of HBM per device.

v0:
```python
import functools
import math

import jax
import jax.numpy as jnp
from jax import lax
from jax.experimental import pallas as pl
from jax.experimental.pallas import tpu as pltpu
from jax.sharding import PartitionSpec as P

PB = 64


precise = lax.Precision.HIGHEST


BLOCK = 128


def nt(a, b):
    return lax.dot_general(a, b, (((1,), (1,)), ((), ())), precision=precise, preferred_element_type=jnp.float32)


def nn(a, b):
    return lax.dot_general(a, b, (((1,), (0,)), ((), ())), precision=precise, preferred_element_type=jnp.float32)


def chol_kernel(g_ref, l_ref, z_ref, d_ref, m_ref, k_ref, *, blocks, last_steps, target):
    b = BLOCK
    lane = lax.broadcasted_iota(jnp.int32, (b, b), 1)
    sub = lax.broadcasted_iota(jnp.int32, (b, b), 0)
    lane_row = lax.broadcasted_iota(jnp.int32, (1, b), 1)
    sub_col = lax.broadcasted_iota(jnp.int32, (b, 1), 0)
    eye = jnp.where(lane == sub, 1.0, 0.0).astype(jnp.float32)
    l_ref[...] = g_ref[...]
    inverses = []
    for k in range(blocks):
        r0 = k * b
        d_ref[...] = l_ref[r0:r0 + b, r0:r0 + b]
        m_ref[...] = eye
        k_ref[...] = jnp.zeros((b, b), jnp.float32)

        def step(j, carry):
            d = d_ref[...]
            col = jnp.sum(jnp.where(lane == j, d, 0.0), axis=1, keepdims=True)
            piv = jnp.sum(jnp.where(sub_col == j, col, 0.0), axis=0, keepdims=True)
            inv = lax.rsqrt(piv)
            lcol = jnp.where(sub_col >= j, col * inv, 0.0)
            lrow = jnp.where(lane_row >= j, d_ref[pl.ds(j, 1), :] * inv, 0.0)
            d_ref[...] = d - lcol * lrow
            k_ref[...] = jnp.where(lane == j, lcol, k_ref[...])
            mrow = m_ref[pl.ds(j, 1), :] * inv
            below = jnp.where(sub_col > j, lcol, 0.0)
            m_ref[...] = jnp.where(sub == j, mrow, m_ref[...] - below * mrow)
            return carry

        steps = b if k < blocks - 1 else last_steps
        lax.fori_loop(0, steps, step, 0)
        inverse = m_ref[...]
        inverses.append(inverse)
        l_ref[r0:r0 + b, r0:r0 + b] = k_ref[...]
        if k < blocks - 1:
            panel = nt(l_ref[r0 + b:, r0:r0 + b], inverse)
            l_ref[r0 + b:, r0:r0 + b] = panel
            l_ref[r0 + b:, r0 + b:] = l_ref[r0 + b:, r0 + b:] - nt(panel, panel)
            l_ref[r0:r0 + b, r0 + b:] = jnp.zeros((b, l_ref.shape[1] - r0 - b), jnp.float32)
    last = blocks - 1
    tl = target - last * b
    lane8 = lax.broadcasted_iota(jnp.int32, (8, b), 1)
    row = l_ref[pl.ds(target, 1), :]
    zs = [None] * blocks
    for k in range(last, -1, -1):
        acc = jnp.broadcast_to(row[:, k * b:(k + 1) * b], (8, b))
        if k == last:
            acc = jnp.where(lane8 < tl, acc, 0.0)
        for i in range(k + 1, blocks):
            acc = acc - nn(zs[i], l_ref[i * b:(i + 1) * b, k * b:(k + 1) * b])
        zk = nn(acc, inverses[k])
        if k == last:
            zk = jnp.where(lane8 < tl, zk, 0.0)
        zs[k] = zk
        z_ref[:, k * b:(k + 1) * b] = zk


def cholesky_and_solve(sym, target):
    n = sym.shape[0]
    blocks = n // BLOCK
    last_steps = target + 1 - (blocks - 1) * BLOCK
    kernel = functools.partial(chol_kernel, blocks=blocks, last_steps=last_steps, target=target)
    vmem = pltpu.VMEM
    return pl.pallas_call(
        kernel,
        out_shape=(jax.ShapeDtypeStruct((n, n), jnp.float32), jax.ShapeDtypeStruct((8, n), jnp.float32)),
        in_specs=[pl.BlockSpec(memory_space=vmem)],
        out_specs=(pl.BlockSpec(memory_space=vmem), pl.BlockSpec(memory_space=vmem)),
        scratch_shapes=[pltpu.VMEM((BLOCK, BLOCK), jnp.float32)] * 3,
    )(sym)


def butterfly_sum(flat, axis):
    size = lax.axis_size(axis)
    steps = size.bit_length() - 1
    me = lax.axis_index(axis)
    current = flat
    for bit in range(steps):
        half = current.shape[0] // 2
        low, high = current[:half], current[half:]
        upper_half = ((me >> bit) & 1) == 1
        send = jnp.where(upper_half, low, high)
        keep = jnp.where(upper_half, high, low)
        pairs = [(i, i ^ (1 << bit)) for i in range(size)]
        current = keep + lax.ppermute(send, axis, pairs)
    for bit in reversed(range(steps)):
        pairs = [(i, i ^ (1 << bit)) for i in range(size)]
        got = lax.ppermute(current, axis, pairs)
        upper_half = ((me >> bit) & 1) == 1
        current = jnp.where(
            upper_half, jnp.concatenate([got, current]), jnp.concatenate([current, got])
        )
    return current


def shards(features, labels, other_predictor, coefficients, panel_block):
    window, rows_here = features.shape
    row_devices = lax.axis_size("row")
    assert row_devices & (row_devices - 1) == 0
    total_rows = rows_here * row_devices
    first_col = panel_block[0] * PB
    window_coef = lax.dynamic_slice(coefficients, (first_col,), (window,))
    as_float = features.astype(jnp.float32)
    linear = jnp.dot(window_coef, as_float, precision=precise) + other_predictor
    fitted = jax.nn.sigmoid(linear)
    weight = jnp.maximum(fitted * (1.0 - fitted), 0.01)
    root_weight = jnp.sqrt(weight)
    norm_scale = 1.0 / math.sqrt(total_rows)
    scaled = as_float * (root_weight * norm_scale)[None, :]
    target = (
        root_weight * linear + (labels.astype(jnp.float32) - fitted) / root_weight
    ) * norm_scale
    working = jnp.concatenate([scaled, target[None, :]], axis=0)
    width = window + 1
    local_gram = lax.dot_general(
        working, working, (((1,), (1,)), ((), ())), precision=precise
    )
    panels = window // PB
    pieces = [local_gram[k * PB:(k + 1) * PB, :(k + 1) * PB].reshape(-1) for k in range(panels)]
    pieces.append(local_gram[window])
    used = sum(p.shape[0] for p in pieces)
    quantum = row_devices * 128
    padded = -(-used // quantum) * quantum
    pieces.append(jnp.zeros((padded - used,), jnp.float32))
    packed = butterfly_sum(jnp.concatenate(pieces), "row")
    size = -(-width // BLOCK) * BLOCK
    lower_gram = jnp.zeros((size, size), jnp.float32)
    offset = 0
    for k in range(panels):
        block = packed[offset:offset + PB * (k + 1) * PB].reshape(PB, (k + 1) * PB)
        lower_gram = lower_gram.at[k * PB:(k + 1) * PB, :(k + 1) * PB].set(block)
        offset += PB * (k + 1) * PB
    lower_gram = lower_gram.at[window, :width].set(packed[offset:offset + width])
    rows = lax.broadcasted_iota(jnp.int32, (size, size), 0)
    cols = lax.broadcasted_iota(jnp.int32, (size, size), 1)
    sym = jnp.where(rows >= cols, lower_gram, lower_gram.T)
    sym = jnp.where((rows == cols) & (rows >= width), 1.0, sym)
    lower, solved = cholesky_and_solve(sym, window)
    lower_window = lower[:window, :window]
    coef = solved[0, :window]
    fitted_part = jnp.dot(coef, scaled, precision=precise)
    residual = (target - fitted_part) * math.sqrt(total_rows)
    return lower_window.T, residual


def solution(mesh):
    in_specs = (
        P(None, ("groups", "row")),
        P(("groups", "row")),
        P(("groups", "row")),
        P("groups"),
        P("groups"),
    )
    out_specs = (P("groups", None), P(("groups", "row")))
    return jax.shard_map(shards, mesh=mesh, in_specs=in_specs, out_specs=out_specs, check_vma=False)
```

profile of v0, /device:TPU:0, one launch (start us, length us, event | category | flops | bytes accessed | tf_op | source)
XLA Modules:
  0.0 187.6 jit_solution(10094346552928739618)
XLA Ops:
  1.3 0.8 dynamic_slice.3
  2.1 1.4 fusion.19
  3.5 0.7 fusion.17
  4.2 1.2 convert_multiply_fusion
  5.4 3.0 %fusion.2 = f32[577,577]{1,0:T(8,128)S(1)} fusion(f32[1,512]{1,0:T(1,128)S(1)} %bitcast.37, f32[576,512]{1,0:T(8,128)S(1)} %convert_multiply_fusion), kind=kOutput, calls=%fused_computation.6 | convolution fusion | flops 2045811200 | bytes 2513412 | tf_op jit(solution)/shard_map/dot_general | solution.py:142
  9.3 1.4 concatenate.197
  10.7 0.6 collective-permute-start
  11.3 1.3 collective-permute-done
  12.7 2.9 %collective-permute-start.1 = (f32[46592]{0:T(1024)S(1)}, f32[46592]{0:T(1024)S(1)}, u32[]{:S(2)}, u32[]{:S(2)}) collective-permute-start(f32[46592]{0:T(1024)S(1)} %slice_select_fusion.1), channel_id=1, source_target_pairs={{0,2},{1,3},{2,0},{3,1},{4,6},{5,7},{6,4},{7,5},{8,10},{9,11},{10,... | collective-permute-start | bytes 559112 | tf_op jit(solution)/shard_map/ppermute | solution.py:112
  15.6 5.0 %collective-permute-done.1 = f32[46592]{0:T(1024)S(1)} collective-permute-done((f32[46592]{0:T(1024)S(1)}, f32[46592]{0:T(1024)S(1)}, u32[]{:S(2)}, u32[]{:S(2)}) %collective-permute-start.1) | collective-permute-done | bytes 186400 | tf_op jit(solution)/shard_map/ppermute | solution.py:112
  20.7 1.9 %collective-permute-start.2 = (f32[23296]{0:T(1024)S(1)}, f32[23296]{0:T(1024)S(1)}, u32[]{:S(2)}, u32[]{:S(2)}) collective-permute-start(f32[23296]{0:T(1024)S(1)} %slice_select_fusion.2), channel_id=1, source_target_pairs={{0,4},{1,5},{2,6},{3,7},{4,0},{5,1},{6,2},{7,3},{8,12},{9,13},{10,... | collective-permute-start | bytes 279560 | tf_op jit(solution)/shard_map/ppermute | solution.py:112
  22.6 2.7 %collective-permute-done.2 = f32[23296]{0:T(1024)S(1)} collective-permute-done((f32[23296]{0:T(1024)S(1)}, f32[23296]{0:T(1024)S(1)}, u32[]{:S(2)}, u32[]{:S(2)}) %collective-permute-start.2) | collective-permute-done | bytes 93216 | tf_op jit(solution)/shard_map/ppermute | solution.py:112
  25.4 2.9 %collective-permute-start.3 = (f32[11648]{0:T(1024)S(1)}, f32[11648]{0:T(1024)S(1)}, u32[]{:S(2)}, u32[]{:S(2)}) collective-permute-start(f32[11648]{0:T(1024)S(1)} %slice_select_fusion.3), channel_id=1, source_target_pairs={{0,8},{1,9},{2,10},{3,11},{4,12},{5,13},{6,14},{7,15},{8,0},{9,1},... | collective-permute-start | bytes 139784 | tf_op jit(solution)/shard_map/ppermute | solution.py:112
  28.3 2.2 %collective-permute-done.3 = f32[11648]{0:T(1024)S(1)} collective-permute-done((f32[11648]{0:T(1024)S(1)}, f32[11648]{0:T(1024)S(1)}, u32[]{:S(2)}, u32[]{:S(2)}) %collective-permute-start.3) | collective-permute-done | bytes 46624 | tf_op jit(solution)/shard_map/ppermute | solution.py:112
  30.5 2.9 %collective-permute-start.4 = (f32[11648]{0:T(1024)S(1)}, f32[11648]{0:T(1024)S(1)}, u32[]{:S(2)}, u32[]{:S(2)}) collective-permute-start(f32[11648]{0:T(1024)S(1)} %select_add_fusion.3), channel_id=1, source_target_pairs={{0,8},{1,9},{2,10},{3,11},{4,12},{5,13},{6,14},{7,15},{8,0},{9,1},... | collective-permute-start | bytes 139784 | tf_op jit(solution)/shard_map/ppermute | solution.py:115
  33.9 1.7 collective-permute-done.4
  35.6 2.1 %collective-permute-start.5 = (f32[23296]{0:T(1024)S(1)}, f32[23296]{0:T(1024)S(1)}, u32[]{:S(2)}, u32[]{:S(2)}) collective-permute-start(f32[23296]{0:T(1024)S(1)} %maximum_select_fusion.15), channel_id=1, source_target_pairs={{0,4},{1,5},{2,6},{3,7},{4,0},{5,1},{6,2},{7,3},{8,12},{9,13},{10,... | collective-permute-start | bytes 279560 | tf_op jit(solution)/shard_map/ppermute | solution.py:115
  38.4 0.2 maximum_select_fusion.8
  38.9 1.5 collective-permute-done.5
  40.4 1.8 collective-permute-start.6
  42.4 0.1 copy.44
  43.0 0.2 maximum_select_fusion.9
  43.3 0.1 maximum_select_fusion.10
  43.5 0.2 maximum_select_fusion.7
  43.7 2.3 %collective-permute-done.6 = f32[46592]{0:T(1024)S(1)} collective-permute-done((f32[46592]{0:T(1024)S(1)}, f32[46592]{0:T(1024)S(1)}, u32[]{:S(2)}, u32[]{:S(2)}) %collective-permute-start.6) | collective-permute-done | bytes 186400 | tf_op jit(solution)/shard_map/ppermute | solution.py:115
  46.7 0.3 maximum_select_fusion.2
  47.0 1.0 maximum_select_fusion.5
  48.0 1.0 maximum_select_fusion.4
  49.3 0.1 copy.15
  49.4 0.3 maximum_select_fusion.1
  49.8 0.9 maximum_select_fusion.3
  50.9 0.8 copy-done.2
  51.7 0.2 copy.54
  51.9 0.1 concatenate.242
  52.0 1.0 copy.48
  53.1 0.9 copy.36
  54.1 0.7 copy.29
  54.9 0.9 copy.27
  55.8 0.2 concatenate.205
  56.0 0.2 copy.17
  56.3 0.8 fusion.11
  57.2 0.7 reshape.442
  57.9 1.7 copy.38
  59.6 0.7 reshape.443
  60.3 1.7 copy.39
  62.1 0.9 copy.56
  63.1 1.0 fusion.6
  64.2 0.3 fusion.7
  64.8 2.1 %scatter.35 = f32[640,640]{0,1:T(8,128)S(1)} dynamic-update-slice(f32[640,640]{0,1:T(8,128)S(1)} %scatter.34, f32[64,128]{0,1:T(8,128)S(1)} %fusion.10, s32[]{:T(128)} %constant.299.clone.1, s32[]{:T(128)} %constant.290.clone.1) | dynamic-update-slice | bytes 65540 | tf_op jit(solution)/shard_map/scatter | solution.py:158
  66.9 2.2 %scatter.36 = f32[640,640]{0,1:T(8,128)S(1)} dynamic-update-slice(f32[640,640]{0,1:T(8,128)S(1)} %scatter.35, f32[64,192]{0,1:T(8,128)S(1)} %copy-done.11, s32[]{:T(128)} %constant.300.clone.1, s32[]{:T(128)} %constant.290.clone.1) | dynamic-update-slice | bytes 98308 | tf_op jit(solution)/shard_map/scatter | solution.py:158
  69.2 3.3 %scatter.39 = f32[640,640]{0,1:T(8,128)S(1)} dynamic-update-slice(f32[640,640]{0,1:T(8,128)S(1)} %scatter.36, f32[64,256]{0,1:T(8,128)S(1)} %fusion.9, s32[]{:T(128)} %constant.301.clone.1, s32[]{:T(128)} %constant.290.clone.1) | dynamic-update-slice | bytes 131076 | tf_op jit(solution)/shard_map/scatter | solution.py:158
  72.5 3.4 %scatter.40 = f32[640,640]{0,1:T(8,128)S(1)} dynamic-update-slice(f32[640,640]{0,1:T(8,128)S(1)} %scatter.39, f32[64,320]{0,1:T(8,128)S(1)} %copy-done.10, s32[]{:T(128)} %constant.302.clone.1, s32[]{:T(128)} %constant.290.clone.1) | dynamic-update-slice | bytes 163844 | tf_op jit(solution)/shard_map/scatter | solution.py:158
  75.9 4.1 %scatter.41 = f32[640,640]{0,1:T(8,128)S(1)} dynamic-update-slice(f32[640,640]{0,1:T(8,128)S(1)} %scatter.40, f32[64,384]{0,1:T(8,128)S(1)} %copy-done.9, s32[]{:T(128)} %constant.303.clone.1, s32[]{:T(128)} %constant.290.clone.1) | dynamic-update-slice | bytes 196612 | tf_op jit(solution)/shard_map/scatter | solution.py:158
  80.0 3.6 %scatter.44 = f32[640,640]{0,1:T(8,128)S(1)} dynamic-update-slice(f32[640,640]{0,1:T(8,128)S(1)} %scatter.41, f32[64,448]{0,1:T(8,128)S(1)} %fusion.7, s32[]{:T(128)} %constant.304.clone.1, s32[]{:T(128)} %constant.290.clone.1) | dynamic-update-slice | bytes 229380 | tf_op jit(solution)/shard_map/scatter | solution.py:158
  83.6 4.8 %scatter.45 = f32[640,640]{0,1:T(8,128)S(1)} dynamic-update-slice(f32[640,640]{0,1:T(8,128)S(1)} %scatter.44, f32[64,512]{0,1:T(8,128)S(1)} %copy-done.8, s32[]{:T(128)} %constant.305.clone.1, s32[]{:T(128)} %constant.290.clone.1) | dynamic-update-slice | bytes 262148 | tf_op jit(solution)/shard_map/scatter | solution.py:158
  88.4 2.7 %scatter.46 = f32[640,640]{0,1:T(8,128)S(1)} dynamic-update-slice(f32[640,640]{0,1:T(8,128)S(1)} %scatter.45, f32[64,576]{0,1:T(8,128)S(1)} %copy-done.7, s32[]{:T(128)} %constant.306.clone.1, s32[]{:T(128)} %constant.290.clone.1) | dynamic-update-slice | bytes 294916 | tf_op jit(solution)/shard_map/scatter | solution.py:158
  91.1 2.3 %scatter.49 = f32[640,640]{0,1:T(8,128)S(1)} dynamic-update-slice(f32[640,640]{0,1:T(8,128)S(1)} %scatter.46, f32[1,577]{0,1:T(8,128)S(1)} %reshape.450, s32[]{:T(128)} %constant.307.clone.1, s32[]{:T(128)} %constant.290.clone.1) | dynamic-update-slice | bytes 4620 | tf_op jit(solution)/shard_map/scatter | solution.py:160
  93.4 1.1 copy.58
  94.5 1.4 fusion.g_ref
  95.9 87.3 %shard_map.68 = (f32[640,640]{1,0:T(8,128)}, f32[8,640]{1,0:T(8,128)}) custom-call(f32[640,640]{1,0:T(8,128)} %fusion.g_ref), custom_call_target="tpu_custom_call" | custom-call | tf_op jit(solution)/shard_map/pallas_call | solution.py:91
  183.2 1.5 slice_bitcast_fusion
  184.7 1.6 copy.59
  186.3 0.7 fusion.8
  187.0 0.6 subtract_multiply_fusion.1
  (114 shorter events, 5.0 us)
Async XLA Ops:
  10.7 1.9 collective-permute-start
  12.7 7.9 %collective-permute-start.1 = (f32[46592]{0:T(1024)S(1)}, f32[46592]{0:T(1024)S(1)}, u32[]{:S(2)}, u32[]{:S(2)}) collective-permute-start(f32[46592]{0:T(1024)S(1)} %slice_select_fusion.1), channel_id=1, source_target_pairs={{0,2},{1,3},{2,0},{3,1},{4,6},{5,7},{6,4},{7,5},{8,10},{9,11},{10,... | collective-permute-start | bytes 559112 | tf_op jit(solution)/shard_map/ppermute | solution.py:112
  20.7 4.6 %collective-permute-start.2 = (f32[23296]{0:T(1024)S(1)}, f32[23296]{0:T(1024)S(1)}, u32[]{:S(2)}, u32[]{:S(2)}) collective-permute-start(f32[23296]{0:T(1024)S(1)} %slice_select_fusion.2), channel_id=1, source_target_pairs={{0,4},{1,5},{2,6},{3,7},{4,0},{5,1},{6,2},{7,3},{8,12},{9,13},{10,... | collective-permute-start | bytes 279560 | tf_op jit(solution)/shard_map/ppermute | solution.py:112
  25.4 5.1 %collective-permute-start.3 = (f32[11648]{0:T(1024)S(1)}, f32[11648]{0:T(1024)S(1)}, u32[]{:S(2)}, u32[]{:S(2)}) collective-permute-start(f32[11648]{0:T(1024)S(1)} %slice_select_fusion.3), channel_id=1, source_target_pairs={{0,8},{1,9},{2,10},{3,11},{4,12},{5,13},{6,14},{7,15},{8,0},{9,1},... | collective-permute-start | bytes 139784 | tf_op jit(solution)/shard_map/ppermute | solution.py:112
  30.5 5.2 %collective-permute-start.4 = (f32[11648]{0:T(1024)S(1)}, f32[11648]{0:T(1024)S(1)}, u32[]{:S(2)}, u32[]{:S(2)}) collective-permute-start(f32[11648]{0:T(1024)S(1)} %select_add_fusion.3), channel_id=1, source_target_pairs={{0,8},{1,9},{2,10},{3,11},{4,12},{5,13},{6,14},{7,15},{8,0},{9,1},... | collective-permute-start | bytes 139784 | tf_op jit(solution)/shard_map/ppermute | solution.py:115
  35.6 4.7 %collective-permute-start.5 = (f32[23296]{0:T(1024)S(1)}, f32[23296]{0:T(1024)S(1)}, u32[]{:S(2)}, u32[]{:S(2)}) collective-permute-start(f32[23296]{0:T(1024)S(1)} %maximum_select_fusion.15), channel_id=1, source_target_pairs={{0,4},{1,5},{2,6},{3,7},{4,0},{5,1},{6,2},{7,3},{8,12},{9,13},{10,... | collective-permute-start | bytes 279560 | tf_op jit(solution)/shard_map/ppermute | solution.py:115
  40.4 5.6 %collective-permute-start.6 = (f32[46592]{0:T(1024)S(1)}, f32[46592]{0:T(1024)S(1)}, u32[]{:S(2)}, u32[]{:S(2)}) collective-permute-start(f32[46592]{0:T(1024)S(1)} %maximum_select_fusion.12), channel_id=1, source_target_pairs={{0,2},{1,3},{2,0},{3,1},{4,6},{5,7},{6,4},{7,5},{8,10},{9,11},{10,... | collective-permute-start | bytes 559112 | tf_op jit(solution)/shard_map/ppermute | solution.py:115
  46.1 4.6 %collective-permute-start.7 = (f32[93184]{0:T(1024)S(1)}, f32[93184]{0:T(1024)S(1)}, u32[]{:S(2)}, u32[]{:S(2)}) collective-permute-start(f32[93184]{0:T(1024)S(1)} %maximum_select_fusion.6), channel_id=1, source_target_pairs={{0,1},{1,0},{2,3},{3,2},{4,5},{5,4},{6,7},{7,6},{8,9},{9,8},{10,11... | collective-permute-start | bytes 1118216 | tf_op jit(solution)/shard_map/ppermute | solution.py:115
  50.8 0.9 copy-start.2
  56.0 1.2 slice-start
  56.2 3.4 %slice-start.1 = ((f32[186368]{0:T(1024)}), f32[24576]{0:T(1024)S(1)}, s32[]{:S(2)}) async-start(f32[186368]{0:T(1024)} %copy-done.2), calls=%async_computation.1 | async-start | bytes 196608 | tf_op jit(solution)/shard_map/slice | solution.py:157
  56.3 5.8 %slice-start.2 = ((f32[186368]{0:T(1024)}), f32[36864]{0:T(1024)S(1)}, s32[]{:S(2)}) async-start(f32[186368]{0:T(1024)} %copy-done.2), calls=%async_computation.2 | async-start | bytes 294912 | tf_op jit(solution)/shard_map/slice | solution.py:157
  57.1 5.9 %slice-start.3 = ((f32[186368]{0:T(1024)}), f32[577]{0:T(1024)S(1)}, s32[]{:S(2)}) async-start(f32[186368]{0:T(1024)} %copy-done.2), calls=%async_computation.3 | async-start | bytes 8192 | tf_op jit(solution)/shard_map/slice | solution.py:160
  63.0 1.2 copy-start.1
  63.0 1.5 copy-start.3
  63.0 1.5 copy-start.4
  63.1 1.6 copy-start.5
  63.1 1.6 copy-start.6
  64.2 2.7 %copy-start.11 = (f32[64,192]{0,1:T(8,128)S(1)}, f32[64,192]{0,1:T(8,128)}, u32[]{:S(2)}) copy-start(f32[64,192]{0,1:T(8,128)} %copy.29) | copy-start | bytes 147460
  64.2 11.6 %copy-start.9 = (f32[64,384]{0,1:T(8,128)S(1)}, f32[64,384]{0,1:T(8,128)}, u32[]{:S(2)}) copy-start(f32[64,384]{0,1:T(8,128)} %copy.39) | copy-start | bytes 294916
  64.5 8.0 %copy-start.10 = (f32[64,320]{0,1:T(8,128)S(1)}, f32[64,320]{0,1:T(8,128)}, u32[]{:S(2)}) copy-start(f32[64,320]{0,1:T(8,128)} %copy.38) | copy-start | bytes 245764
  64.5 19.1 %copy-start.8 = (f32[64,512]{0,1:T(8,128)S(1)}, f32[64,512]{0,1:T(8,128)}, u32[]{:S(2)}) copy-start(f32[64,512]{0,1:T(8,128)} %fusion.6) | copy-start | bytes 393220
  64.7 23.7 %copy-start.7 = (f32[64,576]{0,1:T(8,128)S(1)}, f32[64,576]{0,1:T(8,128)}, u32[]{:S(2)}) copy-start(f32[64,576]{0,1:T(8,128)} %copy.56) | copy-start | bytes 442372
  184.7 1.6 copy-start
  184.7 1.6 copy-start.12
where the time goes:
time: 188 us
  Pallas kernels  87.3 us (46%)
  local copies, waits for them, and re-layouts  49.8 us (26%)
  waiting for transfers between devices  16.8 us (9%)
  starting transfers between devices  15.2 us (8%)
  other arithmetic  11.4 us (6%)
  matrix products  5.12 us (3%)
  between operations  2.1 us (1%)
    pallas_call x1, Pallas kernels, cholesky_and_solve(): pl.pallas_call(kernel, out_shape=(jax.ShapeDtypeStruct((n, n), jnp.float3...  87.3 us
    scatter x9, local copies, waits for them, and re-layouts, shards(): lower_gram = lower_gram.at[k * PB:(k + 1) * PB, :(k + 1) * PB].set(block)  26.3 us
    ppermute x4, waiting for transfers between devices, butterfly_sum(): current = keep + lax.ppermute(send, axis, pairs)  11.2 us
    ppermute x4, starting transfers between devices, butterfly_sum(): current = keep + lax.ppermute(send, axis, pairs)  8.26 us
    select_n x21, other arithmetic, butterfly_sum(): jnp.where(upper_half, jnp.concatenate([got, current]), jnp.concatenate([c...  7.19 us
    ppermute x4, starting transfers between devices, butterfly_sum(): got = lax.ppermute(current, axis, pairs)  6.91 us
    another operation x9, local copies, waits for them, and re-layouts  6.7 us
    concatenate x35, local copies, waits for them, and re-layouts, butterfly_sum(): jnp.concatenate([got, current])  6.31 us
  transfers between devices with their start and end apart: 8, of which 7 were waited for; matrix products, arithmetic and copies ran while one was open for 4% of the time, Pallas kernels for 0%

commit v1 on v0

--- a/solution.py
+++ b/solution.py
@@ -32,7 +32,14 @@
     lane_row = lax.broadcasted_iota(jnp.int32, (1, b), 1)
     sub_col = lax.broadcasted_iota(jnp.int32, (b, 1), 0)
     eye = jnp.where(lane == sub, 1.0, 0.0).astype(jnp.float32)
-    l_ref[...] = g_ref[...]
+    index = 0
+    for i in range(blocks):
+        for k in range(blocks):
+            if k <= i:
+                l_ref[i * b:(i + 1) * b, k * b:(k + 1) * b] = g_ref[index * b:(index + 1) * b, :]
+                index += 1
+            else:
+                l_ref[i * b:(i + 1) * b, k * b:(k + 1) * b] = jnp.zeros((b, b), jnp.float32)
     inverses = []
     for k in range(blocks):
         r0 = k * b
@@ -82,9 +89,8 @@
         z_ref[:, k * b:(k + 1) * b] = zk
 
 
-def cholesky_and_solve(sym, target):
-    n = sym.shape[0]
-    blocks = n // BLOCK
+def cholesky_and_solve(sym, target, blocks):
+    n = blocks * BLOCK
     last_steps = target + 1 - (blocks - 1) * BLOCK
     kernel = functools.partial(chol_kernel, blocks=blocks, last_steps=last_steps, target=target)
     vmem = pltpu.VMEM
@@ -139,30 +145,24 @@
     ) * norm_scale
     working = jnp.concatenate([scaled, target[None, :]], axis=0)
     width = window + 1
+    blocks = -(-width // BLOCK)
+    size = blocks * BLOCK
+    working = jnp.concatenate([working, jnp.zeros((size - width, rows_here), jnp.float32)], axis=0)
     local_gram = lax.dot_general(
         working, working, (((1,), (1,)), ((), ())), precision=precise
     )
-    panels = window // PB
-    pieces = [local_gram[k * PB:(k + 1) * PB, :(k + 1) * PB].reshape(-1) for k in range(panels)]
-    pieces.append(local_gram[window])
-    used = sum(p.shape[0] for p in pieces)
-    quantum = row_devices * 128
+    pieces = [
+        local_gram[i * BLOCK:(i + 1) * BLOCK, k * BLOCK:(k + 1) * BLOCK]
+        for i in range(blocks)
+        for k in range(i + 1)
+    ]
+    used = len(pieces) * BLOCK
+    quantum = row_devices * 8
     padded = -(-used // quantum) * quantum
-    pieces.append(jnp.zeros((padded - used,), jnp.float32))
-    packed = butterfly_sum(jnp.concatenate(pieces), "row")
-    size = -(-width // BLOCK) * BLOCK
-    lower_gram = jnp.zeros((size, size), jnp.float32)
-    offset = 0
-    for k in range(panels):
-        block = packed[offset:offset + PB * (k + 1) * PB].reshape(PB, (k + 1) * PB)
-        lower_gram = lower_gram.at[k * PB:(k + 1) * PB, :(k + 1) * PB].set(block)
-        offset += PB * (k + 1) * PB
-    lower_gram = lower_gram.at[window, :width].set(packed[offset:offset + width])
-    rows = lax.broadcasted_iota(jnp.int32, (size, size), 0)
-    cols = lax.broadcasted_iota(jnp.int32, (size, size), 1)
-    sym = jnp.where(rows >= cols, lower_gram, lower_gram.T)
-    sym = jnp.where((rows == cols) & (rows >= width), 1.0, sym)
-    lower, solved = cholesky_and_solve(sym, window)
+    if padded > used:
+        pieces.append(jnp.zeros((padded - used, BLOCK), jnp.float32))
+    packed = butterfly_sum(jnp.concatenate(pieces, axis=0), "row")
+    lower, solved = cholesky_and_solve(packed, window, blocks)
     lower_window = lower[:window, :window]
     coef = solved[0, :window]
     fitted_part = jnp.dot(coef, scaled, precision=precise)

time: 188 us -> 142 us (0.76)
  local copies, waits for them, and re-layouts: 49.8 us -> 4.03 us
  waiting for transfers between devices: 16.8 us -> 24.8 us
  other arithmetic: 11.4 us -> 3.86 us
    scatter x11 -> x0, local copies, waits for them, and re-layouts: 29.7 us -> none  [the longest x9 26.3 us: shards(): lower_gram = lower_gram.at[k * PB:(k + 1) * PB, :(k + 1) * PB].set(block)]
    concatenate x37 -> x2, local copies, waits for them, and re-layouts: 7.71 us -> 0.09 us  [the longest x1 0.07 us: shards(): jnp.concatenate([working, jnp.zeros((size - width, rows_here), jnp.float3...]
    another operation x9 -> x0, local copies, waits for them, and re-layouts: 6.7 us -> none
    ppermute x4, waiting for transfers between devices: 5.54 us -> 11.7 us  [butterfly_sum(): got = lax.ppermute(current, axis, pairs)]
    select_n x21 -> x4, other arithmetic: 7.19 us -> 1.07 us  [butterfly_sum(): jnp.where(upper_half, jnp.concatenate([got, current]), jnp.concatenate([c...]
  transfers between devices with their start and end apart: 8 -> 8, of which waited for: 7 -> 8; matrix products, arithmetic and copies ran while one was open for 4% -> 0% of each run, Pallas kernels for 0% -> 0%
where the time goes in v1:
time: 142 us
  Pallas kernels  87.1 us (61%)
  waiting for transfers between devices  24.8 us (17%)
  starting transfers between devices  15.1 us (11%)
  matrix products  5.56 us (4%)
  local copies, waits for them, and re-layouts  4.03 us (3%)
  other arithmetic  3.86 us (3%)
  between operations  1.48 us (1%)
    pallas_call x1, Pallas kernels, cholesky_and_solve(): pl.pallas_call(kernel, out_shape=(jax.ShapeDtypeStruct((n, n), jnp.float3...  87.1 us
    ppermute x4, waiting for transfers between devices, butterfly_sum(): current = keep + lax.ppermute(send, axis, pairs)  13.1 us
    ppermute x4, waiting for transfers between devices, butterfly_sum(): got = lax.ppermute(current, axis, pairs)  11.7 us
    ppermute x4, starting transfers between devices, butterfly_sum(): current = keep + lax.ppermute(send, axis, pairs)  8.26 us
    ppermute x4, starting transfers between devices, butterfly_sum(): got = lax.ppermute(current, axis, pairs)  6.85 us
    dot_general x1, matrix products, shards(): lax.dot_general(working, working, (((1,), (1,)), ((), ())), precision=pre...  3.44 us
  transfers between devices with their start and end apart: 8, of which 8 were waited for; matrix products, arithmetic and copies ran while one was open for 0% of the time, Pallas kernels for 0%

profile of v1, /device:TPU:0, one launch (start us, length us, event | category | flops | bytes accessed | tf_op | source)
XLA Modules:
  0.0 141.9 jit_solution(9769758979071469125)
XLA Ops:
  1.3 0.8 dynamic_slice.3
  2.1 1.4 fusion.13
  3.5 0.7 fusion.11
  4.2 1.2 convert_multiply_fusion
  5.4 0.1 pad.18.clone
  5.5 3.4 %fusion = f32[640,640]{1,0:T(8,128)S(1)} fusion(f32[1,512]{1,0:T(1,128)S(1)} %bitcast.11, f32[576,512]{1,0:T(8,128)S(1)} %convert_multiply_fusion, f32[640]{0:T(1024)S(1)} %pad.18.clone), kind=kOutput, calls=%fused_computation.1 | convolution fusion | flops 2517237760 | bytes 2822656 | tf_op jit(solution)/shard_map/dot_general | solution.py:151
  9.1 0.1 slice_select_fusion
  9.2 0.6 collective-permute-start
  9.8 1.5 %collective-permute-done = f32[960,128]{1,0:T(8,128)S(1)} collective-permute-done((f32[960,128]{1,0:T(8,128)S(1)}, f32[960,128]{1,0:T(8,128)S(1)}, u32[]{:S(2)}, u32[]{:S(2)}) %collective-permute-start) | collective-permute-done | bytes 491552 | tf_op jit(solution)/shard_map/ppermute | solution.py:118
  11.2 0.1 select_add_fusion
  11.4 2.9 %collective-permute-start.1 = (f32[480,128]{1,0:T(8,128)S(1)}, f32[480,128]{1,0:T(8,128)S(1)}, u32[]{:S(2)}, u32[]{:S(2)}) collective-permute-start(f32[480,128]{1,0:T(8,128)S(1)} %slice_select_fusion.1), channel_id=1, source_target_pairs={{0,2},{1,3},{2,0},{3,1},{4,6},{5,7},{6,4},{7,5},{8,10},{9,11},{10,... | collective-permute-start | bytes 737288 | tf_op jit(solution)/shard_map/ppermute | solution.py:118
  14.3 6.3 %collective-permute-done.1 = f32[480,128]{1,0:T(8,128)S(1)} collective-permute-done((f32[480,128]{1,0:T(8,128)S(1)}, f32[480,128]{1,0:T(8,128)S(1)}, u32[]{:S(2)}, u32[]{:S(2)}) %collective-permute-start.1) | collective-permute-done | bytes 245792 | tf_op jit(solution)/shard_map/ppermute | solution.py:118
  20.6 1.9 %collective-permute-start.2 = (f32[240,128]{1,0:T(8,128)S(1)}, f32[240,128]{1,0:T(8,128)S(1)}, u32[]{:S(2)}, u32[]{:S(2)}) collective-permute-start(f32[240,128]{1,0:T(8,128)S(1)} %slice_select_fusion.2), channel_id=1, source_target_pairs={{0,4},{1,5},{2,6},{3,7},{4,0},{5,1},{6,2},{7,3},{8,12},{9,13},{10,... | collective-permute-start | bytes 368648 | tf_op jit(solution)/shard_map/ppermute | solution.py:118
  22.5 3.1 %collective-permute-done.2 = f32[240,128]{1,0:T(8,128)S(1)} collective-permute-done((f32[240,128]{1,0:T(8,128)S(1)}, f32[240,128]{1,0:T(8,128)S(1)}, u32[]{:S(2)}, u32[]{:S(2)}) %collective-permute-start.2) | collective-permute-done | bytes 122912 | tf_op jit(solution)/shard_map/ppermute | solution.py:118
  25.6 2.9 %collective-permute-start.3 = (f32[120,128]{1,0:T(8,128)S(1)}, f32[120,128]{1,0:T(8,128)S(1)}, u32[]{:S(2)}, u32[]{:S(2)}) collective-permute-start(f32[120,128]{1,0:T(8,128)S(1)} %slice_select_fusion.3), channel_id=1, source_target_pairs={{0,8},{1,9},{2,10},{3,11},{4,12},{5,13},{6,14},{7,15},{8,0},{9,1},... | collective-permute-start | bytes 184328 | tf_op jit(solution)/shard_map/ppermute | solution.py:118
  28.5 2.3 %collective-permute-done.3 = f32[120,128]{1,0:T(8,128)S(1)} collective-permute-done((f32[120,128]{1,0:T(8,128)S(1)}, f32[120,128]{1,0:T(8,128)S(1)}, u32[]{:S(2)}, u32[]{:S(2)}) %collective-permute-start.3) | collective-permute-done | bytes 61472 | tf_op jit(solution)/shard_map/ppermute | solution.py:118
  30.8 3.0 %collective-permute-start.4 = (f32[120,128]{1,0:T(8,128)S(1)}, f32[120,128]{1,0:T(8,128)S(1)}, u32[]{:S(2)}, u32[]{:S(2)}) collective-permute-start(f32[120,128]{1,0:T(8,128)S(1)} %select_add_fusion.3), channel_id=1, source_target_pairs={{0,8},{1,9},{2,10},{3,11},{4,12},{5,13},{6,14},{7,15},{8,0},{9,1},... | collective-permute-start | bytes 184328 | tf_op jit(solution)/shard_map/ppermute | solution.py:121
  33.7 2.4 %collective-permute-done.4 = f32[120,128]{1,0:T(8,128)S(1)} collective-permute-done((f32[120,128]{1,0:T(8,128)S(1)}, f32[120,128]{1,0:T(8,128)S(1)}, u32[]{:S(2)}, u32[]{:S(2)}) %collective-permute-start.4) | collective-permute-done | bytes 61472 | tf_op jit(solution)/shard_map/ppermute | solution.py:121
  36.1 2.2 %collective-permute-start.5 = (f32[240,128]{1,0:T(8,128)S(1)}, f32[240,128]{1,0:T(8,128)S(1)}, u32[]{:S(2)}, u32[]{:S(2)}) collective-permute-start(f32[240,128]{1,0:T(8,128)S(1)} %maximum_select_fusion.3), channel_id=1, source_target_pairs={{0,4},{1,5},{2,6},{3,7},{4,0},{5,1},{6,2},{7,3},{8,12},{9,13},{10,... | collective-permute-start | bytes 368648 | tf_op jit(solution)/shard_map/ppermute | solution.py:121
  38.3 2.9 %collective-permute-done.5 = f32[240,128]{1,0:T(8,128)S(1)} collective-permute-done((f32[240,128]{1,0:T(8,128)S(1)}, f32[240,128]{1,0:T(8,128)S(1)}, u32[]{:S(2)}, u32[]{:S(2)}) %collective-permute-start.5) | collective-permute-done | bytes 122912 | tf_op jit(solution)/shard_map/ppermute | solution.py:121
  41.2 1.7 %collective-permute-start.6 = (f32[480,128]{1,0:T(8,128)S(1)}, f32[480,128]{1,0:T(8,128)S(1)}, u32[]{:S(2)}, u32[]{:S(2)}) collective-permute-start(f32[480,128]{1,0:T(8,128)S(1)} %maximum_select_fusion.2), channel_id=1, source_target_pairs={{0,2},{1,3},{2,0},{3,1},{4,6},{5,7},{6,4},{7,5},{8,10},{9,11},{10,... | collective-permute-start | bytes 737288 | tf_op jit(solution)/shard_map/ppermute | solution.py:121
  42.8 4.6 %collective-permute-done.6 = f32[480,128]{1,0:T(8,128)S(1)} collective-permute-done((f32[480,128]{1,0:T(8,128)S(1)}, f32[480,128]{1,0:T(8,128)S(1)}, u32[]{:S(2)}, u32[]{:S(2)}) %collective-permute-start.6) | collective-permute-done | bytes 245792 | tf_op jit(solution)/shard_map/ppermute | solution.py:121
  47.5 0.1 collective-permute-start.7
  47.6 1.9 %collective-permute-done.7 = f32[960,128]{1,0:T(8,128)S(1)} collective-permute-done((f32[960,128]{1,0:T(8,128)S(1)}, f32[960,128]{1,0:T(8,128)S(1)}, u32[]{:S(2)}, u32[]{:S(2)}) %collective-permute-start.7) | collective-permute-done | bytes 491552 | tf_op jit(solution)/shard_map/ppermute | solution.py:121
  49.4 1.0 maximum_select_fusion.g_ref
  50.4 87.1 %shard_map.68 = (f32[640,640]{1,0:T(8,128)}, f32[8,640]{1,0:T(8,128)}) custom-call(f32[1920,128]{1,0:T(8,128)} %maximum_select_fusion.g_ref), custom_call_target="tpu_custom_call" | custom-call | tf_op jit(solution)/shard_map/pallas_call | solution.py:97
  137.5 1.5 %slice_bitcast_fusion = f32[576,576]{0,1:T(8,128)S(1)} fusion(f32[640,640]{1,0:T(8,128)} %get-tuple-element.4), kind=kLoop, calls=%fused_computation | loop fusion | bytes 2654208 | tf_op jit(solution)/shard_map/transpose | solution.py:170
  139.0 0.0 copy-start
  139.0 0.0 copy-start.1
  139.0 1.6 %copy.7 = f32[576,576]{1,0:T(8,128)} copy(f32[576,576]{0,1:T(8,128)S(1)} %slice_bitcast_fusion) | data formatting | bytes 2654208
  140.6 0.0 copy-done
  140.6 0.0 copy-done.1
  140.6 0.7 fusion.6
  141.3 0.6 subtract_multiply_fusion.1
  (20 shorter events, 0.3 us)
Async XLA Ops:
  9.2 2.0 %collective-permute-start = (f32[960,128]{1,0:T(8,128)S(1)}, f32[960,128]{1,0:T(8,128)S(1)}, u32[]{:S(2)}, u32[]{:S(2)}) collective-permute-start(f32[960,128]{1,0:T(8,128)S(1)} %slice_select_fusion), channel_id=1, source_target_pairs={{0,1},{1,0},{2,3},{3,2},{4,5},{5,4},{6,7},{7,6},{8,9},{9,8},{10,11... | collective-permute-start | bytes 1474568 | tf_op jit(solution)/shard_map/ppermute | solution.py:118
  11.4 9.2 %collective-permute-start.1 = (f32[480,128]{1,0:T(8,128)S(1)}, f32[480,128]{1,0:T(8,128)S(1)}, u32[]{:S(2)}, u32[]{:S(2)}) collective-permute-start(f32[480,128]{1,0:T(8,128)S(1)} %slice_select_fusion.1), channel_id=1, source_target_pairs={{0,2},{1,3},{2,0},{3,1},{4,6},{5,7},{6,4},{7,5},{8,10},{9,11},{10,... | collective-permute-start | bytes 737288 | tf_op jit(solution)/shard_map/ppermute | solution.py:118
  20.6 4.9 %collective-permute-start.2 = (f32[240,128]{1,0:T(8,128)S(1)}, f32[240,128]{1,0:T(8,128)S(1)}, u32[]{:S(2)}, u32[]{:S(2)}) collective-permute-start(f32[240,128]{1,0:T(8,128)S(1)} %slice_select_fusion.2), channel_id=1, source_target_pairs={{0,4},{1,5},{2,6},{3,7},{4,0},{5,1},{6,2},{7,3},{8,12},{9,13},{10,... | collective-permute-start | bytes 368648 | tf_op jit(solution)/shard_map/ppermute | solution.py:118
  25.6 5.2 %collective-permute-start.3 = (f32[120,128]{1,0:T(8,128)S(1)}, f32[120,128]{1,0:T(8,128)S(1)}, u32[]{:S(2)}, u32[]{:S(2)}) collective-permute-start(f32[120,128]{1,0:T(8,128)S(1)} %slice_select_fusion.3), channel_id=1, source_target_pairs={{0,8},{1,9},{2,10},{3,11},{4,12},{5,13},{6,14},{7,15},{8,0},{9,1},... | collective-permute-start | bytes 184328 | tf_op jit(solution)/shard_map/ppermute | solution.py:118
  30.8 5.4 %collective-permute-start.4 = (f32[120,128]{1,0:T(8,128)S(1)}, f32[120,128]{1,0:T(8,128)S(1)}, u32[]{:S(2)}, u32[]{:S(2)}) collective-permute-start(f32[120,128]{1,0:T(8,128)S(1)} %select_add_fusion.3), channel_id=1, source_target_pairs={{0,8},{1,9},{2,10},{3,11},{4,12},{5,13},{6,14},{7,15},{8,0},{9,1},... | collective-permute-start | bytes 184328 | tf_op jit(solution)/shard_map/ppermute | solution.py:121
  36.1 5.0 %collective-permute-start.5 = (f32[240,128]{1,0:T(8,128)S(1)}, f32[240,128]{1,0:T(8,128)S(1)}, u32[]{:S(2)}, u32[]{:S(2)}) collective-permute-start(f32[240,128]{1,0:T(8,128)S(1)} %maximum_select_fusion.3), channel_id=1, source_target_pairs={{0,4},{1,5},{2,6},{3,7},{4,0},{5,1},{6,2},{7,3},{8,12},{9,13},{10,... | collective-permute-start | bytes 368648 | tf_op jit(solution)/shard_map/ppermute | solution.py:121
  41.2 6.3 %collective-permute-start.6 = (f32[480,128]{1,0:T(8,128)S(1)}, f32[480,128]{1,0:T(8,128)S(1)}, u32[]{:S(2)}, u32[]{:S(2)}) collective-permute-start(f32[480,128]{1,0:T(8,128)S(1)} %maximum_select_fusion.2), channel_id=1, source_target_pairs={{0,2},{1,3},{2,0},{3,1},{4,6},{5,7},{6,4},{7,5},{8,10},{9,11},{10,... | collective-permute-start | bytes 737288 | tf_op jit(solution)/shard_map/ppermute | solution.py:121
  47.5 1.9 %collective-permute-start.7 = (f32[960,128]{1,0:T(8,128)S(1)}, f32[960,128]{1,0:T(8,128)S(1)}, u32[]{:S(2)}, u32[]{:S(2)}) collective-permute-start(f32[960,128]{1,0:T(8,128)S(1)} %maximum_select_fusion.1), channel_id=1, source_target_pairs={{0,1},{1,0},{2,3},{3,2},{4,5},{5,4},{6,7},{7,6},{8,9},{9,8},{10,11... | collective-permute-start | bytes 1474568 | tf_op jit(solution)/shard_map/ppermute | solution.py:121
  139.0 1.6 %copy-start = (bf16[576,512]{1,0:T(8,128)(2,1)S(1)}, bf16[576,512]{1,0:T(8,128)(2,1)}, u32[]{:S(2)}) copy-start(bf16[576,512]{1,0:T(8,128)(2,1)} %param.5) | copy-start | bytes 1769476
  139.0 1.6 %copy-start.1 = (f32[8,640]{1,0:T(8,128)S(1)}, f32[8,640]{1,0:T(8,128)}, u32[]{:S(2)}) copy-start(f32[8,640]{1,0:T(8,128)} %get-tuple-element.5) | copy-start | bytes 61444

commit v2 on v1

--- a/solution.py
+++ b/solution.py
@@ -47,25 +47,32 @@
         m_ref[...] = eye
         k_ref[...] = jnp.zeros((b, b), jnp.float32)
 
-        def step(j, carry):
-            d = d_ref[...]
-            col = jnp.sum(jnp.where(lane == j, d, 0.0), axis=1, keepdims=True)
-            piv = jnp.sum(jnp.where(sub_col == j, col, 0.0), axis=0, keepdims=True)
-            inv = lax.rsqrt(piv)
-            lcol = jnp.where(sub_col >= j, col * inv, 0.0)
-            lrow = jnp.where(lane_row >= j, d_ref[pl.ds(j, 1), :] * inv, 0.0)
-            d_ref[...] = d - lcol * lrow
-            k_ref[...] = jnp.where(lane == j, lcol, k_ref[...])
-            mrow = m_ref[pl.ds(j, 1), :] * inv
-            below = jnp.where(sub_col > j, lcol, 0.0)
-            m_ref[...] = jnp.where(sub == j, mrow, m_ref[...] - below * mrow)
-            return carry
+        steps = b if k < blocks - 1 else last_steps
+        for tile in range(-(-steps // 8)):
+            top = tile * 8
+            rows = b - top
+            lane_t = lane[top:, :]
+            sub_t = sub[top:, :]
+            sub_col_t = sub_col[top:, :]
 
-        steps = b if k < blocks - 1 else last_steps
-        lax.fori_loop(0, steps, step, 0)
+            def step(j, carry, top=top, lane_t=lane_t, sub_t=sub_t, sub_col_t=sub_col_t):
+                d = d_ref[top:, :]
+                col = jnp.sum(jnp.where(lane_t == j, d, 0.0), axis=1, keepdims=True)
+                piv = jnp.sum(jnp.where(sub_col_t == j, col, 0.0), axis=0, keepdims=True)
+                inv = lax.rsqrt(piv)
+                lcol = jnp.where(sub_col_t >= j, col * inv, 0.0)
+                lrow = jnp.where(lane_row >= j, d_ref[pl.ds(j, 1), :] * inv, 0.0)
+                d_ref[top:, :] = d - lcol * lrow
+                k_ref[pl.ds(j, 1), :] = lrow
+                mrow = m_ref[pl.ds(j, 1), :] * inv
+                below = jnp.where(sub_col_t > j, lcol, 0.0)
+                m_ref[top:, :] = jnp.where(sub_t == j, mrow, m_ref[top:, :] - below * mrow)
+                return carry
+
+            lax.fori_loop(top, min(top + 8, steps), step, 0)
         inverse = m_ref[...]
         inverses.append(inverse)
-        l_ref[r0:r0 + b, r0:r0 + b] = k_ref[...]
+        l_ref[r0:r0 + b, r0:r0 + b] = k_ref[...].T
         if k < blocks - 1:
             panel = nt(l_ref[r0 + b:, r0:r0 + b], inverse)
             l_ref[r0 + b:, r0:r0 + b] = panel

time: 142 us -> 130 us (0.915)
  Pallas kernels: 87.1 us -> 75.2 us
    pallas_call x1, Pallas kernels: 87.1 us -> 75.2 us  [cholesky_and_solve(): pl.pallas_call(kernel, out_shape=(jax.ShapeDtypeStruct((n, n), jnp.float3...]
where the time goes in v2:
time: 130 us
  Pallas kernels  75.2 us (58%)
  waiting for transfers between devices  24.8 us (19%)
  starting transfers between devices  15.1 us (12%)
  matrix products  5.56 us (4%)
  local copies, waits for them, and re-layouts  4.03 us (3%)
  other arithmetic  3.86 us (3%)
  between operations  1.48 us (1%)
    pallas_call x1, Pallas kernels, cholesky_and_solve(): pl.pallas_call(kernel, out_shape=(jax.ShapeDtypeStruct((n, n), jnp.float3...  75.2 us
    ppermute x4, waiting for transfers between devices, butterfly_sum(): current = keep + lax.ppermute(send, axis, pairs)  13.1 us
    ppermute x4, waiting for transfers between devices, butterfly_sum(): got = lax.ppermute(current, axis, pairs)  11.7 us
    ppermute x4, starting transfers between devices, butterfly_sum(): current = keep + lax.ppermute(send, axis, pairs)  8.26 us
    ppermute x4, starting transfers between devices, butterfly_sum(): got = lax.ppermute(current, axis, pairs)  6.85 us
    dot_general x1, matrix products, shards(): lax.dot_general(working, working, (((1,), (1,)), ((), ())), precision=pre...  3.44 us
  transfers between devices with their start and end apart: 8, of which 8 were waited for; matrix products, arithmetic and copies ran while one was open for 0% of the time, Pallas kernels for 0%

profile of v2, /device:TPU:0, one launch (start us, length us, event | category | flops | bytes accessed | tf_op | source)
XLA Modules:
  0.0 130.0 jit_solution(5520156844947722506)
XLA Ops:
  1.3 0.8 dynamic_slice.3
  2.1 1.4 %fusion.13 = f32[1,512]{1,0:T(1,128)S(1)} fusion(f32[576,1]{0,1:T(1,128)S(1)} %reshape.7, bf16[576,512]{1,0:T(8,128)(2,1)} %param.5), kind=kOutput, calls=%fused_computation.46 | convolution fusion | flops 3538944 | bytes 594176 | tf_op jit(solution)/shard_map/dot_general | solution.py:144
  3.5 0.7 fusion.11
  4.2 1.2 convert_multiply_fusion
  5.4 0.1 pad.18.clone
  5.5 3.4 %fusion = f32[640,640]{1,0:T(8,128)S(1)} fusion(f32[1,512]{1,0:T(1,128)S(1)} %bitcast.11, f32[576,512]{1,0:T(8,128)S(1)} %convert_multiply_fusion, f32[640]{0:T(1024)S(1)} %pad.18.clone), kind=kOutput, calls=%fused_computation.1 | convolution fusion | flops 2517237760 | bytes 2822656 | tf_op jit(solution)/shard_map/dot_general | solution.py:158
  9.1 0.1 slice_select_fusion
  9.2 0.6 collective-permute-start
  9.8 1.5 %collective-permute-done = f32[960,128]{1,0:T(8,128)S(1)} collective-permute-done((f32[960,128]{1,0:T(8,128)S(1)}, f32[960,128]{1,0:T(8,128)S(1)}, u32[]{:S(2)}, u32[]{:S(2)}) %collective-permute-start) | collective-permute-done | bytes 491552 | tf_op jit(solution)/shard_map/ppermute | solution.py:125
  11.2 0.1 select_add_fusion
  11.4 2.9 %collective-permute-start.1 = (f32[480,128]{1,0:T(8,128)S(1)}, f32[480,128]{1,0:T(8,128)S(1)}, u32[]{:S(2)}, u32[]{:S(2)}) collective-permute-start(f32[480,128]{1,0:T(8,128)S(1)} %slice_select_fusion.1), channel_id=1, source_target_pairs={{0,2},{1,3},{2,0},{3,1},{4,6},{5,7},{6,4},{7,5},{8,10},{9,11},{10,... | collective-permute-start | bytes 737288 | tf_op jit(solution)/shard_map/ppermute | solution.py:125
  14.3 6.3 %collective-permute-done.1 = f32[480,128]{1,0:T(8,128)S(1)} collective-permute-done((f32[480,128]{1,0:T(8,128)S(1)}, f32[480,128]{1,0:T(8,128)S(1)}, u32[]{:S(2)}, u32[]{:S(2)}) %collective-permute-start.1) | collective-permute-done | bytes 245792 | tf_op jit(solution)/shard_map/ppermute | solution.py:125
  20.6 1.9 %collective-permute-start.2 = (f32[240,128]{1,0:T(8,128)S(1)}, f32[240,128]{1,0:T(8,128)S(1)}, u32[]{:S(2)}, u32[]{:S(2)}) collective-permute-start(f32[240,128]{1,0:T(8,128)S(1)} %slice_select_fusion.2), channel_id=1, source_target_pairs={{0,4},{1,5},{2,6},{3,7},{4,0},{5,1},{6,2},{7,3},{8,12},{9,13},{10,... | collective-permute-start | bytes 368648 | tf_op jit(solution)/shard_map/ppermute | solution.py:125
  22.5 3.1 %collective-permute-done.2 = f32[240,128]{1,0:T(8,128)S(1)} collective-permute-done((f32[240,128]{1,0:T(8,128)S(1)}, f32[240,128]{1,0:T(8,128)S(1)}, u32[]{:S(2)}, u32[]{:S(2)}) %collective-permute-start.2) | collective-permute-done | bytes 122912 | tf_op jit(solution)/shard_map/ppermute | solution.py:125
  25.6 2.9 %collective-permute-start.3 = (f32[120,128]{1,0:T(8,128)S(1)}, f32[120,128]{1,0:T(8,128)S(1)}, u32[]{:S(2)}, u32[]{:S(2)}) collective-permute-start(f32[120,128]{1,0:T(8,128)S(1)} %slice_select_fusion.3), channel_id=1, source_target_pairs={{0,8},{1,9},{2,10},{3,11},{4,12},{5,13},{6,14},{7,15},{8,0},{9,1},... | collective-permute-start | bytes 184328 | tf_op jit(solution)/shard_map/ppermute | solution.py:125
  28.5 2.3 %collective-permute-done.3 = f32[120,128]{1,0:T(8,128)S(1)} collective-permute-done((f32[120,128]{1,0:T(8,128)S(1)}, f32[120,128]{1,0:T(8,128)S(1)}, u32[]{:S(2)}, u32[]{:S(2)}) %collective-permute-start.3) | collective-permute-done | bytes 61472 | tf_op jit(solution)/shard_map/ppermute | solution.py:125
  30.8 3.0 %collective-permute-start.4 = (f32[120,128]{1,0:T(8,128)S(1)}, f32[120,128]{1,0:T(8,128)S(1)}, u32[]{:S(2)}, u32[]{:S(2)}) collective-permute-start(f32[120,128]{1,0:T(8,128)S(1)} %select_add_fusion.3), channel_id=1, source_target_pairs={{0,8},{1,9},{2,10},{3,11},{4,12},{5,13},{6,14},{7,15},{8,0},{9,1},... | collective-permute-start | bytes 184328 | tf_op jit(solution)/shard_map/ppermute | solution.py:128
  33.7 2.4 %collective-permute-done.4 = f32[120,128]{1,0:T(8,128)S(1)} collective-permute-done((f32[120,128]{1,0:T(8,128)S(1)}, f32[120,128]{1,0:T(8,128)S(1)}, u32[]{:S(2)}, u32[]{:S(2)}) %collective-permute-start.4) | collective-permute-done | bytes 61472 | tf_op jit(solution)/shard_map/ppermute | solution.py:128
  36.1 2.2 %collective-permute-start.5 = (f32[240,128]{1,0:T(8,128)S(1)}, f32[240,128]{1,0:T(8,128)S(1)}, u32[]{:S(2)}, u32[]{:S(2)}) collective-permute-start(f32[240,128]{1,0:T(8,128)S(1)} %maximum_select_fusion.3), channel_id=1, source_target_pairs={{0,4},{1,5},{2,6},{3,7},{4,0},{5,1},{6,2},{7,3},{8,12},{9,13},{10,... | collective-permute-start | bytes 368648 | tf_op jit(solution)/shard_map/ppermute | solution.py:128
  38.3 2.9 %collective-permute-done.5 = f32[240,128]{1,0:T(8,128)S(1)} collective-permute-done((f32[240,128]{1,0:T(8,128)S(1)}, f32[240,128]{1,0:T(8,128)S(1)}, u32[]{:S(2)}, u32[]{:S(2)}) %collective-permute-start.5) | collective-permute-done | bytes 122912 | tf_op jit(solution)/shard_map/ppermute | solution.py:128
  41.2 1.7 %collective-permute-start.6 = (f32[480,128]{1,0:T(8,128)S(1)}, f32[480,128]{1,0:T(8,128)S(1)}, u32[]{:S(2)}, u32[]{:S(2)}) collective-permute-start(f32[480,128]{1,0:T(8,128)S(1)} %maximum_select_fusion.2), channel_id=1, source_target_pairs={{0,2},{1,3},{2,0},{3,1},{4,6},{5,7},{6,4},{7,5},{8,10},{9,11},{10,... | collective-permute-start | bytes 737288 | tf_op jit(solution)/shard_map/ppermute | solution.py:128
  42.8 4.6 %collective-permute-done.6 = f32[480,128]{1,0:T(8,128)S(1)} collective-permute-done((f32[480,128]{1,0:T(8,128)S(1)}, f32[480,128]{1,0:T(8,128)S(1)}, u32[]{:S(2)}, u32[]{:S(2)}) %collective-permute-start.6) | collective-permute-done | bytes 245792 | tf_op jit(solution)/shard_map/ppermute | solution.py:128
  47.5 0.1 collective-permute-start.7
  47.6 1.9 %collective-permute-done.7 = f32[960,128]{1,0:T(8,128)S(1)} collective-permute-done((f32[960,128]{1,0:T(8,128)S(1)}, f32[960,128]{1,0:T(8,128)S(1)}, u32[]{:S(2)}, u32[]{:S(2)}) %collective-permute-start.7) | collective-permute-done | bytes 491552 | tf_op jit(solution)/shard_map/ppermute | solution.py:128
  49.4 1.0 maximum_select_fusion.g_ref
  50.4 75.2 %shard_map.68 = (f32[640,640]{1,0:T(8,128)}, f32[8,640]{1,0:T(8,128)}) custom-call(f32[1920,128]{1,0:T(8,128)} %maximum_select_fusion.g_ref), custom_call_target="tpu_custom_call" | custom-call | tf_op jit(solution)/shard_map/pallas_call | solution.py:104
  125.6 1.5 %slice_bitcast_fusion = f32[576,576]{0,1:T(8,128)S(1)} fusion(f32[640,640]{1,0:T(8,128)} %get-tuple-element.4), kind=kLoop, calls=%fused_computation | loop fusion | bytes 2654208 | tf_op jit(solution)/shard_map/transpose | solution.py:177
  127.1 0.0 copy-start
  127.1 0.0 copy-start.1
  127.1 1.6 %copy.7 = f32[576,576]{1,0:T(8,128)} copy(f32[576,576]{0,1:T(8,128)S(1)} %slice_bitcast_fusion) | data formatting | bytes 2654208
  128.7 0.0 copy-done
  128.7 0.0 copy-done.1
  128.7 0.7 fusion.6
  129.5 0.6 subtract_multiply_fusion.1
  (20 shorter events, 0.3 us)
Async XLA Ops:
  9.2 2.0 %collective-permute-start = (f32[960,128]{1,0:T(8,128)S(1)}, f32[960,128]{1,0:T(8,128)S(1)}, u32[]{:S(2)}, u32[]{:S(2)}) collective-permute-start(f32[960,128]{1,0:T(8,128)S(1)} %slice_select_fusion), channel_id=1, source_target_pairs={{0,1},{1,0},{2,3},{3,2},{4,5},{5,4},{6,7},{7,6},{8,9},{9,8},{10,11... | collective-permute-start | bytes 1474568 | tf_op jit(solution)/shard_map/ppermute | solution.py:125
  11.4 9.2 %collective-permute-start.1 = (f32[480,128]{1,0:T(8,128)S(1)}, f32[480,128]{1,0:T(8,128)S(1)}, u32[]{:S(2)}, u32[]{:S(2)}) collective-permute-start(f32[480,128]{1,0:T(8,128)S(1)} %slice_select_fusion.1), channel_id=1, source_target_pairs={{0,2},{1,3},{2,0},{3,1},{4,6},{5,7},{6,4},{7,5},{8,10},{9,11},{10,... | collective-permute-start | bytes 737288 | tf_op jit(solution)/shard_map/ppermute | solution.py:125
  20.6 4.9 %collective-permute-start.2 = (f32[240,128]{1,0:T(8,128)S(1)}, f32[240,128]{1,0:T(8,128)S(1)}, u32[]{:S(2)}, u32[]{:S(2)}) collective-permute-start(f32[240,128]{1,0:T(8,128)S(1)} %slice_select_fusion.2), channel_id=1, source_target_pairs={{0,4},{1,5},{2,6},{3,7},{4,0},{5,1},{6,2},{7,3},{8,12},{9,13},{10,... | collective-permute-start | bytes 368648 | tf_op jit(solution)/shard_map/ppermute | solution.py:125
  25.6 5.2 %collective-permute-start.3 = (f32[120,128]{1,0:T(8,128)S(1)}, f32[120,128]{1,0:T(8,128)S(1)}, u32[]{:S(2)}, u32[]{:S(2)}) collective-permute-start(f32[120,128]{1,0:T(8,128)S(1)} %slice_select_fusion.3), channel_id=1, source_target_pairs={{0,8},{1,9},{2,10},{3,11},{4,12},{5,13},{6,14},{7,15},{8,0},{9,1},... | collective-permute-start | bytes 184328 | tf_op jit(solution)/shard_map/ppermute | solution.py:125
  30.8 5.4 %collective-permute-start.4 = (f32[120,128]{1,0:T(8,128)S(1)}, f32[120,128]{1,0:T(8,128)S(1)}, u32[]{:S(2)}, u32[]{:S(2)}) collective-permute-start(f32[120,128]{1,0:T(8,128)S(1)} %select_add_fusion.3), channel_id=1, source_target_pairs={{0,8},{1,9},{2,10},{3,11},{4,12},{5,13},{6,14},{7,15},{8,0},{9,1},... | collective-permute-start | bytes 184328 | tf_op jit(solution)/shard_map/ppermute | solution.py:128
  36.1 5.0 %collective-permute-start.5 = (f32[240,128]{1,0:T(8,128)S(1)}, f32[240,128]{1,0:T(8,128)S(1)}, u32[]{:S(2)}, u32[]{:S(2)}) collective-permute-start(f32[240,128]{1,0:T(8,128)S(1)} %maximum_select_fusion.3), channel_id=1, source_target_pairs={{0,4},{1,5},{2,6},{3,7},{4,0},{5,1},{6,2},{7,3},{8,12},{9,13},{10,... | collective-permute-start | bytes 368648 | tf_op jit(solution)/shard_map/ppermute | solution.py:128
  41.2 6.3 %collective-permute-start.6 = (f32[480,128]{1,0:T(8,128)S(1)}, f32[480,128]{1,0:T(8,128)S(1)}, u32[]{:S(2)}, u32[]{:S(2)}) collective-permute-start(f32[480,128]{1,0:T(8,128)S(1)} %maximum_select_fusion.2), channel_id=1, source_target_pairs={{0,2},{1,3},{2,0},{3,1},{4,6},{5,7},{6,4},{7,5},{8,10},{9,11},{10,... | collective-permute-start | bytes 737288 | tf_op jit(solution)/shard_map/ppermute | solution.py:128
  47.5 1.9 %collective-permute-start.7 = (f32[960,128]{1,0:T(8,128)S(1)}, f32[960,128]{1,0:T(8,128)S(1)}, u32[]{:S(2)}, u32[]{:S(2)}) collective-permute-start(f32[960,128]{1,0:T(8,128)S(1)} %maximum_select_fusion.1), channel_id=1, source_target_pairs={{0,1},{1,0},{2,3},{3,2},{4,5},{5,4},{6,7},{7,6},{8,9},{9,8},{10,11... | collective-permute-start | bytes 1474568 | tf_op jit(solution)/shard_map/ppermute | solution.py:128
  127.1 1.6 %copy-start = (bf16[576,512]{1,0:T(8,128)(2,1)S(1)}, bf16[576,512]{1,0:T(8,128)(2,1)}, u32[]{:S(2)}) copy-start(bf16[576,512]{1,0:T(8,128)(2,1)} %param.5) | copy-start | bytes 1769476
  127.1 1.6 %copy-start.1 = (f32[8,640]{1,0:T(8,128)S(1)}, f32[8,640]{1,0:T(8,128)}, u32[]{:S(2)}) copy-start(f32[8,640]{1,0:T(8,128)} %get-tuple-element.5) | copy-start | bytes 61444

commit v3 on v2

--- a/solution.py
+++ b/solution.py
@@ -48,28 +48,31 @@
         k_ref[...] = jnp.zeros((b, b), jnp.float32)
 
         steps = b if k < blocks - 1 else last_steps
+        column = jnp.sum(jnp.where(lane == 0, d_ref[...], 0.0), axis=1, keepdims=True)
         for tile in range(-(-steps // 8)):
             top = tile * 8
-            rows = b - top
             lane_t = lane[top:, :]
             sub_t = sub[top:, :]
             sub_col_t = sub_col[top:, :]
 
-            def step(j, carry, top=top, lane_t=lane_t, sub_t=sub_t, sub_col_t=sub_col_t):
+            def step(j, c, top=top, lane_t=lane_t, sub_t=sub_t, sub_col_t=sub_col_t):
                 d = d_ref[top:, :]
-                col = jnp.sum(jnp.where(lane_t == j, d, 0.0), axis=1, keepdims=True)
-                piv = jnp.sum(jnp.where(sub_col_t == j, col, 0.0), axis=0, keepdims=True)
+                ahead = jnp.sum(jnp.where(lane_t == j + 1, d, 0.0), axis=1, keepdims=True)
+                piv = jnp.sum(jnp.where(sub_col_t == j, c, 0.0), axis=0, keepdims=True)
+                nxt = jnp.sum(jnp.where(sub_col_t == j + 1, c, 0.0), axis=0, keepdims=True)
                 inv = lax.rsqrt(piv)
-                lcol = jnp.where(sub_col_t >= j, col * inv, 0.0)
+                live = jnp.where(sub_col_t >= j, c, 0.0)
+                lcol = live * inv
                 lrow = jnp.where(lane_row >= j, d_ref[pl.ds(j, 1), :] * inv, 0.0)
                 d_ref[top:, :] = d - lcol * lrow
                 k_ref[pl.ds(j, 1), :] = lrow
                 mrow = m_ref[pl.ds(j, 1), :] * inv
                 below = jnp.where(sub_col_t > j, lcol, 0.0)
                 m_ref[top:, :] = jnp.where(sub_t == j, mrow, m_ref[top:, :] - below * mrow)
-                return carry
+                return ahead - live * (nxt / piv)
 
-            lax.fori_loop(top, min(top + 8, steps), step, 0)
+            column = lax.fori_loop(top, min(top + 8, steps), step, column)
+            column = column[8:]
         inverse = m_ref[...]
         inverses.append(inverse)
         l_ref[r0:r0 + b, r0:r0 + b] = k_ref[...].T

time: 130 us -> 114 us (0.88)
  Pallas kernels: 75.2 us -> 58.6 us
    pallas_call x1, Pallas kernels: 75.2 us -> 58.6 us  [cholesky_and_solve(): pl.pallas_call(kernel, out_shape=(jax.ShapeDtypeStruct((n, n), jnp.float3...]
where the time goes in v3:
time: 114 us; the launch traced here: 113 us
  Pallas kernels  58.6 us (51%)
  waiting for transfers between devices  24.8 us (22%)
  starting transfers between devices  15.1 us (13%)
  matrix products  5.56 us (5%)
  local copies, waits for them, and re-layouts  4.03 us (4%)
  other arithmetic  3.86 us (3%)
  between operations  1.48 us (1%)
    pallas_call x1, Pallas kernels, cholesky_and_solve(): pl.pallas_call(kernel, out_shape=(jax.ShapeDtypeStruct((n, n), jnp.float3...  58.6 us
    ppermute x4, waiting for transfers between devices, butterfly_sum(): current = keep + lax.ppermute(send, axis, pairs)  13.1 us
    ppermute x4, waiting for transfers between devices, butterfly_sum(): got = lax.ppermute(current, axis, pairs)  11.7 us
    ppermute x4, starting transfers between devices, butterfly_sum(): current = keep + lax.ppermute(send, axis, pairs)  8.26 us
    ppermute x4, starting transfers between devices, butterfly_sum(): got = lax.ppermute(current, axis, pairs)  6.85 us
    dot_general x1, matrix products, shards(): lax.dot_general(working, working, (((1,), (1,)), ((), ())), precision=pre...  3.44 us
  transfers between devices with their start and end apart: 8, of which 8 were waited for; matrix products, arithmetic and copies ran while one was open for 0% of the time, Pallas kernels for 0%

profile of v3, /device:TPU:0, one launch (start us, length us, event | category | flops | bytes accessed | tf_op | source)
XLA Modules:
  0.0 113.5 jit_solution(439773579115353485)
XLA Ops:
  1.3 0.8 dynamic_slice.3
  2.1 1.4 %fusion.13 = f32[1,512]{1,0:T(1,128)S(1)} fusion(f32[576,1]{0,1:T(1,128)S(1)} %reshape.7, bf16[576,512]{1,0:T(8,128)(2,1)} %param.5), kind=kOutput, calls=%fused_computation.46 | convolution fusion | flops 3538944 | bytes 594176 | tf_op jit(solution)/shard_map/dot_general | solution.py:147
  3.5 0.7 fusion.11
  4.2 1.2 %convert_multiply_fusion = f32[576,512]{1,0:T(8,128)S(1)} fusion(bf16[576,512]{1,0:T(8,128)(2,1)} %param.5, f32[512]{0:T(512)S(1)} %get-tuple-element.20), kind=kLoop, calls=%fused_computation.6 | loop fusion | flops 589824 | bytes 1771520 | tf_op jit(solution)/shard_map/mul | solution.py:152
  5.4 0.1 pad.18.clone
  5.5 3.4 %fusion = f32[640,640]{1,0:T(8,128)S(1)} fusion(f32[1,512]{1,0:T(1,128)S(1)} %bitcast.11, f32[576,512]{1,0:T(8,128)S(1)} %convert_multiply_fusion, f32[640]{0:T(1024)S(1)} %pad.18.clone), kind=kOutput, calls=%fused_computation.1 | convolution fusion | flops 2517237760 | bytes 2822656 | tf_op jit(solution)/shard_map/dot_general | solution.py:161
  9.1 0.1 slice_select_fusion
  9.2 0.6 collective-permute-start
  9.8 1.5 %collective-permute-done = f32[960,128]{1,0:T(8,128)S(1)} collective-permute-done((f32[960,128]{1,0:T(8,128)S(1)}, f32[960,128]{1,0:T(8,128)S(1)}, u32[]{:S(2)}, u32[]{:S(2)}) %collective-permute-start) | collective-permute-done | bytes 491552 | tf_op jit(solution)/shard_map/ppermute | solution.py:128
  11.2 0.1 select_add_fusion
  11.4 2.9 %collective-permute-start.1 = (f32[480,128]{1,0:T(8,128)S(1)}, f32[480,128]{1,0:T(8,128)S(1)}, u32[]{:S(2)}, u32[]{:S(2)}) collective-permute-start(f32[480,128]{1,0:T(8,128)S(1)} %slice_select_fusion.1), channel_id=1, source_target_pairs={{0,2},{1,3},{2,0},{3,1},{4,6},{5,7},{6,4},{7,5},{8,10},{9,11},{10,... | collective-permute-start | bytes 737288 | tf_op jit(solution)/shard_map/ppermute | solution.py:128
  14.3 6.3 %collective-permute-done.1 = f32[480,128]{1,0:T(8,128)S(1)} collective-permute-done((f32[480,128]{1,0:T(8,128)S(1)}, f32[480,128]{1,0:T(8,128)S(1)}, u32[]{:S(2)}, u32[]{:S(2)}) %collective-permute-start.1) | collective-permute-done | bytes 245792 | tf_op jit(solution)/shard_map/ppermute | solution.py:128
  20.6 1.9 %collective-permute-start.2 = (f32[240,128]{1,0:T(8,128)S(1)}, f32[240,128]{1,0:T(8,128)S(1)}, u32[]{:S(2)}, u32[]{:S(2)}) collective-permute-start(f32[240,128]{1,0:T(8,128)S(1)} %slice_select_fusion.2), channel_id=1, source_target_pairs={{0,4},{1,5},{2,6},{3,7},{4,0},{5,1},{6,2},{7,3},{8,12},{9,13},{10,... | collective-permute-start | bytes 368648 | tf_op jit(solution)/shard_map/ppermute | solution.py:128
  22.5 3.1 %collective-permute-done.2 = f32[240,128]{1,0:T(8,128)S(1)} collective-permute-done((f32[240,128]{1,0:T(8,128)S(1)}, f32[240,128]{1,0:T(8,128)S(1)}, u32[]{:S(2)}, u32[]{:S(2)}) %collective-permute-start.2) | collective-permute-done | bytes 122912 | tf_op jit(solution)/shard_map/ppermute | solution.py:128
  25.6 2.9 %collective-permute-start.3 = (f32[120,128]{1,0:T(8,128)S(1)}, f32[120,128]{1,0:T(8,128)S(1)}, u32[]{:S(2)}, u32[]{:S(2)}) collective-permute-start(f32[120,128]{1,0:T(8,128)S(1)} %slice_select_fusion.3), channel_id=1, source_target_pairs={{0,8},{1,9},{2,10},{3,11},{4,12},{5,13},{6,14},{7,15},{8,0},{9,1},... | collective-permute-start | bytes 184328 | tf_op jit(solution)/shard_map/ppermute | solution.py:128
  28.5 2.3 %collective-permute-done.3 = f32[120,128]{1,0:T(8,128)S(1)} collective-permute-done((f32[120,128]{1,0:T(8,128)S(1)}, f32[120,128]{1,0:T(8,128)S(1)}, u32[]{:S(2)}, u32[]{:S(2)}) %collective-permute-start.3) | collective-permute-done | bytes 61472 | tf_op jit(solution)/shard_map/ppermute | solution.py:128
  30.8 3.0 %collective-permute-start.4 = (f32[120,128]{1,0:T(8,128)S(1)}, f32[120,128]{1,0:T(8,128)S(1)}, u32[]{:S(2)}, u32[]{:S(2)}) collective-permute-start(f32[120,128]{1,0:T(8,128)S(1)} %select_add_fusion.3), channel_id=1, source_target_pairs={{0,8},{1,9},{2,10},{3,11},{4,12},{5,13},{6,14},{7,15},{8,0},{9,1},... | collective-permute-start | bytes 184328 | tf_op jit(solution)/shard_map/ppermute | solution.py:131
  33.7 2.4 %collective-permute-done.4 = f32[120,128]{1,0:T(8,128)S(1)} collective-permute-done((f32[120,128]{1,0:T(8,128)S(1)}, f32[120,128]{1,0:T(8,128)S(1)}, u32[]{:S(2)}, u32[]{:S(2)}) %collective-permute-start.4) | collective-permute-done | bytes 61472 | tf_op jit(solution)/shard_map/ppermute | solution.py:131
  36.1 2.2 %collective-permute-start.5 = (f32[240,128]{1,0:T(8,128)S(1)}, f32[240,128]{1,0:T(8,128)S(1)}, u32[]{:S(2)}, u32[]{:S(2)}) collective-permute-start(f32[240,128]{1,0:T(8,128)S(1)} %maximum_select_fusion.3), channel_id=1, source_target_pairs={{0,4},{1,5},{2,6},{3,7},{4,0},{5,1},{6,2},{7,3},{8,12},{9,13},{10,... | collective-permute-start | bytes 368648 | tf_op jit(solution)/shard_map/ppermute | solution.py:131
  38.3 2.9 %collective-permute-done.5 = f32[240,128]{1,0:T(8,128)S(1)} collective-permute-done((f32[240,128]{1,0:T(8,128)S(1)}, f32[240,128]{1,0:T(8,128)S(1)}, u32[]{:S(2)}, u32[]{:S(2)}) %collective-permute-start.5) | collective-permute-done | bytes 122912 | tf_op jit(solution)/shard_map/ppermute | solution.py:131
  41.2 1.7 %collective-permute-start.6 = (f32[480,128]{1,0:T(8,128)S(1)}, f32[480,128]{1,0:T(8,128)S(1)}, u32[]{:S(2)}, u32[]{:S(2)}) collective-permute-start(f32[480,128]{1,0:T(8,128)S(1)} %maximum_select_fusion.2), channel_id=1, source_target_pairs={{0,2},{1,3},{2,0},{3,1},{4,6},{5,7},{6,4},{7,5},{8,10},{9,11},{10,... | collective-permute-start | bytes 737288 | tf_op jit(solution)/shard_map/ppermute | solution.py:131
  42.8 4.6 %collective-permute-done.6 = f32[480,128]{1,0:T(8,128)S(1)} collective-permute-done((f32[480,128]{1,0:T(8,128)S(1)}, f32[480,128]{1,0:T(8,128)S(1)}, u32[]{:S(2)}, u32[]{:S(2)}) %collective-permute-start.6) | collective-permute-done | bytes 245792 | tf_op jit(solution)/shard_map/ppermute | solution.py:131
  47.5 0.1 collective-permute-start.7
  47.6 1.9 %collective-permute-done.7 = f32[960,128]{1,0:T(8,128)S(1)} collective-permute-done((f32[960,128]{1,0:T(8,128)S(1)}, f32[960,128]{1,0:T(8,128)S(1)}, u32[]{:S(2)}, u32[]{:S(2)}) %collective-permute-start.7) | collective-permute-done | bytes 491552 | tf_op jit(solution)/shard_map/ppermute | solution.py:131
  49.4 1.0 maximum_select_fusion.g_ref
  50.4 58.6 %shard_map.68 = (f32[640,640]{1,0:T(8,128)}, f32[8,640]{1,0:T(8,128)}) custom-call(f32[1920,128]{1,0:T(8,128)} %maximum_select_fusion.g_ref), custom_call_target="tpu_custom_call" | custom-call | tf_op jit(solution)/shard_map/pallas_call | solution.py:107
  109.1 1.5 %slice_bitcast_fusion = f32[576,576]{0,1:T(8,128)S(1)} fusion(f32[640,640]{1,0:T(8,128)} %get-tuple-element.4), kind=kLoop, calls=%fused_computation | loop fusion | bytes 2654208 | tf_op jit(solution)/shard_map/transpose | solution.py:180
  110.5 0.0 copy-start
  110.6 0.0 copy-start.1
  110.6 1.6 %copy.7 = f32[576,576]{1,0:T(8,128)} copy(f32[576,576]{0,1:T(8,128)S(1)} %slice_bitcast_fusion) | data formatting | bytes 2654208
  112.2 0.0 copy-done
  112.2 0.0 copy-done.1
  112.2 0.7 fusion.6
  112.9 0.6 subtract_multiply_fusion.1
  (20 shorter events, 0.3 us)
Async XLA Ops:
  9.2 2.0 %collective-permute-start = (f32[960,128]{1,0:T(8,128)S(1)}, f32[960,128]{1,0:T(8,128)S(1)}, u32[]{:S(2)}, u32[]{:S(2)}) collective-permute-start(f32[960,128]{1,0:T(8,128)S(1)} %slice_select_fusion), channel_id=1, source_target_pairs={{0,1},{1,0},{2,3},{3,2},{4,5},{5,4},{6,7},{7,6},{8,9},{9,8},{10,11... | collective-permute-start | bytes 1474568 | tf_op jit(solution)/shard_map/ppermute | solution.py:128
  11.4 9.2 %collective-permute-start.1 = (f32[480,128]{1,0:T(8,128)S(1)}, f32[480,128]{1,0:T(8,128)S(1)}, u32[]{:S(2)}, u32[]{:S(2)}) collective-permute-start(f32[480,128]{1,0:T(8,128)S(1)} %slice_select_fusion.1), channel_id=1, source_target_pairs={{0,2},{1,3},{2,0},{3,1},{4,6},{5,7},{6,4},{7,5},{8,10},{9,11},{10,... | collective-permute-start | bytes 737288 | tf_op jit(solution)/shard_map/ppermute | solution.py:128
  20.6 4.9 %collective-permute-start.2 = (f32[240,128]{1,0:T(8,128)S(1)}, f32[240,128]{1,0:T(8,128)S(1)}, u32[]{:S(2)}, u32[]{:S(2)}) collective-permute-start(f32[240,128]{1,0:T(8,128)S(1)} %slice_select_fusion.2), channel_id=1, source_target_pairs={{0,4},{1,5},{2,6},{3,7},{4,0},{5,1},{6,2},{7,3},{8,12},{9,13},{10,... | collective-permute-start | bytes 368648 | tf_op jit(solution)/shard_map/ppermute | solution.py:128
  25.6 5.2 %collective-permute-start.3 = (f32[120,128]{1,0:T(8,128)S(1)}, f32[120,128]{1,0:T(8,128)S(1)}, u32[]{:S(2)}, u32[]{:S(2)}) collective-permute-start(f32[120,128]{1,0:T(8,128)S(1)} %slice_select_fusion.3), channel_id=1, source_target_pairs={{0,8},{1,9},{2,10},{3,11},{4,12},{5,13},{6,14},{7,15},{8,0},{9,1},... | collective-permute-start | bytes 184328 | tf_op jit(solution)/shard_map/ppermute | solution.py:128
  30.8 5.4 %collective-permute-start.4 = (f32[120,128]{1,0:T(8,128)S(1)}, f32[120,128]{1,0:T(8,128)S(1)}, u32[]{:S(2)}, u32[]{:S(2)}) collective-permute-start(f32[120,128]{1,0:T(8,128)S(1)} %select_add_fusion.3), channel_id=1, source_target_pairs={{0,8},{1,9},{2,10},{3,11},{4,12},{5,13},{6,14},{7,15},{8,0},{9,1},... | collective-permute-start | bytes 184328 | tf_op jit(solution)/shard_map/ppermute | solution.py:131
  36.1 5.0 %collective-permute-start.5 = (f32[240,128]{1,0:T(8,128)S(1)}, f32[240,128]{1,0:T(8,128)S(1)}, u32[]{:S(2)}, u32[]{:S(2)}) collective-permute-start(f32[240,128]{1,0:T(8,128)S(1)} %maximum_select_fusion.3), channel_id=1, source_target_pairs={{0,4},{1,5},{2,6},{3,7},{4,0},{5,1},{6,2},{7,3},{8,12},{9,13},{10,... | collective-permute-start | bytes 368648 | tf_op jit(solution)/shard_map/ppermute | solution.py:131
  41.2 6.3 %collective-permute-start.6 = (f32[480,128]{1,0:T(8,128)S(1)}, f32[480,128]{1,0:T(8,128)S(1)}, u32[]{:S(2)}, u32[]{:S(2)}) collective-permute-start(f32[480,128]{1,0:T(8,128)S(1)} %maximum_select_fusion.2), channel_id=1, source_target_pairs={{0,2},{1,3},{2,0},{3,1},{4,6},{5,7},{6,4},{7,5},{8,10},{9,11},{10,... | collective-permute-start | bytes 737288 | tf_op jit(solution)/shard_map/ppermute | solution.py:131
  47.5 1.9 %collective-permute-start.7 = (f32[960,128]{1,0:T(8,128)S(1)}, f32[960,128]{1,0:T(8,128)S(1)}, u32[]{:S(2)}, u32[]{:S(2)}) collective-permute-start(f32[960,128]{1,0:T(8,128)S(1)} %maximum_select_fusion.1), channel_id=1, source_target_pairs={{0,1},{1,0},{2,3},{3,2},{4,5},{5,4},{6,7},{7,6},{8,9},{9,8},{10,11... | collective-permute-start | bytes 1474568 | tf_op jit(solution)/shard_map/ppermute | solution.py:131
  110.5 1.6 %copy-start = (bf16[576,512]{1,0:T(8,128)(2,1)S(1)}, bf16[576,512]{1,0:T(8,128)(2,1)}, u32[]{:S(2)}) copy-start(bf16[576,512]{1,0:T(8,128)(2,1)} %param.5) | copy-start | bytes 1769476
  110.6 1.6 %copy-start.1 = (f32[8,640]{1,0:T(8,128)S(1)}, f32[8,640]{1,0:T(8,128)}, u32[]{:S(2)}) copy-start(f32[8,640]{1,0:T(8,128)} %get-tuple-element.5) | copy-start | bytes 61444

commit v4 on v3

--- a/solution.py
+++ b/solution.py
@@ -58,8 +58,9 @@
             def step(j, c, top=top, lane_t=lane_t, sub_t=sub_t, sub_col_t=sub_col_t):
                 d = d_ref[top:, :]
                 ahead = jnp.sum(jnp.where(lane_t == j + 1, d, 0.0), axis=1, keepdims=True)
-                piv = jnp.sum(jnp.where(sub_col_t == j, c, 0.0), axis=0, keepdims=True)
-                nxt = jnp.sum(jnp.where(sub_col_t == j + 1, c, 0.0), axis=0, keepdims=True)
+                lead = min(16, b - top)
+                piv = jnp.sum(jnp.where(sub_col_t[:lead] == j, c[:lead], 0.0), axis=0, keepdims=True)
+                nxt = jnp.sum(jnp.where(sub_col_t[:lead] == j + 1, c[:lead], 0.0), axis=0, keepdims=True)
                 inv = lax.rsqrt(piv)
                 live = jnp.where(sub_col_t >= j, c, 0.0)
                 lcol = live * inv

time: 114 us -> 114 us (level)
  no operation moved by 1% of the time
where the time goes in v4:
time: 114 us
  Pallas kernels  58.8 us (52%)
  waiting for transfers between devices  24.8 us (22%)
  starting transfers between devices  15.1 us (13%)
  matrix products  5.56 us (5%)
  local copies, waits for them, and re-layouts  4.03 us (4%)
  other arithmetic  3.86 us (3%)
  between operations  1.48 us (1%)
    pallas_call x1, Pallas kernels, cholesky_and_solve(): pl.pallas_call(kernel, out_shape=(jax.ShapeDtypeStruct((n, n), jnp.float3...  58.8 us
    ppermute x4, waiting for transfers between devices, butterfly_sum(): current = keep + lax.ppermute(send, axis, pairs)  13.1 us
    ppermute x4, waiting for transfers between devices, butterfly_sum(): got = lax.ppermute(current, axis, pairs)  11.7 us
    ppermute x4, starting transfers between devices, butterfly_sum(): current = keep + lax.ppermute(send, axis, pairs)  8.26 us
    ppermute x4, starting transfers between devices, butterfly_sum(): got = lax.ppermute(current, axis, pairs)  6.85 us
    dot_general x1, matrix products, shards(): lax.dot_general(working, working, (((1,), (1,)), ((), ())), precision=pre...  3.44 us
  transfers between devices with their start and end apart: 8, of which 8 were waited for; matrix products, arithmetic and copies ran while one was open for 0% of the time, Pallas kernels for 0%

profile of v4, /device:TPU:0, one launch (start us, length us, event | category | flops | bytes accessed | tf_op | source)
XLA Modules:
  0.0 113.7 jit_solution(5818892785312638226)
XLA Ops:
  1.3 0.8 dynamic_slice.3
  2.1 1.4 %fusion.13 = f32[1,512]{1,0:T(1,128)S(1)} fusion(f32[576,1]{0,1:T(1,128)S(1)} %reshape.7, bf16[576,512]{1,0:T(8,128)(2,1)} %param.5), kind=kOutput, calls=%fused_computation.46 | convolution fusion | flops 3538944 | bytes 594176 | tf_op jit(solution)/shard_map/dot_general | solution.py:148
  3.5 0.7 fusion.11
  4.2 1.2 %convert_multiply_fusion = f32[576,512]{1,0:T(8,128)S(1)} fusion(bf16[576,512]{1,0:T(8,128)(2,1)} %param.5, f32[512]{0:T(512)S(1)} %get-tuple-element.20), kind=kLoop, calls=%fused_computation.6 | loop fusion | flops 589824 | bytes 1771520 | tf_op jit(solution)/shard_map/mul | solution.py:153
  5.4 0.1 pad.18.clone
  5.5 3.4 %fusion = f32[640,640]{1,0:T(8,128)S(1)} fusion(f32[1,512]{1,0:T(1,128)S(1)} %bitcast.11, f32[576,512]{1,0:T(8,128)S(1)} %convert_multiply_fusion, f32[640]{0:T(1024)S(1)} %pad.18.clone), kind=kOutput, calls=%fused_computation.1 | convolution fusion | flops 2517237760 | bytes 2822656 | tf_op jit(solution)/shard_map/dot_general | solution.py:162
  9.1 0.1 slice_select_fusion
  9.2 0.6 collective-permute-start
  9.8 1.5 %collective-permute-done = f32[960,128]{1,0:T(8,128)S(1)} collective-permute-done((f32[960,128]{1,0:T(8,128)S(1)}, f32[960,128]{1,0:T(8,128)S(1)}, u32[]{:S(2)}, u32[]{:S(2)}) %collective-permute-start) | collective-permute-done | bytes 491552 | tf_op jit(solution)/shard_map/ppermute | solution.py:129
  11.2 0.1 select_add_fusion
  11.4 2.9 %collective-permute-start.1 = (f32[480,128]{1,0:T(8,128)S(1)}, f32[480,128]{1,0:T(8,128)S(1)}, u32[]{:S(2)}, u32[]{:S(2)}) collective-permute-start(f32[480,128]{1,0:T(8,128)S(1)} %slice_select_fusion.1), channel_id=1, source_target_pairs={{0,2},{1,3},{2,0},{3,1},{4,6},{5,7},{6,4},{7,5},{8,10},{9,11},{10,... | collective-permute-start | bytes 737288 | tf_op jit(solution)/shard_map/ppermute | solution.py:129
  14.3 6.3 %collective-permute-done.1 = f32[480,128]{1,0:T(8,128)S(1)} collective-permute-done((f32[480,128]{1,0:T(8,128)S(1)}, f32[480,128]{1,0:T(8,128)S(1)}, u32[]{:S(2)}, u32[]{:S(2)}) %collective-permute-start.1) | collective-permute-done | bytes 245792 | tf_op jit(solution)/shard_map/ppermute | solution.py:129
  20.6 1.9 %collective-permute-start.2 = (f32[240,128]{1,0:T(8,128)S(1)}, f32[240,128]{1,0:T(8,128)S(1)}, u32[]{:S(2)}, u32[]{:S(2)}) collective-permute-start(f32[240,128]{1,0:T(8,128)S(1)} %slice_select_fusion.2), channel_id=1, source_target_pairs={{0,4},{1,5},{2,6},{3,7},{4,0},{5,1},{6,2},{7,3},{8,12},{9,13},{10,... | collective-permute-start | bytes 368648 | tf_op jit(solution)/shard_map/ppermute | solution.py:129
  22.5 3.1 %collective-permute-done.2 = f32[240,128]{1,0:T(8,128)S(1)} collective-permute-done((f32[240,128]{1,0:T(8,128)S(1)}, f32[240,128]{1,0:T(8,128)S(1)}, u32[]{:S(2)}, u32[]{:S(2)}) %collective-permute-start.2) | collective-permute-done | bytes 122912 | tf_op jit(solution)/shard_map/ppermute | solution.py:129
  25.6 2.9 %collective-permute-start.3 = (f32[120,128]{1,0:T(8,128)S(1)}, f32[120,128]{1,0:T(8,128)S(1)}, u32[]{:S(2)}, u32[]{:S(2)}) collective-permute-start(f32[120,128]{1,0:T(8,128)S(1)} %slice_select_fusion.3), channel_id=1, source_target_pairs={{0,8},{1,9},{2,10},{3,11},{4,12},{5,13},{6,14},{7,15},{8,0},{9,1},... | collective-permute-start | bytes 184328 | tf_op jit(solution)/shard_map/ppermute | solution.py:129
  28.5 2.3 %collective-permute-done.3 = f32[120,128]{1,0:T(8,128)S(1)} collective-permute-done((f32[120,128]{1,0:T(8,128)S(1)}, f32[120,128]{1,0:T(8,128)S(1)}, u32[]{:S(2)}, u32[]{:S(2)}) %collective-permute-start.3) | collective-permute-done | bytes 61472 | tf_op jit(solution)/shard_map/ppermute | solution.py:129
  30.8 3.0 %collective-permute-start.4 = (f32[120,128]{1,0:T(8,128)S(1)}, f32[120,128]{1,0:T(8,128)S(1)}, u32[]{:S(2)}, u32[]{:S(2)}) collective-permute-start(f32[120,128]{1,0:T(8,128)S(1)} %select_add_fusion.3), channel_id=1, source_target_pairs={{0,8},{1,9},{2,10},{3,11},{4,12},{5,13},{6,14},{7,15},{8,0},{9,1},... | collective-permute-start | bytes 184328 | tf_op jit(solution)/shard_map/ppermute | solution.py:132
  33.7 2.4 %collective-permute-done.4 = f32[120,128]{1,0:T(8,128)S(1)} collective-permute-done((f32[120,128]{1,0:T(8,128)S(1)}, f32[120,128]{1,0:T(8,128)S(1)}, u32[]{:S(2)}, u32[]{:S(2)}) %collective-permute-start.4) | collective-permute-done | bytes 61472 | tf_op jit(solution)/shard_map/ppermute | solution.py:132
  36.1 2.2 %collective-permute-start.5 = (f32[240,128]{1,0:T(8,128)S(1)}, f32[240,128]{1,0:T(8,128)S(1)}, u32[]{:S(2)}, u32[]{:S(2)}) collective-permute-start(f32[240,128]{1,0:T(8,128)S(1)} %maximum_select_fusion.3), channel_id=1, source_target_pairs={{0,4},{1,5},{2,6},{3,7},{4,0},{5,1},{6,2},{7,3},{8,12},{9,13},{10,... | collective-permute-start | bytes 368648 | tf_op jit(solution)/shard_map/ppermute | solution.py:132
  38.3 2.9 %collective-permute-done.5 = f32[240,128]{1,0:T(8,128)S(1)} collective-permute-done((f32[240,128]{1,0:T(8,128)S(1)}, f32[240,128]{1,0:T(8,128)S(1)}, u32[]{:S(2)}, u32[]{:S(2)}) %collective-permute-start.5) | collective-permute-done | bytes 122912 | tf_op jit(solution)/shard_map/ppermute | solution.py:132
  41.2 1.7 %collective-permute-start.6 = (f32[480,128]{1,0:T(8,128)S(1)}, f32[480,128]{1,0:T(8,128)S(1)}, u32[]{:S(2)}, u32[]{:S(2)}) collective-permute-start(f32[480,128]{1,0:T(8,128)S(1)} %maximum_select_fusion.2), channel_id=1, source_target_pairs={{0,2},{1,3},{2,0},{3,1},{4,6},{5,7},{6,4},{7,5},{8,10},{9,11},{10,... | collective-permute-start | bytes 737288 | tf_op jit(solution)/shard_map/ppermute | solution.py:132
  42.8 4.6 %collective-permute-done.6 = f32[480,128]{1,0:T(8,128)S(1)} collective-permute-done((f32[480,128]{1,0:T(8,128)S(1)}, f32[480,128]{1,0:T(8,128)S(1)}, u32[]{:S(2)}, u32[]{:S(2)}) %collective-permute-start.6) | collective-permute-done | bytes 245792 | tf_op jit(solution)/shard_map/ppermute | solution.py:132
  47.5 0.1 collective-permute-start.7
  47.6 1.9 %collective-permute-done.7 = f32[960,128]{1,0:T(8,128)S(1)} collective-permute-done((f32[960,128]{1,0:T(8,128)S(1)}, f32[960,128]{1,0:T(8,128)S(1)}, u32[]{:S(2)}, u32[]{:S(2)}) %collective-permute-start.7) | collective-permute-done | bytes 491552 | tf_op jit(solution)/shard_map/ppermute | solution.py:132
  49.4 1.0 maximum_select_fusion.g_ref
  50.4 58.8 %shard_map.68 = (f32[640,640]{1,0:T(8,128)}, f32[8,640]{1,0:T(8,128)}) custom-call(f32[1920,128]{1,0:T(8,128)} %maximum_select_fusion.g_ref), custom_call_target="tpu_custom_call" | custom-call | tf_op jit(solution)/shard_map/pallas_call | solution.py:108
  109.3 1.5 %slice_bitcast_fusion = f32[576,576]{0,1:T(8,128)S(1)} fusion(f32[640,640]{1,0:T(8,128)} %get-tuple-element.4), kind=kLoop, calls=%fused_computation | loop fusion | bytes 2654208 | tf_op jit(solution)/shard_map/transpose | solution.py:181
  110.7 0.0 copy-start
  110.8 0.0 copy-start.1
  110.8 1.6 %copy.7 = f32[576,576]{1,0:T(8,128)} copy(f32[576,576]{0,1:T(8,128)S(1)} %slice_bitcast_fusion) | data formatting | bytes 2654208
  112.4 0.0 copy-done
  112.4 0.0 copy-done.1
  112.4 0.7 fusion.6
  113.1 0.6 subtract_multiply_fusion.1
  (20 shorter events, 0.3 us)
Async XLA Ops:
  9.2 2.0 %collective-permute-start = (f32[960,128]{1,0:T(8,128)S(1)}, f32[960,128]{1,0:T(8,128)S(1)}, u32[]{:S(2)}, u32[]{:S(2)}) collective-permute-start(f32[960,128]{1,0:T(8,128)S(1)} %slice_select_fusion), channel_id=1, source_target_pairs={{0,1},{1,0},{2,3},{3,2},{4,5},{5,4},{6,7},{7,6},{8,9},{9,8},{10,11... | collective-permute-start | bytes 1474568 | tf_op jit(solution)/shard_map/ppermute | solution.py:129
  11.4 9.2 %collective-permute-start.1 = (f32[480,128]{1,0:T(8,128)S(1)}, f32[480,128]{1,0:T(8,128)S(1)}, u32[]{:S(2)}, u32[]{:S(2)}) collective-permute-start(f32[480,128]{1,0:T(8,128)S(1)} %slice_select_fusion.1), channel_id=1, source_target_pairs={{0,2},{1,3},{2,0},{3,1},{4,6},{5,7},{6,4},{7,5},{8,10},{9,11},{10,... | collective-permute-start | bytes 737288 | tf_op jit(solution)/shard_map/ppermute | solution.py:129
  20.6 4.9 %collective-permute-start.2 = (f32[240,128]{1,0:T(8,128)S(1)}, f32[240,128]{1,0:T(8,128)S(1)}, u32[]{:S(2)}, u32[]{:S(2)}) collective-permute-start(f32[240,128]{1,0:T(8,128)S(1)} %slice_select_fusion.2), channel_id=1, source_target_pairs={{0,4},{1,5},{2,6},{3,7},{4,0},{5,1},{6,2},{7,3},{8,12},{9,13},{10,... | collective-permute-start | bytes 368648 | tf_op jit(solution)/shard_map/ppermute | solution.py:129
  25.6 5.2 %collective-permute-start.3 = (f32[120,128]{1,0:T(8,128)S(1)}, f32[120,128]{1,0:T(8,128)S(1)}, u32[]{:S(2)}, u32[]{:S(2)}) collective-permute-start(f32[120,128]{1,0:T(8,128)S(1)} %slice_select_fusion.3), channel_id=1, source_target_pairs={{0,8},{1,9},{2,10},{3,11},{4,12},{5,13},{6,14},{7,15},{8,0},{9,1},... | collective-permute-start | bytes 184328 | tf_op jit(solution)/shard_map/ppermute | solution.py:129
  30.8 5.4 %collective-permute-start.4 = (f32[120,128]{1,0:T(8,128)S(1)}, f32[120,128]{1,0:T(8,128)S(1)}, u32[]{:S(2)}, u32[]{:S(2)}) collective-permute-start(f32[120,128]{1,0:T(8,128)S(1)} %select_add_fusion.3), channel_id=1, source_target_pairs={{0,8},{1,9},{2,10},{3,11},{4,12},{5,13},{6,14},{7,15},{8,0},{9,1},... | collective-permute-start | bytes 184328 | tf_op jit(solution)/shard_map/ppermute | solution.py:132
  36.1 5.0 %collective-permute-start.5 = (f32[240,128]{1,0:T(8,128)S(1)}, f32[240,128]{1,0:T(8,128)S(1)}, u32[]{:S(2)}, u32[]{:S(2)}) collective-permute-start(f32[240,128]{1,0:T(8,128)S(1)} %maximum_select_fusion.3), channel_id=1, source_target_pairs={{0,4},{1,5},{2,6},{3,7},{4,0},{5,1},{6,2},{7,3},{8,12},{9,13},{10,... | collective-permute-start | bytes 368648 | tf_op jit(solution)/shard_map/ppermute | solution.py:132
  41.2 6.3 %collective-permute-start.6 = (f32[480,128]{1,0:T(8,128)S(1)}, f32[480,128]{1,0:T(8,128)S(1)}, u32[]{:S(2)}, u32[]{:S(2)}) collective-permute-start(f32[480,128]{1,0:T(8,128)S(1)} %maximum_select_fusion.2), channel_id=1, source_target_pairs={{0,2},{1,3},{2,0},{3,1},{4,6},{5,7},{6,4},{7,5},{8,10},{9,11},{10,... | collective-permute-start | bytes 737288 | tf_op jit(solution)/shard_map/ppermute | solution.py:132
  47.5 1.9 %collective-permute-start.7 = (f32[960,128]{1,0:T(8,128)S(1)}, f32[960,128]{1,0:T(8,128)S(1)}, u32[]{:S(2)}, u32[]{:S(2)}) collective-permute-start(f32[960,128]{1,0:T(8,128)S(1)} %maximum_select_fusion.1), channel_id=1, source_target_pairs={{0,1},{1,0},{2,3},{3,2},{4,5},{5,4},{6,7},{7,6},{8,9},{9,8},{10,11... | collective-permute-start | bytes 1474568 | tf_op jit(solution)/shard_map/ppermute | solution.py:132
  110.7 1.6 %copy-start = (bf16[576,512]{1,0:T(8,128)(2,1)S(1)}, bf16[576,512]{1,0:T(8,128)(2,1)}, u32[]{:S(2)}) copy-start(bf16[576,512]{1,0:T(8,128)(2,1)} %param.5) | copy-start | bytes 1769476
  110.8 1.6 %copy-start.1 = (f32[8,640]{1,0:T(8,128)S(1)}, f32[8,640]{1,0:T(8,128)}, u32[]{:S(2)}) copy-start(f32[8,640]{1,0:T(8,128)} %get-tuple-element.5) | copy-start | bytes 61444

commit v5 on v4

--- a/solution.py
+++ b/solution.py
@@ -72,7 +72,7 @@
                 m_ref[top:, :] = jnp.where(sub_t == j, mrow, m_ref[top:, :] - below * mrow)
                 return ahead - live * (nxt / piv)
 
-            column = lax.fori_loop(top, min(top + 8, steps), step, column)
+            column = lax.fori_loop(top, min(top + 8, steps), step, column, unroll=True)
             column = column[8:]
         inverse = m_ref[...]
         inverses.append(inverse)

time: 114 us -> 93.6 us (0.82)
  Pallas kernels: 58.8 us -> 38.4 us
    pallas_call x1, Pallas kernels: 58.8 us -> 38.4 us  [cholesky_and_solve(): pl.pallas_call(kernel, out_shape=(jax.ShapeDtypeStruct((n, n), jnp.float3...]
where the time goes in v5:
time: 93.6 us; the launch traced here: 93.2 us
  Pallas kernels  38.4 us (41%)
  waiting for transfers between devices  24.8 us (26%)
  starting transfers between devices  15.1 us (16%)
  matrix products  5.56 us (6%)
  local copies, waits for them, and re-layouts  4.03 us (4%)
  other arithmetic  3.86 us (4%)
  between operations  1.48 us (2%)
    pallas_call x1, Pallas kernels, cholesky_and_solve(): pl.pallas_call(kernel, out_shape=(jax.ShapeDtypeStruct((n, n), jnp.float3...  38.4 us
    ppermute x4, waiting for transfers between devices, butterfly_sum(): current = keep + lax.ppermute(send, axis, pairs)  13.1 us
    ppermute x4, waiting for transfers between devices, butterfly_sum(): got = lax.ppermute(current, axis, pairs)  11.7 us
    ppermute x4, starting transfers between devices, butterfly_sum(): current = keep + lax.ppermute(send, axis, pairs)  8.26 us
    ppermute x4, starting transfers between devices, butterfly_sum(): got = lax.ppermute(current, axis, pairs)  6.85 us
    dot_general x1, matrix products, shards(): lax.dot_general(working, working, (((1,), (1,)), ((), ())), precision=pre...  3.44 us
    mul x2, other arithmetic, shards(): scaled = as_float * (root_weight * norm_scale)[None, :]  1.95 us
  transfers between devices with their start and end apart: 8, of which 8 were waited for; matrix products, arithmetic and copies ran while one was open for 0% of the time, Pallas kernels for 0%

profile of v5, /device:TPU:0, one launch (start us, length us, event | category | flops | bytes accessed | tf_op | source)
XLA Modules:
  0.0 93.2 jit_solution(119012156033416998)
XLA Ops:
  1.3 0.8 dynamic_slice.3
  2.1 1.4 %fusion.13 = f32[1,512]{1,0:T(1,128)S(1)} fusion(f32[576,1]{0,1:T(1,128)S(1)} %reshape.7, bf16[576,512]{1,0:T(8,128)(2,1)} %param.5), kind=kOutput, calls=%fused_computation.46 | convolution fusion | flops 3538944 | bytes 594176 | tf_op jit(solution)/shard_map/dot_general | solution.py:148
  3.5 0.7 fusion.11
  4.2 1.2 %convert_multiply_fusion = f32[576,512]{1,0:T(8,128)S(1)} fusion(bf16[576,512]{1,0:T(8,128)(2,1)} %param.5, f32[512]{0:T(512)S(1)} %get-tuple-element.20), kind=kLoop, calls=%fused_computation.6 | loop fusion | flops 589824 | bytes 1771520 | tf_op jit(solution)/shard_map/mul | solution.py:153
  5.4 0.1 pad.18.clone
  5.5 3.4 %fusion = f32[640,640]{1,0:T(8,128)S(1)} fusion(f32[1,512]{1,0:T(1,128)S(1)} %bitcast.11, f32[576,512]{1,0:T(8,128)S(1)} %convert_multiply_fusion, f32[640]{0:T(1024)S(1)} %pad.18.clone), kind=kOutput, calls=%fused_computation.1 | convolution fusion | flops 2517237760 | bytes 2822656 | tf_op jit(solution)/shard_map/dot_general | solution.py:162
  9.1 0.1 slice_select_fusion
  9.2 0.6 collective-permute-start
  9.8 1.5 %collective-permute-done = f32[960,128]{1,0:T(8,128)S(1)} collective-permute-done((f32[960,128]{1,0:T(8,128)S(1)}, f32[960,128]{1,0:T(8,128)S(1)}, u32[]{:S(2)}, u32[]{:S(2)}) %collective-permute-start) | collective-permute-done | bytes 491552 | tf_op jit(solution)/shard_map/ppermute | solution.py:129
  11.2 0.1 select_add_fusion
  11.4 2.9 %collective-permute-start.1 = (f32[480,128]{1,0:T(8,128)S(1)}, f32[480,128]{1,0:T(8,128)S(1)}, u32[]{:S(2)}, u32[]{:S(2)}) collective-permute-start(f32[480,128]{1,0:T(8,128)S(1)} %slice_select_fusion.1), channel_id=1, source_target_pairs={{0,2},{1,3},{2,0},{3,1},{4,6},{5,7},{6,4},{7,5},{8,10},{9,11},{10,... | collective-permute-start | bytes 737288 | tf_op jit(solution)/shard_map/ppermute | solution.py:129
  14.3 6.3 %collective-permute-done.1 = f32[480,128]{1,0:T(8,128)S(1)} collective-permute-done((f32[480,128]{1,0:T(8,128)S(1)}, f32[480,128]{1,0:T(8,128)S(1)}, u32[]{:S(2)}, u32[]{:S(2)}) %collective-permute-start.1) | collective-permute-done | bytes 245792 | tf_op jit(solution)/shard_map/ppermute | solution.py:129
  20.6 1.9 %collective-permute-start.2 = (f32[240,128]{1,0:T(8,128)S(1)}, f32[240,128]{1,0:T(8,128)S(1)}, u32[]{:S(2)}, u32[]{:S(2)}) collective-permute-start(f32[240,128]{1,0:T(8,128)S(1)} %slice_select_fusion.2), channel_id=1, source_target_pairs={{0,4},{1,5},{2,6},{3,7},{4,0},{5,1},{6,2},{7,3},{8,12},{9,13},{10,... | collective-permute-start | bytes 368648 | tf_op jit(solution)/shard_map/ppermute | solution.py:129
  22.5 3.1 %collective-permute-done.2 = f32[240,128]{1,0:T(8,128)S(1)} collective-permute-done((f32[240,128]{1,0:T(8,128)S(1)}, f32[240,128]{1,0:T(8,128)S(1)}, u32[]{:S(2)}, u32[]{:S(2)}) %collective-permute-start.2) | collective-permute-done | bytes 122912 | tf_op jit(solution)/shard_map/ppermute | solution.py:129
  25.6 2.9 %collective-permute-start.3 = (f32[120,128]{1,0:T(8,128)S(1)}, f32[120,128]{1,0:T(8,128)S(1)}, u32[]{:S(2)}, u32[]{:S(2)}) collective-permute-start(f32[120,128]{1,0:T(8,128)S(1)} %slice_select_fusion.3), channel_id=1, source_target_pairs={{0,8},{1,9},{2,10},{3,11},{4,12},{5,13},{6,14},{7,15},{8,0},{9,1},... | collective-permute-start | bytes 184328 | tf_op jit(solution)/shard_map/ppermute | solution.py:129
  28.5 2.3 %collective-permute-done.3 = f32[120,128]{1,0:T(8,128)S(1)} collective-permute-done((f32[120,128]{1,0:T(8,128)S(1)}, f32[120,128]{1,0:T(8,128)S(1)}, u32[]{:S(2)}, u32[]{:S(2)}) %collective-permute-start.3) | collective-permute-done | bytes 61472 | tf_op jit(solution)/shard_map/ppermute | solution.py:129
  30.8 3.0 %collective-permute-start.4 = (f32[120,128]{1,0:T(8,128)S(1)}, f32[120,128]{1,0:T(8,128)S(1)}, u32[]{:S(2)}, u32[]{:S(2)}) collective-permute-start(f32[120,128]{1,0:T(8,128)S(1)} %select_add_fusion.3), channel_id=1, source_target_pairs={{0,8},{1,9},{2,10},{3,11},{4,12},{5,13},{6,14},{7,15},{8,0},{9,1},... | collective-permute-start | bytes 184328 | tf_op jit(solution)/shard_map/ppermute | solution.py:132
  33.7 2.4 %collective-permute-done.4 = f32[120,128]{1,0:T(8,128)S(1)} collective-permute-done((f32[120,128]{1,0:T(8,128)S(1)}, f32[120,128]{1,0:T(8,128)S(1)}, u32[]{:S(2)}, u32[]{:S(2)}) %collective-permute-start.4) | collective-permute-done | bytes 61472 | tf_op jit(solution)/shard_map/ppermute | solution.py:132
  36.1 2.2 %collective-permute-start.5 = (f32[240,128]{1,0:T(8,128)S(1)}, f32[240,128]{1,0:T(8,128)S(1)}, u32[]{:S(2)}, u32[]{:S(2)}) collective-permute-start(f32[240,128]{1,0:T(8,128)S(1)} %maximum_select_fusion.3), channel_id=1, source_target_pairs={{0,4},{1,5},{2,6},{3,7},{4,0},{5,1},{6,2},{7,3},{8,12},{9,13},{10,... | collective-permute-start | bytes 368648 | tf_op jit(solution)/shard_map/ppermute | solution.py:132
  38.3 2.9 %collective-permute-done.5 = f32[240,128]{1,0:T(8,128)S(1)} collective-permute-done((f32[240,128]{1,0:T(8,128)S(1)}, f32[240,128]{1,0:T(8,128)S(1)}, u32[]{:S(2)}, u32[]{:S(2)}) %collective-permute-start.5) | collective-permute-done | bytes 122912 | tf_op jit(solution)/shard_map/ppermute | solution.py:132
  41.2 1.7 %collective-permute-start.6 = (f32[480,128]{1,0:T(8,128)S(1)}, f32[480,128]{1,0:T(8,128)S(1)}, u32[]{:S(2)}, u32[]{:S(2)}) collective-permute-start(f32[480,128]{1,0:T(8,128)S(1)} %maximum_select_fusion.2), channel_id=1, source_target_pairs={{0,2},{1,3},{2,0},{3,1},{4,6},{5,7},{6,4},{7,5},{8,10},{9,11},{10,... | collective-permute-start | bytes 737288 | tf_op jit(solution)/shard_map/ppermute | solution.py:132
  42.8 4.6 %collective-permute-done.6 = f32[480,128]{1,0:T(8,128)S(1)} collective-permute-done((f32[480,128]{1,0:T(8,128)S(1)}, f32[480,128]{1,0:T(8,128)S(1)}, u32[]{:S(2)}, u32[]{:S(2)}) %collective-permute-start.6) | collective-permute-done | bytes 245792 | tf_op jit(solution)/shard_map/ppermute | solution.py:132
  47.5 0.1 collective-permute-start.7
  47.6 1.9 %collective-permute-done.7 = f32[960,128]{1,0:T(8,128)S(1)} collective-permute-done((f32[960,128]{1,0:T(8,128)S(1)}, f32[960,128]{1,0:T(8,128)S(1)}, u32[]{:S(2)}, u32[]{:S(2)}) %collective-permute-start.7) | collective-permute-done | bytes 491552 | tf_op jit(solution)/shard_map/ppermute | solution.py:132
  49.4 1.0 %maximum_select_fusion.g_ref = f32[1920,128]{1,0:T(8,128)} fusion(f32[960,128]{1,0:T(8,128)S(1)} %maximum_select_fusion.1, f32[960,128]{1,0:T(8,128)S(1)} %collective-permute-done.7, pred[]{:T(512)S(6)} %eq.16), kind=kLoop, calls=%fused_computation.7 | loop fusion | flops 737280 | bytes 1966081 | tf_op jit(solution)/shard_map/jit(_where)/select_n | solution.py:134
  50.4 38.4 %shard_map.68 = (f32[640,640]{1,0:T(8,128)}, f32[8,640]{1,0:T(8,128)}) custom-call(f32[1920,128]{1,0:T(8,128)} %maximum_select_fusion.g_ref), custom_call_target="tpu_custom_call" | custom-call | tf_op jit(solution)/shard_map/pallas_call | solution.py:108
  88.8 1.5 %slice_bitcast_fusion = f32[576,576]{0,1:T(8,128)S(1)} fusion(f32[640,640]{1,0:T(8,128)} %get-tuple-element.4), kind=kLoop, calls=%fused_computation | loop fusion | bytes 2654208 | tf_op jit(solution)/shard_map/transpose | solution.py:181
  90.3 0.0 copy-start
  90.3 0.0 copy-start.1
  90.3 1.6 %copy.7 = f32[576,576]{1,0:T(8,128)} copy(f32[576,576]{0,1:T(8,128)S(1)} %slice_bitcast_fusion) | data formatting | bytes 2654208
  91.9 0.0 copy-done
  91.9 0.0 copy-done.1
  91.9 0.7 fusion.6
  92.6 0.6 subtract_multiply_fusion.1
  (20 shorter events, 0.3 us)
Async XLA Ops:
  9.2 2.0 %collective-permute-start = (f32[960,128]{1,0:T(8,128)S(1)}, f32[960,128]{1,0:T(8,128)S(1)}, u32[]{:S(2)}, u32[]{:S(2)}) collective-permute-start(f32[960,128]{1,0:T(8,128)S(1)} %slice_select_fusion), channel_id=1, source_target_pairs={{0,1},{1,0},{2,3},{3,2},{4,5},{5,4},{6,7},{7,6},{8,9},{9,8},{10,11... | collective-permute-start | bytes 1474568 | tf_op jit(solution)/shard_map/ppermute | solution.py:129
  11.4 9.2 %collective-permute-start.1 = (f32[480,128]{1,0:T(8,128)S(1)}, f32[480,128]{1,0:T(8,128)S(1)}, u32[]{:S(2)}, u32[]{:S(2)}) collective-permute-start(f32[480,128]{1,0:T(8,128)S(1)} %slice_select_fusion.1), channel_id=1, source_target_pairs={{0,2},{1,3},{2,0},{3,1},{4,6},{5,7},{6,4},{7,5},{8,10},{9,11},{10,... | collective-permute-start | bytes 737288 | tf_op jit(solution)/shard_map/ppermute | solution.py:129
  20.6 4.9 %collective-permute-start.2 = (f32[240,128]{1,0:T(8,128)S(1)}, f32[240,128]{1,0:T(8,128)S(1)}, u32[]{:S(2)}, u32[]{:S(2)}) collective-permute-start(f32[240,128]{1,0:T(8,128)S(1)} %slice_select_fusion.2), channel_id=1, source_target_pairs={{0,4},{1,5},{2,6},{3,7},{4,0},{5,1},{6,2},{7,3},{8,12},{9,13},{10,... | collective-permute-start | bytes 368648 | tf_op jit(solution)/shard_map/ppermute | solution.py:129
  25.6 5.2 %collective-permute-start.3 = (f32[120,128]{1,0:T(8,128)S(1)}, f32[120,128]{1,0:T(8,128)S(1)}, u32[]{:S(2)}, u32[]{:S(2)}) collective-permute-start(f32[120,128]{1,0:T(8,128)S(1)} %slice_select_fusion.3), channel_id=1, source_target_pairs={{0,8},{1,9},{2,10},{3,11},{4,12},{5,13},{6,14},{7,15},{8,0},{9,1},... | collective-permute-start | bytes 184328 | tf_op jit(solution)/shard_map/ppermute | solution.py:129
  30.8 5.4 %collective-permute-start.4 = (f32[120,128]{1,0:T(8,128)S(1)}, f32[120,128]{1,0:T(8,128)S(1)}, u32[]{:S(2)}, u32[]{:S(2)}) collective-permute-start(f32[120,128]{1,0:T(8,128)S(1)} %select_add_fusion.3), channel_id=1, source_target_pairs={{0,8},{1,9},{2,10},{3,11},{4,12},{5,13},{6,14},{7,15},{8,0},{9,1},... | collective-permute-start | bytes 184328 | tf_op jit(solution)/shard_map/ppermute | solution.py:132
  36.1 5.0 %collective-permute-start.5 = (f32[240,128]{1,0:T(8,128)S(1)}, f32[240,128]{1,0:T(8,128)S(1)}, u32[]{:S(2)}, u32[]{:S(2)}) collective-permute-start(f32[240,128]{1,0:T(8,128)S(1)} %maximum_select_fusion.3), channel_id=1, source_target_pairs={{0,4},{1,5},{2,6},{3,7},{4,0},{5,1},{6,2},{7,3},{8,12},{9,13},{10,... | collective-permute-start | bytes 368648 | tf_op jit(solution)/shard_map/ppermute | solution.py:132
  41.2 6.3 %collective-permute-start.6 = (f32[480,128]{1,0:T(8,128)S(1)}, f32[480,128]{1,0:T(8,128)S(1)}, u32[]{:S(2)}, u32[]{:S(2)}) collective-permute-start(f32[480,128]{1,0:T(8,128)S(1)} %maximum_select_fusion.2), channel_id=1, source_target_pairs={{0,2},{1,3},{2,0},{3,1},{4,6},{5,7},{6,4},{7,5},{8,10},{9,11},{10,... | collective-permute-start | bytes 737288 | tf_op jit(solution)/shard_map/ppermute | solution.py:132
  47.5 1.9 %collective-permute-start.7 = (f32[960,128]{1,0:T(8,128)S(1)}, f32[960,128]{1,0:T(8,128)S(1)}, u32[]{:S(2)}, u32[]{:S(2)}) collective-permute-start(f32[960,128]{1,0:T(8,128)S(1)} %maximum_select_fusion.1), channel_id=1, source_target_pairs={{0,1},{1,0},{2,3},{3,2},{4,5},{5,4},{6,7},{7,6},{8,9},{9,8},{10,11... | collective-permute-start | bytes 1474568 | tf_op jit(solution)/shard_map/ppermute | solution.py:132
  90.3 1.6 %copy-start = (bf16[576,512]{1,0:T(8,128)(2,1)S(1)}, bf16[576,512]{1,0:T(8,128)(2,1)}, u32[]{:S(2)}) copy-start(bf16[576,512]{1,0:T(8,128)(2,1)} %param.5) | copy-start | bytes 1769476
  90.3 1.6 %copy-start.1 = (f32[8,640]{1,0:T(8,128)S(1)}, f32[8,640]{1,0:T(8,128)}, u32[]{:S(2)}) copy-start(f32[8,640]{1,0:T(8,128)} %get-tuple-element.5) | copy-start | bytes 61444

commit v6 on v5

--- a/solution.py
+++ b/solution.py
@@ -114,12 +114,12 @@
     )(sym)
 
 
-def butterfly_sum(flat, axis):
+def butterfly_sum(flat, axis, order):
     size = lax.axis_size(axis)
     steps = size.bit_length() - 1
     me = lax.axis_index(axis)
     current = flat
-    for bit in range(steps):
+    for bit in order:
         half = current.shape[0] // 2
         low, high = current[:half], current[half:]
         upper_half = ((me >> bit) & 1) == 1
@@ -127,7 +127,7 @@
         keep = jnp.where(upper_half, high, low)
         pairs = [(i, i ^ (1 << bit)) for i in range(size)]
         current = keep + lax.ppermute(send, axis, pairs)
-    for bit in reversed(range(steps)):
+    for bit in reversed(order):
         pairs = [(i, i ^ (1 << bit)) for i in range(size)]
         got = lax.ppermute(current, axis, pairs)
         upper_half = ((me >> bit) & 1) == 1
@@ -172,7 +172,14 @@
     padded = -(-used // quantum) * quantum
     if padded > used:
         pieces.append(jnp.zeros((padded - used, BLOCK), jnp.float32))
-    packed = butterfly_sum(jnp.concatenate(pieces, axis=0), "row")
+    stacked = jnp.concatenate(pieces, axis=0)
+    steps = row_devices.bit_length() - 1
+    first = list(range(steps))
+    second = [0, 2, 1] + first[3:] if steps >= 3 else first
+    half = padded // 2
+    packed = jnp.concatenate(
+        [butterfly_sum(stacked[:half], "row", first), butterfly_sum(stacked[half:], "row", second)], axis=0
+    )
     lower, solved = cholesky_and_solve(packed, window, blocks)
     lower_window = lower[:window, :window]
     coef = solved[0, :window]

time: 93.6 us -> 89.7 us (0.958)
  waiting for transfers between devices: 24.8 us -> 11.4 us
  starting transfers between devices: 15.1 us -> 24.3 us
    ppermute x4 -> x8, waiting for transfers between devices: 13.1 us -> 4.2 us  [butterfly_sum(): current = keep + lax.ppermute(send, axis, pairs)]
    ppermute x4 -> x8, starting transfers between devices: 8.26 us -> 13.2 us  [butterfly_sum(): current = keep + lax.ppermute(send, axis, pairs)]
    ppermute x4 -> x8, waiting for transfers between devices: 11.7 us -> 7.18 us  [butterfly_sum(): got = lax.ppermute(current, axis, pairs)]
    ppermute x4 -> x8, starting transfers between devices: 6.85 us -> 11.1 us  [butterfly_sum(): got = lax.ppermute(current, axis, pairs)]
    concatenate x0 -> x1, other arithmetic: none -> 1.01 us  [shards(): jnp.concatenate([butterfly_sum(stacked[:half], 'row', first), butterfly_s...]
  transfers between devices with their start and end apart: 8 -> 16, of which waited for: 8 -> 11; matrix products, arithmetic and copies ran while one was open for 0% -> 0% of each run, Pallas kernels for 0% -> 0%
where the time goes in v6:
time: 89.7 us; the launch traced here: 89.3 us
  Pallas kernels  38.4 us (43%)
  starting transfers between devices  24.3 us (27%)
  waiting for transfers between devices  11.4 us (13%)
  matrix products  5.63 us (6%)
  local copies, waits for them, and re-layouts  4.05 us (5%)
  other arithmetic  3.99 us (4%)
  between operations  1.57 us (2%)
    pallas_call x1, Pallas kernels, cholesky_and_solve(): pl.pallas_call(kernel, out_shape=(jax.ShapeDtypeStruct((n, n), jnp.float3...  38.4 us
    ppermute x8, starting transfers between devices, butterfly_sum(): current = keep + lax.ppermute(send, axis, pairs)  13.2 us
    ppermute x8, starting transfers between devices, butterfly_sum(): got = lax.ppermute(current, axis, pairs)  11.1 us
    ppermute x8, waiting for transfers between devices, butterfly_sum(): got = lax.ppermute(current, axis, pairs)  7.18 us
    ppermute x8, waiting for transfers between devices, butterfly_sum(): current = keep + lax.ppermute(send, axis, pairs)  4.2 us
    dot_general x1, matrix products, shards(): lax.dot_general(working, working, (((1,), (1,)), ((), ())), precision=pre...  3.5 us
    mul x2, other arithmetic, shards(): scaled = as_float * (root_weight * norm_scale)[None, :]  1.95 us
  transfers between devices with their start and end apart: 16, of which 11 were waited for; matrix products, arithmetic and copies ran while one was open for 0% of the time, Pallas kernels for 0%

profile of v6, /device:TPU:0, one launch (start us, length us, event | category | flops | bytes accessed | tf_op | source)
XLA Modules:
  0.0 89.3 jit_solution(8908620985666464332)
XLA Ops:
  1.3 0.8 dynamic_slice.3
  2.1 1.4 %fusion.14 = f32[1,512]{1,0:T(1,128)S(1)} fusion(f32[576,1]{0,1:T(1,128)S(1)} %reshape.7, bf16[576,512]{1,0:T(8,128)(2,1)} %param.5), kind=kOutput, calls=%fused_computation.60 | convolution fusion | flops 3538944 | bytes 594176 | tf_op jit(solution)/shard_map/dot_general | solution.py:148
  3.5 0.7 fusion.11
  4.2 1.2 %convert_multiply_fusion = f32[576,512]{1,0:T(8,128)S(1)} fusion(bf16[576,512]{1,0:T(8,128)(2,1)} %param.5, f32[512]{0:T(512)S(1)} %get-tuple-element.16), kind=kLoop, calls=%fused_computation.6 | loop fusion | flops 589824 | bytes 1771520 | tf_op jit(solution)/shard_map/mul | solution.py:153
  5.4 0.1 pad.43.clone
  5.5 3.5 %fusion = f32[640,640]{1,0:T(8,128)S(1)} fusion(f32[1,512]{1,0:T(1,128)S(1)} %bitcast.11, f32[576,512]{1,0:T(8,128)S(1)} %convert_multiply_fusion, f32[640]{0:T(1024)S(1)} %pad.43.clone), kind=kOutput, calls=%fused_computation.1 | convolution fusion | flops 2517237760 | bytes 2822656 | tf_op jit(solution)/shard_map/dot_general | solution.py:162
  9.2 0.6 collective-permute-start
  9.8 0.1 collective-permute-start.8
  9.9 1.0 %collective-permute-done = f32[480,128]{1,0:T(8,128)S(1)} collective-permute-done((f32[480,128]{1,0:T(8,128)S(1)}, f32[480,128]{1,0:T(8,128)S(1)}, u32[]{:S(2)}, u32[]{:S(2)}) %collective-permute-start) | collective-permute-done | bytes 245792 | tf_op jit(solution)/shard_map/ppermute | solution.py:129
  11.0 2.9 %collective-permute-start.1 = (f32[240,128]{1,0:T(8,128)S(1)}, f32[240,128]{1,0:T(8,128)S(1)}, u32[]{:S(2)}, u32[]{:S(2)}) collective-permute-start(f32[240,128]{1,0:T(8,128)S(1)} %slice_select_fusion.3), channel_id=1, source_target_pairs={{0,2},{1,3},{2,0},{3,1},{4,6},{5,7},{6,4},{7,5},{8,10},{9,11},{10,... | collective-permute-start | bytes 368648 | tf_op jit(solution)/shard_map/ppermute | solution.py:129
  13.9 0.0 collective-permute-done.8
  14.0 1.6 %collective-permute-start.9 = (f32[240,128]{1,0:T(8,128)S(1)}, f32[240,128]{1,0:T(8,128)S(1)}, u32[]{:S(2)}, u32[]{:S(2)}) collective-permute-start(f32[240,128]{1,0:T(8,128)S(1)} %slice_select_fusion.2), channel_id=1, source_target_pairs={{0,4},{1,5},{2,6},{3,7},{4,0},{5,1},{6,2},{7,3},{8,12},{9,13},{10,... | collective-permute-start | bytes 368648 | tf_op jit(solution)/shard_map/ppermute | solution.py:129
  15.6 1.9 %collective-permute-done.1 = f32[240,128]{1,0:T(8,128)S(1)} collective-permute-done((f32[240,128]{1,0:T(8,128)S(1)}, f32[240,128]{1,0:T(8,128)S(1)}, u32[]{:S(2)}, u32[]{:S(2)}) %collective-permute-start.1) | collective-permute-done | bytes 122912 | tf_op jit(solution)/shard_map/ppermute | solution.py:129
  17.6 1.9 %collective-permute-start.2 = (f32[120,128]{1,0:T(8,128)S(1)}, f32[120,128]{1,0:T(8,128)S(1)}, u32[]{:S(2)}, u32[]{:S(2)}) collective-permute-start(f32[120,128]{1,0:T(8,128)S(1)} %slice_select_fusion.5), channel_id=1, source_target_pairs={{0,4},{1,5},{2,6},{3,7},{4,0},{5,1},{6,2},{7,3},{8,12},{9,13},{10,... | collective-permute-start | bytes 184328 | tf_op jit(solution)/shard_map/ppermute | solution.py:129
  19.5 0.0 collective-permute-done.9
  19.5 1.6 %collective-permute-start.10 = (f32[120,128]{1,0:T(8,128)S(1)}, f32[120,128]{1,0:T(8,128)S(1)}, u32[]{:S(2)}, u32[]{:S(2)}) collective-permute-start(f32[120,128]{1,0:T(8,128)S(1)} %slice_select_fusion.4), channel_id=1, source_target_pairs={{0,2},{1,3},{2,0},{3,1},{4,6},{5,7},{6,4},{7,5},{8,10},{9,11},{10,... | collective-permute-start | bytes 184328 | tf_op jit(solution)/shard_map/ppermute | solution.py:129
  21.1 0.8 collective-permute-done.2
  21.9 2.9 %collective-permute-start.3 = (f32[60,128]{1,0:T(8,128)S(1)}, f32[60,128]{1,0:T(8,128)S(1)}, u32[]{:S(2)}, u32[]{:S(2)}) collective-permute-start(f32[60,128]{1,0:T(8,128)S(1)} %slice_select_fusion.7), channel_id=1, source_target_pairs={{0,8},{1,9},{2,10},{3,11},{4,12},{5,13},{6,14},{7,15},{8,0},{9,1},... | collective-permute-start | bytes 92168 | tf_op jit(solution)/shard_map/ppermute | solution.py:129
  24.8 0.0 collective-permute-done.10
  24.8 1.6 %collective-permute-start.11 = (f32[60,128]{1,0:T(8,128)S(1)}, f32[60,128]{1,0:T(8,128)S(1)}, u32[]{:S(2)}, u32[]{:S(2)}) collective-permute-start(f32[60,128]{1,0:T(8,128)S(1)} %slice_select_fusion.6), channel_id=1, source_target_pairs={{0,8},{1,9},{2,10},{3,11},{4,12},{5,13},{6,14},{7,15},{8,0},{9,1},... | collective-permute-start | bytes 92168 | tf_op jit(solution)/shard_map/ppermute | solution.py:129
  26.5 0.5 collective-permute-done.3
  27.0 2.8 %collective-permute-start.4 = (f32[60,128]{1,0:T(8,128)S(1)}, f32[60,128]{1,0:T(8,128)S(1)}, u32[]{:S(2)}, u32[]{:S(2)}) collective-permute-start(f32[60,128]{1,0:T(8,128)S(1)} %select_add_fusion.7), channel_id=1, source_target_pairs={{0,8},{1,9},{2,10},{3,11},{4,12},{5,13},{6,14},{7,15},{8,0},{9,1},... | collective-permute-start | bytes 92168 | tf_op jit(solution)/shard_map/ppermute | solution.py:132
  29.7 0.0 collective-permute-done.11
  29.7 1.6 %collective-permute-start.12 = (f32[60,128]{1,0:T(8,128)S(1)}, f32[60,128]{1,0:T(8,128)S(1)}, u32[]{:S(2)}, u32[]{:S(2)}) collective-permute-start(f32[60,128]{1,0:T(8,128)S(1)} %select_add_fusion.6), channel_id=1, source_target_pairs={{0,8},{1,9},{2,10},{3,11},{4,12},{5,13},{6,14},{7,15},{8,0},{9,1},... | collective-permute-start | bytes 92168 | tf_op jit(solution)/shard_map/ppermute | solution.py:132
  31.4 0.6 collective-permute-done.4
  32.0 1.5 %collective-permute-start.5 = (f32[120,128]{1,0:T(8,128)S(1)}, f32[120,128]{1,0:T(8,128)S(1)}, u32[]{:S(2)}, u32[]{:S(2)}) collective-permute-start(f32[120,128]{1,0:T(8,128)S(1)} %maximum_select_fusion.6), channel_id=1, source_target_pairs={{0,4},{1,5},{2,6},{3,7},{4,0},{5,1},{6,2},{7,3},{8,12},{9,13},{10,... | collective-permute-start | bytes 184328 | tf_op jit(solution)/shard_map/ppermute | solution.py:132
  33.6 1.0 %collective-permute-done.12 = f32[60,128]{1,0:T(8,128)S(1)} collective-permute-done((f32[60,128]{1,0:T(8,128)S(1)}, f32[60,128]{1,0:T(8,128)S(1)}, u32[]{:S(2)}, u32[]{:S(2)}) %collective-permute-start.12) | collective-permute-done | bytes 30752 | tf_op jit(solution)/shard_map/ppermute | solution.py:132
  34.6 1.6 %collective-permute-start.13 = (f32[120,128]{1,0:T(8,128)S(1)}, f32[120,128]{1,0:T(8,128)S(1)}, u32[]{:S(2)}, u32[]{:S(2)}) collective-permute-start(f32[120,128]{1,0:T(8,128)S(1)} %maximum_select_fusion.7), channel_id=1, source_target_pairs={{0,2},{1,3},{2,0},{3,1},{4,6},{5,7},{6,4},{7,5},{8,10},{9,11},{10,... | collective-permute-start | bytes 184328 | tf_op jit(solution)/shard_map/ppermute | solution.py:132
  36.2 0.1 collective-permute-done.5
  36.3 1.6 %collective-permute-start.6 = (f32[240,128]{1,0:T(8,128)S(1)}, f32[240,128]{1,0:T(8,128)S(1)}, u32[]{:S(2)}, u32[]{:S(2)}) collective-permute-start(f32[240,128]{1,0:T(8,128)S(1)} %maximum_select_fusion.4), channel_id=1, source_target_pairs={{0,2},{1,3},{2,0},{3,1},{4,6},{5,7},{6,4},{7,5},{8,10},{9,11},{10,... | collective-permute-start | bytes 368648 | tf_op jit(solution)/shard_map/ppermute | solution.py:132
  38.0 0.9 %collective-permute-done.13 = f32[120,128]{1,0:T(8,128)S(1)} collective-permute-done((f32[120,128]{1,0:T(8,128)S(1)}, f32[120,128]{1,0:T(8,128)S(1)}, u32[]{:S(2)}, u32[]{:S(2)}) %collective-permute-start.13) | collective-permute-done | bytes 61472 | tf_op jit(solution)/shard_map/ppermute | solution.py:132
  38.9 1.9 %collective-permute-start.14 = (f32[240,128]{1,0:T(8,128)S(1)}, f32[240,128]{1,0:T(8,128)S(1)}, u32[]{:S(2)}, u32[]{:S(2)}) collective-permute-start(f32[240,128]{1,0:T(8,128)S(1)} %maximum_select_fusion.5), channel_id=1, source_target_pairs={{0,4},{1,5},{2,6},{3,7},{4,0},{5,1},{6,2},{7,3},{8,12},{9,13},{10,... | collective-permute-start | bytes 368648 | tf_op jit(solution)/shard_map/ppermute | solution.py:132
  40.8 0.5 collective-permute-done.6
  41.3 0.1 collective-permute-start.7
  41.4 2.5 %collective-permute-done.14 = f32[240,128]{1,0:T(8,128)S(1)} collective-permute-done((f32[240,128]{1,0:T(8,128)S(1)}, f32[240,128]{1,0:T(8,128)S(1)}, u32[]{:S(2)}, u32[]{:S(2)}) %collective-permute-start.14) | collective-permute-done | bytes 122912 | tf_op jit(solution)/shard_map/ppermute | solution.py:132
  43.9 0.1 collective-permute-start.15
  44.0 0.0 collective-permute-done.7
  44.0 1.4 %collective-permute-done.15 = f32[480,128]{1,0:T(8,128)S(1)} collective-permute-done((f32[480,128]{1,0:T(8,128)S(1)}, f32[480,128]{1,0:T(8,128)S(1)}, u32[]{:S(2)}, u32[]{:S(2)}) %collective-permute-start.15) | collective-permute-done | bytes 245792 | tf_op jit(solution)/shard_map/ppermute | solution.py:132
  45.5 1.0 %pad_maximum_fusion.g_ref = f32[1920,128]{1,0:T(8,128)} fusion(f32[960,128]{1,0:T(8,128)S(1)} %maximum_select_fusion.1, f32[960,128]{1,0:T(8,128)S(1)} %maximum_select_fusion), kind=kLoop, calls=%fused_computation.7 | loop fusion | flops 245760 | bytes 1966080 | tf_op jit(solution)/shard_map/concatenate | solution.py:180
  46.5 38.4 %shard_map.68 = (f32[640,640]{1,0:T(8,128)}, f32[8,640]{1,0:T(8,128)}) custom-call(f32[1920,128]{1,0:T(8,128)} %pad_maximum_fusion.g_ref), custom_call_target="tpu_custom_call" | custom-call | tf_op jit(solution)/shard_map/pallas_call | solution.py:108
  84.9 1.5 %slice_bitcast_fusion = f32[576,576]{0,1:T(8,128)S(1)} fusion(f32[640,640]{1,0:T(8,128)} %get-tuple-element.4), kind=kLoop, calls=%fused_computation | loop fusion | bytes 2654208 | tf_op jit(solution)/shard_map/transpose | solution.py:188
  86.4 0.0 copy-start
  86.4 0.0 copy-start.1
  86.4 1.6 %copy.7 = f32[576,576]{1,0:T(8,128)} copy(f32[576,576]{0,1:T(8,128)S(1)} %slice_bitcast_fusion) | data formatting | bytes 2654208
  88.0 0.0 copy-done
  88.0 0.0 copy-done.1
  88.0 0.7 fusion.6
  88.7 0.6 subtract_multiply_fusion.1
  (36 shorter events, 0.6 us)
Async XLA Ops:
  9.2 1.7 %collective-permute-start = (f32[480,128]{1,0:T(8,128)S(1)}, f32[480,128]{1,0:T(8,128)S(1)}, u32[]{:S(2)}, u32[]{:S(2)}) collective-permute-start(f32[480,128]{1,0:T(8,128)S(1)} %slice_select_fusion.1), channel_id=1, source_target_pairs={{0,1},{1,0},{2,3},{3,2},{4,5},{5,4},{6,7},{7,6},{8,9},{9,8},{10,11... | collective-permute-start | bytes 737288 | tf_op jit(solution)/shard_map/ppermute | solution.py:129
  9.8 4.1 %collective-permute-start.8 = (f32[480,128]{1,0:T(8,128)S(1)}, f32[480,128]{1,0:T(8,128)S(1)}, u32[]{:S(2)}, u32[]{:S(2)}) collective-permute-start(f32[480,128]{1,0:T(8,128)S(1)} %slice_select_fusion), channel_id=1, source_target_pairs={{0,1},{1,0},{2,3},{3,2},{4,5},{5,4},{6,7},{7,6},{8,9},{9,8},{10,11... | collective-permute-start | bytes 737288 | tf_op jit(solution)/shard_map/ppermute | solution.py:129
  11.0 6.5 %collective-permute-start.1 = (f32[240,128]{1,0:T(8,128)S(1)}, f32[240,128]{1,0:T(8,128)S(1)}, u32[]{:S(2)}, u32[]{:S(2)}) collective-permute-start(f32[240,128]{1,0:T(8,128)S(1)} %slice_select_fusion.3), channel_id=1, source_target_pairs={{0,2},{1,3},{2,0},{3,1},{4,6},{5,7},{6,4},{7,5},{8,10},{9,11},{10,... | collective-permute-start | bytes 368648 | tf_op jit(solution)/shard_map/ppermute | solution.py:129
  14.0 5.5 %collective-permute-start.9 = (f32[240,128]{1,0:T(8,128)S(1)}, f32[240,128]{1,0:T(8,128)S(1)}, u32[]{:S(2)}, u32[]{:S(2)}) collective-permute-start(f32[240,128]{1,0:T(8,128)S(1)} %slice_select_fusion.2), channel_id=1, source_target_pairs={{0,4},{1,5},{2,6},{3,7},{4,0},{5,1},{6,2},{7,3},{8,12},{9,13},{10,... | collective-permute-start | bytes 368648 | tf_op jit(solution)/shard_map/ppermute | solution.py:129
  17.6 4.3 %collective-permute-start.2 = (f32[120,128]{1,0:T(8,128)S(1)}, f32[120,128]{1,0:T(8,128)S(1)}, u32[]{:S(2)}, u32[]{:S(2)}) collective-permute-start(f32[120,128]{1,0:T(8,128)S(1)} %slice_select_fusion.5), channel_id=1, source_target_pairs={{0,4},{1,5},{2,6},{3,7},{4,0},{5,1},{6,2},{7,3},{8,12},{9,13},{10,... | collective-permute-start | bytes 184328 | tf_op jit(solution)/shard_map/ppermute | solution.py:129
  19.5 5.3 %collective-permute-start.10 = (f32[120,128]{1,0:T(8,128)S(1)}, f32[120,128]{1,0:T(8,128)S(1)}, u32[]{:S(2)}, u32[]{:S(2)}) collective-permute-start(f32[120,128]{1,0:T(8,128)S(1)} %slice_select_fusion.4), channel_id=1, source_target_pairs={{0,2},{1,3},{2,0},{3,1},{4,6},{5,7},{6,4},{7,5},{8,10},{9,11},{10,... | collective-permute-start | bytes 184328 | tf_op jit(solution)/shard_map/ppermute | solution.py:129
  21.9 5.0 %collective-permute-start.3 = (f32[60,128]{1,0:T(8,128)S(1)}, f32[60,128]{1,0:T(8,128)S(1)}, u32[]{:S(2)}, u32[]{:S(2)}) collective-permute-start(f32[60,128]{1,0:T(8,128)S(1)} %slice_select_fusion.7), channel_id=1, source_target_pairs={{0,8},{1,9},{2,10},{3,11},{4,12},{5,13},{6,14},{7,15},{8,0},{9,1},... | collective-permute-start | bytes 92168 | tf_op jit(solution)/shard_map/ppermute | solution.py:129
  24.8 4.9 %collective-permute-start.11 = (f32[60,128]{1,0:T(8,128)S(1)}, f32[60,128]{1,0:T(8,128)S(1)}, u32[]{:S(2)}, u32[]{:S(2)}) collective-permute-start(f32[60,128]{1,0:T(8,128)S(1)} %slice_select_fusion.6), channel_id=1, source_target_pairs={{0,8},{1,9},{2,10},{3,11},{4,12},{5,13},{6,14},{7,15},{8,0},{9,1},... | collective-permute-start | bytes 92168 | tf_op jit(solution)/shard_map/ppermute | solution.py:129
  27.0 5.1 %collective-permute-start.4 = (f32[60,128]{1,0:T(8,128)S(1)}, f32[60,128]{1,0:T(8,128)S(1)}, u32[]{:S(2)}, u32[]{:S(2)}) collective-permute-start(f32[60,128]{1,0:T(8,128)S(1)} %select_add_fusion.7), channel_id=1, source_target_pairs={{0,8},{1,9},{2,10},{3,11},{4,12},{5,13},{6,14},{7,15},{8,0},{9,1},... | collective-permute-start | bytes 92168 | tf_op jit(solution)/shard_map/ppermute | solution.py:132
  29.7 4.9 %collective-permute-start.12 = (f32[60,128]{1,0:T(8,128)S(1)}, f32[60,128]{1,0:T(8,128)S(1)}, u32[]{:S(2)}, u32[]{:S(2)}) collective-permute-start(f32[60,128]{1,0:T(8,128)S(1)} %select_add_fusion.6), channel_id=1, source_target_pairs={{0,8},{1,9},{2,10},{3,11},{4,12},{5,13},{6,14},{7,15},{8,0},{9,1},... | collective-permute-start | bytes 92168 | tf_op jit(solution)/shard_map/ppermute | solution.py:132
  32.0 4.3 %collective-permute-start.5 = (f32[120,128]{1,0:T(8,128)S(1)}, f32[120,128]{1,0:T(8,128)S(1)}, u32[]{:S(2)}, u32[]{:S(2)}) collective-permute-start(f32[120,128]{1,0:T(8,128)S(1)} %maximum_select_fusion.6), channel_id=1, source_target_pairs={{0,4},{1,5},{2,6},{3,7},{4,0},{5,1},{6,2},{7,3},{8,12},{9,13},{10,... | collective-permute-start | bytes 184328 | tf_op jit(solution)/shard_map/ppermute | solution.py:132
  34.6 4.3 %collective-permute-start.13 = (f32[120,128]{1,0:T(8,128)S(1)}, f32[120,128]{1,0:T(8,128)S(1)}, u32[]{:S(2)}, u32[]{:S(2)}) collective-permute-start(f32[120,128]{1,0:T(8,128)S(1)} %maximum_select_fusion.7), channel_id=1, source_target_pairs={{0,2},{1,3},{2,0},{3,1},{4,6},{5,7},{6,4},{7,5},{8,10},{9,11},{10,... | collective-permute-start | bytes 184328 | tf_op jit(solution)/shard_map/ppermute | solution.py:132
  36.3 4.9 %collective-permute-start.6 = (f32[240,128]{1,0:T(8,128)S(1)}, f32[240,128]{1,0:T(8,128)S(1)}, u32[]{:S(2)}, u32[]{:S(2)}) collective-permute-start(f32[240,128]{1,0:T(8,128)S(1)} %maximum_select_fusion.4), channel_id=1, source_target_pairs={{0,2},{1,3},{2,0},{3,1},{4,6},{5,7},{6,4},{7,5},{8,10},{9,11},{10,... | collective-permute-start | bytes 368648 | tf_op jit(solution)/shard_map/ppermute | solution.py:132
  38.9 4.9 %collective-permute-start.14 = (f32[240,128]{1,0:T(8,128)S(1)}, f32[240,128]{1,0:T(8,128)S(1)}, u32[]{:S(2)}, u32[]{:S(2)}) collective-permute-start(f32[240,128]{1,0:T(8,128)S(1)} %maximum_select_fusion.5), channel_id=1, source_target_pairs={{0,4},{1,5},{2,6},{3,7},{4,0},{5,1},{6,2},{7,3},{8,12},{9,13},{10,... | collective-permute-start | bytes 368648 | tf_op jit(solution)/shard_map/ppermute | solution.py:132
  41.3 2.7 %collective-permute-start.7 = (f32[480,128]{1,0:T(8,128)S(1)}, f32[480,128]{1,0:T(8,128)S(1)}, u32[]{:S(2)}, u32[]{:S(2)}) collective-permute-start(f32[480,128]{1,0:T(8,128)S(1)} %maximum_select_fusion.2), channel_id=1, source_target_pairs={{0,1},{1,0},{2,3},{3,2},{4,5},{5,4},{6,7},{7,6},{8,9},{9,8},{10,11... | collective-permute-start | bytes 737288 | tf_op jit(solution)/shard_map/ppermute | solution.py:132
  43.9 1.6 %collective-permute-start.15 = (f32[480,128]{1,0:T(8,128)S(1)}, f32[480,128]{1,0:T(8,128)S(1)}, u32[]{:S(2)}, u32[]{:S(2)}) collective-permute-start(f32[480,128]{1,0:T(8,128)S(1)} %maximum_select_fusion.3), channel_id=1, source_target_pairs={{0,1},{1,0},{2,3},{3,2},{4,5},{5,4},{6,7},{7,6},{8,9},{9,8},{10,11... | collective-permute-start | bytes 737288 | tf_op jit(solution)/shard_map/ppermute | solution.py:132
  86.4 1.6 %copy-start = (bf16[576,512]{1,0:T(8,128)(2,1)S(1)}, bf16[576,512]{1,0:T(8,128)(2,1)}, u32[]{:S(2)}) copy-start(bf16[576,512]{1,0:T(8,128)(2,1)} %param.5) | copy-start | bytes 1769476
  86.4 1.6 %copy-start.1 = (f32[8,640]{1,0:T(8,128)S(1)}, f32[8,640]{1,0:T(8,128)}, u32[]{:S(2)}) copy-start(f32[8,640]{1,0:T(8,128)} %get-tuple-element.5) | copy-start | bytes 61444

commit v7 on v6

--- a/solution.py
+++ b/solution.py
@@ -48,31 +48,26 @@
         k_ref[...] = jnp.zeros((b, b), jnp.float32)
 
         steps = b if k < blocks - 1 else last_steps
-        column = jnp.sum(jnp.where(lane == 0, d_ref[...], 0.0), axis=1, keepdims=True)
+        column = jnp.broadcast_to(d_ref[:, 0:1], (b, b))
         for tile in range(-(-steps // 8)):
             top = tile * 8
-            lane_t = lane[top:, :]
             sub_t = sub[top:, :]
-            sub_col_t = sub_col[top:, :]
-
-            def step(j, c, top=top, lane_t=lane_t, sub_t=sub_t, sub_col_t=sub_col_t):
+            for j in range(top, min(top + 8, steps)):
+                r = j - top
                 d = d_ref[top:, :]
-                ahead = jnp.sum(jnp.where(lane_t == j + 1, d, 0.0), axis=1, keepdims=True)
-                lead = min(16, b - top)
-                piv = jnp.sum(jnp.where(sub_col_t[:lead] == j, c[:lead], 0.0), axis=0, keepdims=True)
-                nxt = jnp.sum(jnp.where(sub_col_t[:lead] == j + 1, c[:lead], 0.0), axis=0, keepdims=True)
+                piv = column[r:r + 1, :]
                 inv = lax.rsqrt(piv)
-                live = jnp.where(sub_col_t >= j, c, 0.0)
+                live = jnp.where(sub_t >= j, column, 0.0)
                 lcol = live * inv
-                lrow = jnp.where(lane_row >= j, d_ref[pl.ds(j, 1), :] * inv, 0.0)
+                lrow = jnp.where(lane_row >= j, d[r:r + 1, :] * inv, 0.0)
                 d_ref[top:, :] = d - lcol * lrow
-                k_ref[pl.ds(j, 1), :] = lrow
-                mrow = m_ref[pl.ds(j, 1), :] * inv
-                below = jnp.where(sub_col_t > j, lcol, 0.0)
+                k_ref[j:j + 1, :] = lrow
+                mrow = m_ref[j:j + 1, :] * inv
+                below = jnp.where(sub_t > j, lcol, 0.0)
                 m_ref[top:, :] = jnp.where(sub_t == j, mrow, m_ref[top:, :] - below * mrow)
-                return ahead - live * (nxt / piv)
-
-            column = lax.fori_loop(top, min(top + 8, steps), step, column, unroll=True)
+                if j + 1 < steps:
+                    ahead = jnp.broadcast_to(d[:, j + 1:j + 2], d.shape)
+                    column = ahead - live * (column[r + 1:r + 2, :] / piv)
             column = column[8:]
         inverse = m_ref[...]
         inverses.append(inverse)

time: 89.7 us -> 84.5 us (0.942)
  Pallas kernels: 38.4 us -> 33.2 us
    pallas_call x1, Pallas kernels: 38.4 us -> 33.2 us  [cholesky_and_solve(): pl.pallas_call(kernel, out_shape=(jax.ShapeDtypeStruct((n, n), jnp.float3...]
where the time goes in v7:
time: 84.5 us; the launch traced here: 84.2 us
  Pallas kernels  33.2 us (39%)
  starting transfers between devices  24.3 us (29%)
  waiting for transfers between devices  11.4 us (13%)
  matrix products  5.63 us (7%)
  local copies, waits for them, and re-layouts  4.05 us (5%)
  other arithmetic  3.99 us (5%)
  between operations  1.57 us (2%)
    pallas_call x1, Pallas kernels, cholesky_and_solve(): pl.pallas_call(kernel, out_shape=(jax.ShapeDtypeStruct((n, n), jnp.float3...  33.2 us
    ppermute x8, starting transfers between devices, butterfly_sum(): current = keep + lax.ppermute(send, axis, pairs)  13.2 us
    ppermute x8, starting transfers between devices, butterfly_sum(): got = lax.ppermute(current, axis, pairs)  11.1 us
    ppermute x8, waiting for transfers between devices, butterfly_sum(): got = lax.ppermute(current, axis, pairs)  7.18 us
    ppermute x8, waiting for transfers between devices, butterfly_sum(): current = keep + lax.ppermute(send, axis, pairs)  4.2 us
    dot_general x1, matrix products, shards(): lax.dot_general(working, working, (((1,), (1,)), ((), ())), precision=pre...  3.5 us
    mul x2, other arithmetic, shards(): scaled = as_float * (root_weight * norm_scale)[None, :]  1.95 us
  transfers between devices with their start and end apart: 16, of which 11 were waited for; matrix products, arithmetic and copies ran while one was open for 0% of the time, Pallas kernels for 0%

profile of v7, /device:TPU:0, one launch (start us, length us, event | category | flops | bytes accessed | tf_op | source)
XLA Modules:
  0.0 84.2 jit_solution(12699231857734693806)
XLA Ops:
  1.3 0.8 dynamic_slice.3
  2.1 1.4 %fusion.14 = f32[1,512]{1,0:T(1,128)S(1)} fusion(f32[576,1]{0,1:T(1,128)S(1)} %reshape.7, bf16[576,512]{1,0:T(8,128)(2,1)} %param.5), kind=kOutput, calls=%fused_computation.60 | convolution fusion | flops 3538944 | bytes 594176 | tf_op jit(solution)/shard_map/dot_general | solution.py:143
  3.5 0.7 fusion.11
  4.2 1.2 %convert_multiply_fusion = f32[576,512]{1,0:T(8,128)S(1)} fusion(bf16[576,512]{1,0:T(8,128)(2,1)} %param.5, f32[512]{0:T(512)S(1)} %get-tuple-element.16), kind=kLoop, calls=%fused_computation.6 | loop fusion | flops 589824 | bytes 1771520 | tf_op jit(solution)/shard_map/mul | solution.py:148
  5.4 0.1 pad.43.clone
  5.5 3.5 %fusion = f32[640,640]{1,0:T(8,128)S(1)} fusion(f32[1,512]{1,0:T(1,128)S(1)} %bitcast.11, f32[576,512]{1,0:T(8,128)S(1)} %convert_multiply_fusion, f32[640]{0:T(1024)S(1)} %pad.43.clone), kind=kOutput, calls=%fused_computation.1 | convolution fusion | flops 2517237760 | bytes 2822656 | tf_op jit(solution)/shard_map/dot_general | solution.py:157
  9.2 0.6 collective-permute-start
  9.8 0.1 collective-permute-start.8
  9.9 1.0 %collective-permute-done = f32[480,128]{1,0:T(8,128)S(1)} collective-permute-done((f32[480,128]{1,0:T(8,128)S(1)}, f32[480,128]{1,0:T(8,128)S(1)}, u32[]{:S(2)}, u32[]{:S(2)}) %collective-permute-start) | collective-permute-done | bytes 245792 | tf_op jit(solution)/shard_map/ppermute | solution.py:124
  11.0 2.9 %collective-permute-start.1 = (f32[240,128]{1,0:T(8,128)S(1)}, f32[240,128]{1,0:T(8,128)S(1)}, u32[]{:S(2)}, u32[]{:S(2)}) collective-permute-start(f32[240,128]{1,0:T(8,128)S(1)} %slice_select_fusion.3), channel_id=1, source_target_pairs={{0,2},{1,3},{2,0},{3,1},{4,6},{5,7},{6,4},{7,5},{8,10},{9,11},{10,... | collective-permute-start | bytes 368648 | tf_op jit(solution)/shard_map/ppermute | solution.py:124
  13.9 0.0 collective-permute-done.8
  14.0 1.6 %collective-permute-start.9 = (f32[240,128]{1,0:T(8,128)S(1)}, f32[240,128]{1,0:T(8,128)S(1)}, u32[]{:S(2)}, u32[]{:S(2)}) collective-permute-start(f32[240,128]{1,0:T(8,128)S(1)} %slice_select_fusion.2), channel_id=1, source_target_pairs={{0,4},{1,5},{2,6},{3,7},{4,0},{5,1},{6,2},{7,3},{8,12},{9,13},{10,... | collective-permute-start | bytes 368648 | tf_op jit(solution)/shard_map/ppermute | solution.py:124
  15.6 1.9 %collective-permute-done.1 = f32[240,128]{1,0:T(8,128)S(1)} collective-permute-done((f32[240,128]{1,0:T(8,128)S(1)}, f32[240,128]{1,0:T(8,128)S(1)}, u32[]{:S(2)}, u32[]{:S(2)}) %collective-permute-start.1) | collective-permute-done | bytes 122912 | tf_op jit(solution)/shard_map/ppermute | solution.py:124
  17.6 1.9 %collective-permute-start.2 = (f32[120,128]{1,0:T(8,128)S(1)}, f32[120,128]{1,0:T(8,128)S(1)}, u32[]{:S(2)}, u32[]{:S(2)}) collective-permute-start(f32[120,128]{1,0:T(8,128)S(1)} %slice_select_fusion.5), channel_id=1, source_target_pairs={{0,4},{1,5},{2,6},{3,7},{4,0},{5,1},{6,2},{7,3},{8,12},{9,13},{10,... | collective-permute-start | bytes 184328 | tf_op jit(solution)/shard_map/ppermute | solution.py:124
  19.5 0.0 collective-permute-done.9
  19.5 1.6 %collective-permute-start.10 = (f32[120,128]{1,0:T(8,128)S(1)}, f32[120,128]{1,0:T(8,128)S(1)}, u32[]{:S(2)}, u32[]{:S(2)}) collective-permute-start(f32[120,128]{1,0:T(8,128)S(1)} %slice_select_fusion.4), channel_id=1, source_target_pairs={{0,2},{1,3},{2,0},{3,1},{4,6},{5,7},{6,4},{7,5},{8,10},{9,11},{10,... | collective-permute-start | bytes 184328 | tf_op jit(solution)/shard_map/ppermute | solution.py:124
  21.1 0.8 collective-permute-done.2
  21.9 2.9 %collective-permute-start.3 = (f32[60,128]{1,0:T(8,128)S(1)}, f32[60,128]{1,0:T(8,128)S(1)}, u32[]{:S(2)}, u32[]{:S(2)}) collective-permute-start(f32[60,128]{1,0:T(8,128)S(1)} %slice_select_fusion.7), channel_id=1, source_target_pairs={{0,8},{1,9},{2,10},{3,11},{4,12},{5,13},{6,14},{7,15},{8,0},{9,1},... | collective-permute-start | bytes 92168 | tf_op jit(solution)/shard_map/ppermute | solution.py:124
  24.8 0.0 collective-permute-done.10
  24.8 1.6 %collective-permute-start.11 = (f32[60,128]{1,0:T(8,128)S(1)}, f32[60,128]{1,0:T(8,128)S(1)}, u32[]{:S(2)}, u32[]{:S(2)}) collective-permute-start(f32[60,128]{1,0:T(8,128)S(1)} %slice_select_fusion.6), channel_id=1, source_target_pairs={{0,8},{1,9},{2,10},{3,11},{4,12},{5,13},{6,14},{7,15},{8,0},{9,1},... | collective-permute-start | bytes 92168 | tf_op jit(solution)/shard_map/ppermute | solution.py:124
  26.5 0.5 collective-permute-done.3
  27.0 2.8 %collective-permute-start.4 = (f32[60,128]{1,0:T(8,128)S(1)}, f32[60,128]{1,0:T(8,128)S(1)}, u32[]{:S(2)}, u32[]{:S(2)}) collective-permute-start(f32[60,128]{1,0:T(8,128)S(1)} %select_add_fusion.7), channel_id=1, source_target_pairs={{0,8},{1,9},{2,10},{3,11},{4,12},{5,13},{6,14},{7,15},{8,0},{9,1},... | collective-permute-start | bytes 92168 | tf_op jit(solution)/shard_map/ppermute | solution.py:127
  29.7 0.0 collective-permute-done.11
  29.7 1.6 %collective-permute-start.12 = (f32[60,128]{1,0:T(8,128)S(1)}, f32[60,128]{1,0:T(8,128)S(1)}, u32[]{:S(2)}, u32[]{:S(2)}) collective-permute-start(f32[60,128]{1,0:T(8,128)S(1)} %select_add_fusion.6), channel_id=1, source_target_pairs={{0,8},{1,9},{2,10},{3,11},{4,12},{5,13},{6,14},{7,15},{8,0},{9,1},... | collective-permute-start | bytes 92168 | tf_op jit(solution)/shard_map/ppermute | solution.py:127
  31.4 0.6 collective-permute-done.4
  32.0 1.5 %collective-permute-start.5 = (f32[120,128]{1,0:T(8,128)S(1)}, f32[120,128]{1,0:T(8,128)S(1)}, u32[]{:S(2)}, u32[]{:S(2)}) collective-permute-start(f32[120,128]{1,0:T(8,128)S(1)} %maximum_select_fusion.6), channel_id=1, source_target_pairs={{0,4},{1,5},{2,6},{3,7},{4,0},{5,1},{6,2},{7,3},{8,12},{9,13},{10,... | collective-permute-start | bytes 184328 | tf_op jit(solution)/shard_map/ppermute | solution.py:127
  33.6 1.0 %collective-permute-done.12 = f32[60,128]{1,0:T(8,128)S(1)} collective-permute-done((f32[60,128]{1,0:T(8,128)S(1)}, f32[60,128]{1,0:T(8,128)S(1)}, u32[]{:S(2)}, u32[]{:S(2)}) %collective-permute-start.12) | collective-permute-done | bytes 30752 | tf_op jit(solution)/shard_map/ppermute | solution.py:127
  34.6 1.6 %collective-permute-start.13 = (f32[120,128]{1,0:T(8,128)S(1)}, f32[120,128]{1,0:T(8,128)S(1)}, u32[]{:S(2)}, u32[]{:S(2)}) collective-permute-start(f32[120,128]{1,0:T(8,128)S(1)} %maximum_select_fusion.7), channel_id=1, source_target_pairs={{0,2},{1,3},{2,0},{3,1},{4,6},{5,7},{6,4},{7,5},{8,10},{9,11},{10,... | collective-permute-start | bytes 184328 | tf_op jit(solution)/shard_map/ppermute | solution.py:127
  36.2 0.1 collective-permute-done.5
  36.3 1.6 %collective-permute-start.6 = (f32[240,128]{1,0:T(8,128)S(1)}, f32[240,128]{1,0:T(8,128)S(1)}, u32[]{:S(2)}, u32[]{:S(2)}) collective-permute-start(f32[240,128]{1,0:T(8,128)S(1)} %maximum_select_fusion.4), channel_id=1, source_target_pairs={{0,2},{1,3},{2,0},{3,1},{4,6},{5,7},{6,4},{7,5},{8,10},{9,11},{10,... | collective-permute-start | bytes 368648 | tf_op jit(solution)/shard_map/ppermute | solution.py:127
  38.0 0.9 %collective-permute-done.13 = f32[120,128]{1,0:T(8,128)S(1)} collective-permute-done((f32[120,128]{1,0:T(8,128)S(1)}, f32[120,128]{1,0:T(8,128)S(1)}, u32[]{:S(2)}, u32[]{:S(2)}) %collective-permute-start.13) | collective-permute-done | bytes 61472 | tf_op jit(solution)/shard_map/ppermute | solution.py:127
  38.9 1.9 %collective-permute-start.14 = (f32[240,128]{1,0:T(8,128)S(1)}, f32[240,128]{1,0:T(8,128)S(1)}, u32[]{:S(2)}, u32[]{:S(2)}) collective-permute-start(f32[240,128]{1,0:T(8,128)S(1)} %maximum_select_fusion.5), channel_id=1, source_target_pairs={{0,4},{1,5},{2,6},{3,7},{4,0},{5,1},{6,2},{7,3},{8,12},{9,13},{10,... | collective-permute-start | bytes 368648 | tf_op jit(solution)/shard_map/ppermute | solution.py:127
  40.8 0.5 collective-permute-done.6
  41.3 0.1 collective-permute-start.7
  41.4 2.5 %collective-permute-done.14 = f32[240,128]{1,0:T(8,128)S(1)} collective-permute-done((f32[240,128]{1,0:T(8,128)S(1)}, f32[240,128]{1,0:T(8,128)S(1)}, u32[]{:S(2)}, u32[]{:S(2)}) %collective-permute-start.14) | collective-permute-done | bytes 122912 | tf_op jit(solution)/shard_map/ppermute | solution.py:127
  43.9 0.1 collective-permute-start.15
  44.0 0.0 collective-permute-done.7
  44.0 1.4 %collective-permute-done.15 = f32[480,128]{1,0:T(8,128)S(1)} collective-permute-done((f32[480,128]{1,0:T(8,128)S(1)}, f32[480,128]{1,0:T(8,128)S(1)}, u32[]{:S(2)}, u32[]{:S(2)}) %collective-permute-start.15) | collective-permute-done | bytes 245792 | tf_op jit(solution)/shard_map/ppermute | solution.py:127
  45.5 1.0 %pad_maximum_fusion.g_ref = f32[1920,128]{1,0:T(8,128)} fusion(f32[960,128]{1,0:T(8,128)S(1)} %maximum_select_fusion.1, f32[960,128]{1,0:T(8,128)S(1)} %maximum_select_fusion), kind=kLoop, calls=%fused_computation.7 | loop fusion | flops 245760 | bytes 1966080 | tf_op jit(solution)/shard_map/concatenate | solution.py:175
  46.5 33.2 %shard_map.68 = (f32[640,640]{1,0:T(8,128)}, f32[8,640]{1,0:T(8,128)}) custom-call(f32[1920,128]{1,0:T(8,128)} %pad_maximum_fusion.g_ref), custom_call_target="tpu_custom_call" | custom-call | tf_op jit(solution)/shard_map/pallas_call | solution.py:103
  79.7 1.5 %slice_bitcast_fusion = f32[576,576]{0,1:T(8,128)S(1)} fusion(f32[640,640]{1,0:T(8,128)} %get-tuple-element.4), kind=kLoop, calls=%fused_computation | loop fusion | bytes 2654208 | tf_op jit(solution)/shard_map/transpose | solution.py:183
  81.2 0.0 copy-start
  81.2 0.0 copy-start.1
  81.2 1.6 %copy.7 = f32[576,576]{1,0:T(8,128)} copy(f32[576,576]{0,1:T(8,128)S(1)} %slice_bitcast_fusion) | data formatting | bytes 2654208
  82.8 0.0 copy-done
  82.8 0.0 copy-done.1
  82.8 0.7 fusion.6
  83.6 0.6 subtract_multiply_fusion.1
  (36 shorter events, 0.6 us)
Async XLA Ops:
  9.2 1.7 %collective-permute-start = (f32[480,128]{1,0:T(8,128)S(1)}, f32[480,128]{1,0:T(8,128)S(1)}, u32[]{:S(2)}, u32[]{:S(2)}) collective-permute-start(f32[480,128]{1,0:T(8,128)S(1)} %slice_select_fusion.1), channel_id=1, source_target_pairs={{0,1},{1,0},{2,3},{3,2},{4,5},{5,4},{6,7},{7,6},{8,9},{9,8},{10,11... | collective-permute-start | bytes 737288 | tf_op jit(solution)/shard_map/ppermute | solution.py:124
  9.8 4.1 %collective-permute-start.8 = (f32[480,128]{1,0:T(8,128)S(1)}, f32[480,128]{1,0:T(8,128)S(1)}, u32[]{:S(2)}, u32[]{:S(2)}) collective-permute-start(f32[480,128]{1,0:T(8,128)S(1)} %slice_select_fusion), channel_id=1, source_target_pairs={{0,1},{1,0},{2,3},{3,2},{4,5},{5,4},{6,7},{7,6},{8,9},{9,8},{10,11... | collective-permute-start | bytes 737288 | tf_op jit(solution)/shard_map/ppermute | solution.py:124
  11.0 6.5 %collective-permute-start.1 = (f32[240,128]{1,0:T(8,128)S(1)}, f32[240,128]{1,0:T(8,128)S(1)}, u32[]{:S(2)}, u32[]{:S(2)}) collective-permute-start(f32[240,128]{1,0:T(8,128)S(1)} %slice_select_fusion.3), channel_id=1, source_target_pairs={{0,2},{1,3},{2,0},{3,1},{4,6},{5,7},{6,4},{7,5},{8,10},{9,11},{10,... | collective-permute-start | bytes 368648 | tf_op jit(solution)/shard_map/ppermute | solution.py:124
  14.0 5.5 %collective-permute-start.9 = (f32[240,128]{1,0:T(8,128)S(1)}, f32[240,128]{1,0:T(8,128)S(1)}, u32[]{:S(2)}, u32[]{:S(2)}) collective-permute-start(f32[240,128]{1,0:T(8,128)S(1)} %slice_select_fusion.2), channel_id=1, source_target_pairs={{0,4},{1,5},{2,6},{3,7},{4,0},{5,1},{6,2},{7,3},{8,12},{9,13},{10,... | collective-permute-start | bytes 368648 | tf_op jit(solution)/shard_map/ppermute | solution.py:124
  17.6 4.3 %collective-permute-start.2 = (f32[120,128]{1,0:T(8,128)S(1)}, f32[120,128]{1,0:T(8,128)S(1)}, u32[]{:S(2)}, u32[]{:S(2)}) collective-permute-start(f32[120,128]{1,0:T(8,128)S(1)} %slice_select_fusion.5), channel_id=1, source_target_pairs={{0,4},{1,5},{2,6},{3,7},{4,0},{5,1},{6,2},{7,3},{8,12},{9,13},{10,... | collective-permute-start | bytes 184328 | tf_op jit(solution)/shard_map/ppermute | solution.py:124
  19.5 5.3 %collective-permute-start.10 = (f32[120,128]{1,0:T(8,128)S(1)}, f32[120,128]{1,0:T(8,128)S(1)}, u32[]{:S(2)}, u32[]{:S(2)}) collective-permute-start(f32[120,128]{1,0:T(8,128)S(1)} %slice_select_fusion.4), channel_id=1, source_target_pairs={{0,2},{1,3},{2,0},{3,1},{4,6},{5,7},{6,4},{7,5},{8,10},{9,11},{10,... | collective-permute-start | bytes 184328 | tf_op jit(solution)/shard_map/ppermute | solution.py:124
  21.9 5.0 %collective-permute-start.3 = (f32[60,128]{1,0:T(8,128)S(1)}, f32[60,128]{1,0:T(8,128)S(1)}, u32[]{:S(2)}, u32[]{:S(2)}) collective-permute-start(f32[60,128]{1,0:T(8,128)S(1)} %slice_select_fusion.7), channel_id=1, source_target_pairs={{0,8},{1,9},{2,10},{3,11},{4,12},{5,13},{6,14},{7,15},{8,0},{9,1},... | collective-permute-start | bytes 92168 | tf_op jit(solution)/shard_map/ppermute | solution.py:124
  24.8 4.9 %collective-permute-start.11 = (f32[60,128]{1,0:T(8,128)S(1)}, f32[60,128]{1,0:T(8,128)S(1)}, u32[]{:S(2)}, u32[]{:S(2)}) collective-permute-start(f32[60,128]{1,0:T(8,128)S(1)} %slice_select_fusion.6), channel_id=1, source_target_pairs={{0,8},{1,9},{2,10},{3,11},{4,12},{5,13},{6,14},{7,15},{8,0},{9,1},... | collective-permute-start | bytes 92168 | tf_op jit(solution)/shard_map/ppermute | solution.py:124
  27.0 5.1 %collective-permute-start.4 = (f32[60,128]{1,0:T(8,128)S(1)}, f32[60,128]{1,0:T(8,128)S(1)}, u32[]{:S(2)}, u32[]{:S(2)}) collective-permute-start(f32[60,128]{1,0:T(8,128)S(1)} %select_add_fusion.7), channel_id=1, source_target_pairs={{0,8},{1,9},{2,10},{3,11},{4,12},{5,13},{6,14},{7,15},{8,0},{9,1},... | collective-permute-start | bytes 92168 | tf_op jit(solution)/shard_map/ppermute | solution.py:127
  29.7 4.9 %collective-permute-start.12 = (f32[60,128]{1,0:T(8,128)S(1)}, f32[60,128]{1,0:T(8,128)S(1)}, u32[]{:S(2)}, u32[]{:S(2)}) collective-permute-start(f32[60,128]{1,0:T(8,128)S(1)} %select_add_fusion.6), channel_id=1, source_target_pairs={{0,8},{1,9},{2,10},{3,11},{4,12},{5,13},{6,14},{7,15},{8,0},{9,1},... | collective-permute-start | bytes 92168 | tf_op jit(solution)/shard_map/ppermute | solution.py:127
  32.0 4.3 %collective-permute-start.5 = (f32[120,128]{1,0:T(8,128)S(1)}, f32[120,128]{1,0:T(8,128)S(1)}, u32[]{:S(2)}, u32[]{:S(2)}) collective-permute-start(f32[120,128]{1,0:T(8,128)S(1)} %maximum_select_fusion.6), channel_id=1, source_target_pairs={{0,4},{1,5},{2,6},{3,7},{4,0},{5,1},{6,2},{7,3},{8,12},{9,13},{10,... | collective-permute-start | bytes 184328 | tf_op jit(solution)/shard_map/ppermute | solution.py:127
  34.6 4.3 %collective-permute-start.13 = (f32[120,128]{1,0:T(8,128)S(1)}, f32[120,128]{1,0:T(8,128)S(1)}, u32[]{:S(2)}, u32[]{:S(2)}) collective-permute-start(f32[120,128]{1,0:T(8,128)S(1)} %maximum_select_fusion.7), channel_id=1, source_target_pairs={{0,2},{1,3},{2,0},{3,1},{4,6},{5,7},{6,4},{7,5},{8,10},{9,11},{10,... | collective-permute-start | bytes 184328 | tf_op jit(solution)/shard_map/ppermute | solution.py:127
  36.3 4.9 %collective-permute-start.6 = (f32[240,128]{1,0:T(8,128)S(1)}, f32[240,128]{1,0:T(8,128)S(1)}, u32[]{:S(2)}, u32[]{:S(2)}) collective-permute-start(f32[240,128]{1,0:T(8,128)S(1)} %maximum_select_fusion.4), channel_id=1, source_target_pairs={{0,2},{1,3},{2,0},{3,1},{4,6},{5,7},{6,4},{7,5},{8,10},{9,11},{10,... | collective-permute-start | bytes 368648 | tf_op jit(solution)/shard_map/ppermute | solution.py:127
  38.9 4.9 %collective-permute-start.14 = (f32[240,128]{1,0:T(8,128)S(1)}, f32[240,128]{1,0:T(8,128)S(1)}, u32[]{:S(2)}, u32[]{:S(2)}) collective-permute-start(f32[240,128]{1,0:T(8,128)S(1)} %maximum_select_fusion.5), channel_id=1, source_target_pairs={{0,4},{1,5},{2,6},{3,7},{4,0},{5,1},{6,2},{7,3},{8,12},{9,13},{10,... | collective-permute-start | bytes 368648 | tf_op jit(solution)/shard_map/ppermute | solution.py:127
  41.3 2.7 %collective-permute-start.7 = (f32[480,128]{1,0:T(8,128)S(1)}, f32[480,128]{1,0:T(8,128)S(1)}, u32[]{:S(2)}, u32[]{:S(2)}) collective-permute-start(f32[480,128]{1,0:T(8,128)S(1)} %maximum_select_fusion.2), channel_id=1, source_target_pairs={{0,1},{1,0},{2,3},{3,2},{4,5},{5,4},{6,7},{7,6},{8,9},{9,8},{10,11... | collective-permute-start | bytes 737288 | tf_op jit(solution)/shard_map/ppermute | solution.py:127
  43.9 1.6 %collective-permute-start.15 = (f32[480,128]{1,0:T(8,128)S(1)}, f32[480,128]{1,0:T(8,128)S(1)}, u32[]{:S(2)}, u32[]{:S(2)}) collective-permute-start(f32[480,128]{1,0:T(8,128)S(1)} %maximum_select_fusion.3), channel_id=1, source_target_pairs={{0,1},{1,0},{2,3},{3,2},{4,5},{5,4},{6,7},{7,6},{8,9},{9,8},{10,11... | collective-permute-start | bytes 737288 | tf_op jit(solution)/shard_map/ppermute | solution.py:127
  81.2 1.6 %copy-start = (bf16[576,512]{1,0:T(8,128)(2,1)S(1)}, bf16[576,512]{1,0:T(8,128)(2,1)}, u32[]{:S(2)}) copy-start(bf16[576,512]{1,0:T(8,128)(2,1)} %param.5) | copy-start | bytes 1769476
  81.2 1.6 %copy-start.1 = (f32[8,640]{1,0:T(8,128)S(1)}, f32[8,640]{1,0:T(8,128)}, u32[]{:S(2)}) copy-start(f32[8,640]{1,0:T(8,128)} %get-tuple-element.5) | copy-start | bytes 61444

commit v8 on v7

--- a/solution.py
+++ b/solution.py
@@ -75,7 +75,10 @@
         if k < blocks - 1:
             panel = nt(l_ref[r0 + b:, r0:r0 + b], inverse)
             l_ref[r0 + b:, r0:r0 + b] = panel
-            l_ref[r0 + b:, r0 + b:] = l_ref[r0 + b:, r0 + b:] - nt(panel, panel)
+            for i in range(k + 1, blocks):
+                part = panel[(i - k - 1) * b:(i - k) * b]
+                hi = (i + 1) * b
+                l_ref[i * b:hi, r0 + b:hi] = l_ref[i * b:hi, r0 + b:hi] - nt(part, panel[:(i - k) * b])
             l_ref[r0:r0 + b, r0 + b:] = jnp.zeros((b, l_ref.shape[1] - r0 - b), jnp.float32)
     last = blocks - 1
     tl = target - last * b

time: 84.5 us -> 83.5 us (0.988)
  Pallas kernels: 33.2 us -> 32.2 us
    pallas_call x1, Pallas kernels: 33.2 us -> 32.2 us  [cholesky_and_solve(): pl.pallas_call(kernel, out_shape=(jax.ShapeDtypeStruct((n, n), jnp.float3...]
where the time goes in v8:
time: 83.5 us; the launch traced here: 83.1 us
  Pallas kernels  32.2 us (39%)
  starting transfers between devices  24.3 us (29%)
  waiting for transfers between devices  11.4 us (14%)
  matrix products  5.62 us (7%)
  local copies, waits for them, and re-layouts  4.04 us (5%)
  other arithmetic  3.99 us (5%)
  between operations  1.57 us (2%)
    pallas_call x1, Pallas kernels, cholesky_and_solve(): pl.pallas_call(kernel, out_shape=(jax.ShapeDtypeStruct((n, n), jnp.float3...  32.2 us
    ppermute x8, starting transfers between devices, butterfly_sum(): current = keep + lax.ppermute(send, axis, pairs)  13.2 us
    ppermute x8, starting transfers between devices, butterfly_sum(): got = lax.ppermute(current, axis, pairs)  11.1 us
    ppermute x8, waiting for transfers between devices, butterfly_sum(): got = lax.ppermute(current, axis, pairs)  7.18 us
    ppermute x8, waiting for transfers between devices, butterfly_sum(): current = keep + lax.ppermute(send, axis, pairs)  4.2 us
    dot_general x1, matrix products, shards(): lax.dot_general(working, working, (((1,), (1,)), ((), ())), precision=pre...  3.5 us
    mul x2, other arithmetic, shards(): scaled = as_float * (root_weight * norm_scale)[None, :]  1.95 us
  transfers between devices with their start and end apart: 16, of which 11 were waited for; matrix products, arithmetic and copies ran while one was open for 0% of the time, Pallas kernels for 0%

profile of v8, /device:TPU:0, one launch (start us, length us, event | category | flops | bytes accessed | tf_op | source)
XLA Modules:
  0.0 83.1 jit_solution(2571356528147365144)
XLA Ops:
  1.3 0.8 dynamic_slice.3
  2.1 1.4 %fusion.14 = f32[1,512]{1,0:T(1,128)S(1)} fusion(f32[576,1]{0,1:T(1,128)S(1)} %reshape.7, bf16[576,512]{1,0:T(8,128)(2,1)} %param.5), kind=kOutput, calls=%fused_computation.60 | convolution fusion | flops 3538944 | bytes 594176 | tf_op jit(solution)/shard_map/dot_general | solution.py:146
  3.4 0.7 fusion.11
  4.2 1.2 %convert_multiply_fusion = f32[576,512]{1,0:T(8,128)S(1)} fusion(bf16[576,512]{1,0:T(8,128)(2,1)} %param.5, f32[512]{0:T(512)S(1)} %get-tuple-element.16), kind=kLoop, calls=%fused_computation.6 | loop fusion | flops 589824 | bytes 1771520 | tf_op jit(solution)/shard_map/mul | solution.py:151
  5.4 0.1 pad.43.clone
  5.5 3.5 %fusion = f32[640,640]{1,0:T(8,128)S(1)} fusion(f32[1,512]{1,0:T(1,128)S(1)} %bitcast.11, f32[576,512]{1,0:T(8,128)S(1)} %convert_multiply_fusion, f32[640]{0:T(1024)S(1)} %pad.43.clone), kind=kOutput, calls=%fused_computation.1 | convolution fusion | flops 2517237760 | bytes 2822656 | tf_op jit(solution)/shard_map/dot_general | solution.py:160
  9.2 0.6 collective-permute-start
  9.8 0.1 collective-permute-start.8
  9.9 1.0 %collective-permute-done = f32[480,128]{1,0:T(8,128)S(1)} collective-permute-done((f32[480,128]{1,0:T(8,128)S(1)}, f32[480,128]{1,0:T(8,128)S(1)}, u32[]{:S(2)}, u32[]{:S(2)}) %collective-permute-start) | collective-permute-done | bytes 245792 | tf_op jit(solution)/shard_map/ppermute | solution.py:127
  11.0 2.9 %collective-permute-start.1 = (f32[240,128]{1,0:T(8,128)S(1)}, f32[240,128]{1,0:T(8,128)S(1)}, u32[]{:S(2)}, u32[]{:S(2)}) collective-permute-start(f32[240,128]{1,0:T(8,128)S(1)} %slice_select_fusion.3), channel_id=1, source_target_pairs={{0,2},{1,3},{2,0},{3,1},{4,6},{5,7},{6,4},{7,5},{8,10},{9,11},{10,... | collective-permute-start | bytes 368648 | tf_op jit(solution)/shard_map/ppermute | solution.py:127
  13.9 0.0 collective-permute-done.8
  14.0 1.6 %collective-permute-start.9 = (f32[240,128]{1,0:T(8,128)S(1)}, f32[240,128]{1,0:T(8,128)S(1)}, u32[]{:S(2)}, u32[]{:S(2)}) collective-permute-start(f32[240,128]{1,0:T(8,128)S(1)} %slice_select_fusion.2), channel_id=1, source_target_pairs={{0,4},{1,5},{2,6},{3,7},{4,0},{5,1},{6,2},{7,3},{8,12},{9,13},{10,... | collective-permute-start | bytes 368648 | tf_op jit(solution)/shard_map/ppermute | solution.py:127
  15.6 1.9 %collective-permute-done.1 = f32[240,128]{1,0:T(8,128)S(1)} collective-permute-done((f32[240,128]{1,0:T(8,128)S(1)}, f32[240,128]{1,0:T(8,128)S(1)}, u32[]{:S(2)}, u32[]{:S(2)}) %collective-permute-start.1) | collective-permute-done | bytes 122912 | tf_op jit(solution)/shard_map/ppermute | solution.py:127
  17.6 1.9 %collective-permute-start.2 = (f32[120,128]{1,0:T(8,128)S(1)}, f32[120,128]{1,0:T(8,128)S(1)}, u32[]{:S(2)}, u32[]{:S(2)}) collective-permute-start(f32[120,128]{1,0:T(8,128)S(1)} %slice_select_fusion.5), channel_id=1, source_target_pairs={{0,4},{1,5},{2,6},{3,7},{4,0},{5,1},{6,2},{7,3},{8,12},{9,13},{10,... | collective-permute-start | bytes 184328 | tf_op jit(solution)/shard_map/ppermute | solution.py:127
  19.5 0.0 collective-permute-done.9
  19.5 1.6 %collective-permute-start.10 = (f32[120,128]{1,0:T(8,128)S(1)}, f32[120,128]{1,0:T(8,128)S(1)}, u32[]{:S(2)}, u32[]{:S(2)}) collective-permute-start(f32[120,128]{1,0:T(8,128)S(1)} %slice_select_fusion.4), channel_id=1, source_target_pairs={{0,2},{1,3},{2,0},{3,1},{4,6},{5,7},{6,4},{7,5},{8,10},{9,11},{10,... | collective-permute-start | bytes 184328 | tf_op jit(solution)/shard_map/ppermute | solution.py:127
  21.1 0.8 collective-permute-done.2
  21.9 2.9 %collective-permute-start.3 = (f32[60,128]{1,0:T(8,128)S(1)}, f32[60,128]{1,0:T(8,128)S(1)}, u32[]{:S(2)}, u32[]{:S(2)}) collective-permute-start(f32[60,128]{1,0:T(8,128)S(1)} %slice_select_fusion.7), channel_id=1, source_target_pairs={{0,8},{1,9},{2,10},{3,11},{4,12},{5,13},{6,14},{7,15},{8,0},{9,1},... | collective-permute-start | bytes 92168 | tf_op jit(solution)/shard_map/ppermute | solution.py:127
  24.8 0.0 collective-permute-done.10
  24.8 1.7 %collective-permute-start.11 = (f32[60,128]{1,0:T(8,128)S(1)}, f32[60,128]{1,0:T(8,128)S(1)}, u32[]{:S(2)}, u32[]{:S(2)}) collective-permute-start(f32[60,128]{1,0:T(8,128)S(1)} %slice_select_fusion.6), channel_id=1, source_target_pairs={{0,8},{1,9},{2,10},{3,11},{4,12},{5,13},{6,14},{7,15},{8,0},{9,1},... | collective-permute-start | bytes 92168 | tf_op jit(solution)/shard_map/ppermute | solution.py:127
  26.5 0.5 collective-permute-done.3
  27.0 2.8 %collective-permute-start.4 = (f32[60,128]{1,0:T(8,128)S(1)}, f32[60,128]{1,0:T(8,128)S(1)}, u32[]{:S(2)}, u32[]{:S(2)}) collective-permute-start(f32[60,128]{1,0:T(8,128)S(1)} %select_add_fusion.7), channel_id=1, source_target_pairs={{0,8},{1,9},{2,10},{3,11},{4,12},{5,13},{6,14},{7,15},{8,0},{9,1},... | collective-permute-start | bytes 92168 | tf_op jit(solution)/shard_map/ppermute | solution.py:130
  29.7 0.0 collective-permute-done.11
  29.7 1.6 %collective-permute-start.12 = (f32[60,128]{1,0:T(8,128)S(1)}, f32[60,128]{1,0:T(8,128)S(1)}, u32[]{:S(2)}, u32[]{:S(2)}) collective-permute-start(f32[60,128]{1,0:T(8,128)S(1)} %select_add_fusion.6), channel_id=1, source_target_pairs={{0,8},{1,9},{2,10},{3,11},{4,12},{5,13},{6,14},{7,15},{8,0},{9,1},... | collective-permute-start | bytes 92168 | tf_op jit(solution)/shard_map/ppermute | solution.py:130
  31.4 0.6 collective-permute-done.4
  32.0 1.5 %collective-permute-start.5 = (f32[120,128]{1,0:T(8,128)S(1)}, f32[120,128]{1,0:T(8,128)S(1)}, u32[]{:S(2)}, u32[]{:S(2)}) collective-permute-start(f32[120,128]{1,0:T(8,128)S(1)} %maximum_select_fusion.6), channel_id=1, source_target_pairs={{0,4},{1,5},{2,6},{3,7},{4,0},{5,1},{6,2},{7,3},{8,12},{9,13},{10,... | collective-permute-start | bytes 184328 | tf_op jit(solution)/shard_map/ppermute | solution.py:130
  33.6 1.0 %collective-permute-done.12 = f32[60,128]{1,0:T(8,128)S(1)} collective-permute-done((f32[60,128]{1,0:T(8,128)S(1)}, f32[60,128]{1,0:T(8,128)S(1)}, u32[]{:S(2)}, u32[]{:S(2)}) %collective-permute-start.12) | collective-permute-done | bytes 30752 | tf_op jit(solution)/shard_map/ppermute | solution.py:130
  34.6 1.6 %collective-permute-start.13 = (f32[120,128]{1,0:T(8,128)S(1)}, f32[120,128]{1,0:T(8,128)S(1)}, u32[]{:S(2)}, u32[]{:S(2)}) collective-permute-start(f32[120,128]{1,0:T(8,128)S(1)} %maximum_select_fusion.7), channel_id=1, source_target_pairs={{0,2},{1,3},{2,0},{3,1},{4,6},{5,7},{6,4},{7,5},{8,10},{9,11},{10,... | collective-permute-start | bytes 184328 | tf_op jit(solution)/shard_map/ppermute | solution.py:130
  36.2 0.1 collective-permute-done.5
  36.3 1.6 %collective-permute-start.6 = (f32[240,128]{1,0:T(8,128)S(1)}, f32[240,128]{1,0:T(8,128)S(1)}, u32[]{:S(2)}, u32[]{:S(2)}) collective-permute-start(f32[240,128]{1,0:T(8,128)S(1)} %maximum_select_fusion.4), channel_id=1, source_target_pairs={{0,2},{1,3},{2,0},{3,1},{4,6},{5,7},{6,4},{7,5},{8,10},{9,11},{10,... | collective-permute-start | bytes 368648 | tf_op jit(solution)/shard_map/ppermute | solution.py:130
  38.0 0.9 %collective-permute-done.13 = f32[120,128]{1,0:T(8,128)S(1)} collective-permute-done((f32[120,128]{1,0:T(8,128)S(1)}, f32[120,128]{1,0:T(8,128)S(1)}, u32[]{:S(2)}, u32[]{:S(2)}) %collective-permute-start.13) | collective-permute-done | bytes 61472 | tf_op jit(solution)/shard_map/ppermute | solution.py:130
  38.9 1.9 %collective-permute-start.14 = (f32[240,128]{1,0:T(8,128)S(1)}, f32[240,128]{1,0:T(8,128)S(1)}, u32[]{:S(2)}, u32[]{:S(2)}) collective-permute-start(f32[240,128]{1,0:T(8,128)S(1)} %maximum_select_fusion.5), channel_id=1, source_target_pairs={{0,4},{1,5},{2,6},{3,7},{4,0},{5,1},{6,2},{7,3},{8,12},{9,13},{10,... | collective-permute-start | bytes 368648 | tf_op jit(solution)/shard_map/ppermute | solution.py:130
  40.8 0.5 collective-permute-done.6
  41.3 0.1 collective-permute-start.7
  41.4 2.5 %collective-permute-done.14 = f32[240,128]{1,0:T(8,128)S(1)} collective-permute-done((f32[240,128]{1,0:T(8,128)S(1)}, f32[240,128]{1,0:T(8,128)S(1)}, u32[]{:S(2)}, u32[]{:S(2)}) %collective-permute-start.14) | collective-permute-done | bytes 122912 | tf_op jit(solution)/shard_map/ppermute | solution.py:130
  43.9 0.1 collective-permute-start.15
  44.0 0.0 collective-permute-done.7
  44.0 1.4 %collective-permute-done.15 = f32[480,128]{1,0:T(8,128)S(1)} collective-permute-done((f32[480,128]{1,0:T(8,128)S(1)}, f32[480,128]{1,0:T(8,128)S(1)}, u32[]{:S(2)}, u32[]{:S(2)}) %collective-permute-start.15) | collective-permute-done | bytes 245792 | tf_op jit(solution)/shard_map/ppermute | solution.py:130
  45.5 1.0 %pad_maximum_fusion.g_ref = f32[1920,128]{1,0:T(8,128)} fusion(f32[960,128]{1,0:T(8,128)S(1)} %maximum_select_fusion.1, f32[960,128]{1,0:T(8,128)S(1)} %maximum_select_fusion), kind=kLoop, calls=%fused_computation.7 | loop fusion | flops 245760 | bytes 1966080 | tf_op jit(solution)/shard_map/concatenate | solution.py:178
  46.5 32.2 %shard_map.68 = (f32[640,640]{1,0:T(8,128)}, f32[8,640]{1,0:T(8,128)}) custom-call(f32[1920,128]{1,0:T(8,128)} %pad_maximum_fusion.g_ref), custom_call_target="tpu_custom_call" | custom-call | tf_op jit(solution)/shard_map/pallas_call | solution.py:106
  78.7 1.5 %slice_bitcast_fusion = f32[576,576]{0,1:T(8,128)S(1)} fusion(f32[640,640]{1,0:T(8,128)} %get-tuple-element.4), kind=kLoop, calls=%fused_computation | loop fusion | bytes 2654208 | tf_op jit(solution)/shard_map/transpose | solution.py:186
  80.2 0.0 copy-start
  80.2 0.0 copy-start.1
  80.2 1.6 %copy.7 = f32[576,576]{1,0:T(8,128)} copy(f32[576,576]{0,1:T(8,128)S(1)} %slice_bitcast_fusion) | data formatting | bytes 2654208
  81.8 0.0 copy-done
  81.8 0.0 copy-done.1
  81.8 0.7 fusion.6
  82.6 0.6 subtract_multiply_fusion.1
  (36 shorter events, 0.6 us)
Async XLA Ops:
  9.2 1.7 %collective-permute-start = (f32[480,128]{1,0:T(8,128)S(1)}, f32[480,128]{1,0:T(8,128)S(1)}, u32[]{:S(2)}, u32[]{:S(2)}) collective-permute-start(f32[480,128]{1,0:T(8,128)S(1)} %slice_select_fusion.1), channel_id=1, source_target_pairs={{0,1},{1,0},{2,3},{3,2},{4,5},{5,4},{6,7},{7,6},{8,9},{9,8},{10,11... | collective-permute-start | bytes 737288 | tf_op jit(solution)/shard_map/ppermute | solution.py:127
  9.8 4.1 %collective-permute-start.8 = (f32[480,128]{1,0:T(8,128)S(1)}, f32[480,128]{1,0:T(8,128)S(1)}, u32[]{:S(2)}, u32[]{:S(2)}) collective-permute-start(f32[480,128]{1,0:T(8,128)S(1)} %slice_select_fusion), channel_id=1, source_target_pairs={{0,1},{1,0},{2,3},{3,2},{4,5},{5,4},{6,7},{7,6},{8,9},{9,8},{10,11... | collective-permute-start | bytes 737288 | tf_op jit(solution)/shard_map/ppermute | solution.py:127
  11.0 6.5 %collective-permute-start.1 = (f32[240,128]{1,0:T(8,128)S(1)}, f32[240,128]{1,0:T(8,128)S(1)}, u32[]{:S(2)}, u32[]{:S(2)}) collective-permute-start(f32[240,128]{1,0:T(8,128)S(1)} %slice_select_fusion.3), channel_id=1, source_target_pairs={{0,2},{1,3},{2,0},{3,1},{4,6},{5,7},{6,4},{7,5},{8,10},{9,11},{10,... | collective-permute-start | bytes 368648 | tf_op jit(solution)/shard_map/ppermute | solution.py:127
  14.0 5.5 %collective-permute-start.9 = (f32[240,128]{1,0:T(8,128)S(1)}, f32[240,128]{1,0:T(8,128)S(1)}, u32[]{:S(2)}, u32[]{:S(2)}) collective-permute-start(f32[240,128]{1,0:T(8,128)S(1)} %slice_select_fusion.2), channel_id=1, source_target_pairs={{0,4},{1,5},{2,6},{3,7},{4,0},{5,1},{6,2},{7,3},{8,12},{9,13},{10,... | collective-permute-start | bytes 368648 | tf_op jit(solution)/shard_map/ppermute | solution.py:127
  17.6 4.3 %collective-permute-start.2 = (f32[120,128]{1,0:T(8,128)S(1)}, f32[120,128]{1,0:T(8,128)S(1)}, u32[]{:S(2)}, u32[]{:S(2)}) collective-permute-start(f32[120,128]{1,0:T(8,128)S(1)} %slice_select_fusion.5), channel_id=1, source_target_pairs={{0,4},{1,5},{2,6},{3,7},{4,0},{5,1},{6,2},{7,3},{8,12},{9,13},{10,... | collective-permute-start | bytes 184328 | tf_op jit(solution)/shard_map/ppermute | solution.py:127
  19.5 5.3 %collective-permute-start.10 = (f32[120,128]{1,0:T(8,128)S(1)}, f32[120,128]{1,0:T(8,128)S(1)}, u32[]{:S(2)}, u32[]{:S(2)}) collective-permute-start(f32[120,128]{1,0:T(8,128)S(1)} %slice_select_fusion.4), channel_id=1, source_target_pairs={{0,2},{1,3},{2,0},{3,1},{4,6},{5,7},{6,4},{7,5},{8,10},{9,11},{10,... | collective-permute-start | bytes 184328 | tf_op jit(solution)/shard_map/ppermute | solution.py:127
  21.9 5.0 %collective-permute-start.3 = (f32[60,128]{1,0:T(8,128)S(1)}, f32[60,128]{1,0:T(8,128)S(1)}, u32[]{:S(2)}, u32[]{:S(2)}) collective-permute-start(f32[60,128]{1,0:T(8,128)S(1)} %slice_select_fusion.7), channel_id=1, source_target_pairs={{0,8},{1,9},{2,10},{3,11},{4,12},{5,13},{6,14},{7,15},{8,0},{9,1},... | collective-permute-start | bytes 92168 | tf_op jit(solution)/shard_map/ppermute | solution.py:127
  24.8 4.9 %collective-permute-start.11 = (f32[60,128]{1,0:T(8,128)S(1)}, f32[60,128]{1,0:T(8,128)S(1)}, u32[]{:S(2)}, u32[]{:S(2)}) collective-permute-start(f32[60,128]{1,0:T(8,128)S(1)} %slice_select_fusion.6), channel_id=1, source_target_pairs={{0,8},{1,9},{2,10},{3,11},{4,12},{5,13},{6,14},{7,15},{8,0},{9,1},... | collective-permute-start | bytes 92168 | tf_op jit(solution)/shard_map/ppermute | solution.py:127
  27.0 5.1 %collective-permute-start.4 = (f32[60,128]{1,0:T(8,128)S(1)}, f32[60,128]{1,0:T(8,128)S(1)}, u32[]{:S(2)}, u32[]{:S(2)}) collective-permute-start(f32[60,128]{1,0:T(8,128)S(1)} %select_add_fusion.7), channel_id=1, source_target_pairs={{0,8},{1,9},{2,10},{3,11},{4,12},{5,13},{6,14},{7,15},{8,0},{9,1},... | collective-permute-start | bytes 92168 | tf_op jit(solution)/shard_map/ppermute | solution.py:130
  29.7 4.9 %collective-permute-start.12 = (f32[60,128]{1,0:T(8,128)S(1)}, f32[60,128]{1,0:T(8,128)S(1)}, u32[]{:S(2)}, u32[]{:S(2)}) collective-permute-start(f32[60,128]{1,0:T(8,128)S(1)} %select_add_fusion.6), channel_id=1, source_target_pairs={{0,8},{1,9},{2,10},{3,11},{4,12},{5,13},{6,14},{7,15},{8,0},{9,1},... | collective-permute-start | bytes 92168 | tf_op jit(solution)/shard_map/ppermute | solution.py:130
  32.0 4.3 %collective-permute-start.5 = (f32[120,128]{1,0:T(8,128)S(1)}, f32[120,128]{1,0:T(8,128)S(1)}, u32[]{:S(2)}, u32[]{:S(2)}) collective-permute-start(f32[120,128]{1,0:T(8,128)S(1)} %maximum_select_fusion.6), channel_id=1, source_target_pairs={{0,4},{1,5},{2,6},{3,7},{4,0},{5,1},{6,2},{7,3},{8,12},{9,13},{10,... | collective-permute-start | bytes 184328 | tf_op jit(solution)/shard_map/ppermute | solution.py:130
  34.6 4.3 %collective-permute-start.13 = (f32[120,128]{1,0:T(8,128)S(1)}, f32[120,128]{1,0:T(8,128)S(1)}, u32[]{:S(2)}, u32[]{:S(2)}) collective-permute-start(f32[120,128]{1,0:T(8,128)S(1)} %maximum_select_fusion.7), channel_id=1, source_target_pairs={{0,2},{1,3},{2,0},{3,1},{4,6},{5,7},{6,4},{7,5},{8,10},{9,11},{10,... | collective-permute-start | bytes 184328 | tf_op jit(solution)/shard_map/ppermute | solution.py:130
  36.3 4.9 %collective-permute-start.6 = (f32[240,128]{1,0:T(8,128)S(1)}, f32[240,128]{1,0:T(8,128)S(1)}, u32[]{:S(2)}, u32[]{:S(2)}) collective-permute-start(f32[240,128]{1,0:T(8,128)S(1)} %maximum_select_fusion.4), channel_id=1, source_target_pairs={{0,2},{1,3},{2,0},{3,1},{4,6},{5,7},{6,4},{7,5},{8,10},{9,11},{10,... | collective-permute-start | bytes 368648 | tf_op jit(solution)/shard_map/ppermute | solution.py:130
  38.9 4.9 %collective-permute-start.14 = (f32[240,128]{1,0:T(8,128)S(1)}, f32[240,128]{1,0:T(8,128)S(1)}, u32[]{:S(2)}, u32[]{:S(2)}) collective-permute-start(f32[240,128]{1,0:T(8,128)S(1)} %maximum_select_fusion.5), channel_id=1, source_target_pairs={{0,4},{1,5},{2,6},{3,7},{4,0},{5,1},{6,2},{7,3},{8,12},{9,13},{10,... | collective-permute-start | bytes 368648 | tf_op jit(solution)/shard_map/ppermute | solution.py:130
  41.3 2.7 %collective-permute-start.7 = (f32[480,128]{1,0:T(8,128)S(1)}, f32[480,128]{1,0:T(8,128)S(1)}, u32[]{:S(2)}, u32[]{:S(2)}) collective-permute-start(f32[480,128]{1,0:T(8,128)S(1)} %maximum_select_fusion.2), channel_id=1, source_target_pairs={{0,1},{1,0},{2,3},{3,2},{4,5},{5,4},{6,7},{7,6},{8,9},{9,8},{10,11... | collective-permute-start | bytes 737288 | tf_op jit(solution)/shard_map/ppermute | solution.py:130
  43.9 1.6 %collective-permute-start.15 = (f32[480,128]{1,0:T(8,128)S(1)}, f32[480,128]{1,0:T(8,128)S(1)}, u32[]{:S(2)}, u32[]{:S(2)}) collective-permute-start(f32[480,128]{1,0:T(8,128)S(1)} %maximum_select_fusion.3), channel_id=1, source_target_pairs={{0,1},{1,0},{2,3},{3,2},{4,5},{5,4},{6,7},{7,6},{8,9},{9,8},{10,11... | collective-permute-start | bytes 737288 | tf_op jit(solution)/shard_map/ppermute | solution.py:130
  80.2 1.6 %copy-start = (bf16[576,512]{1,0:T(8,128)(2,1)S(1)}, bf16[576,512]{1,0:T(8,128)(2,1)}, u32[]{:S(2)}) copy-start(bf16[576,512]{1,0:T(8,128)(2,1)} %param.5) | copy-start | bytes 1769476
  80.2 1.6 %copy-start.1 = (f32[8,640]{1,0:T(8,128)S(1)}, f32[8,640]{1,0:T(8,128)}, u32[]{:S(2)}) copy-start(f32[8,640]{1,0:T(8,128)} %get-tuple-element.5) | copy-start | bytes 61444
